TPU v7x, 512 devices: a whole 4x4x16 slice. The times are simulated.
512 devices in a mesh: exp: 16 (over z), sky: 32 (over y, x, core).
Axes of the slice: x: 4, y: 4, z: 16, core: 2. Of those that a mesh axis runs over, the one named last changes fastest.
Arguments:
- sky_start: float32 [16, 128, 4096], P(None, None, 'sky'), may hold values from -6 to 6
- exposures: bfloat16 [16, 1024, 2, 128, 128], P('exp', 'sky'), may hold values from -16 to 16
- weights: bfloat16 [16, 1024, 2], P('exp', 'sky'), may hold values from 0.5 to 2
- footprint_owner: int32 [16, 1024, 1], P('exp', 'sky'), may hold values from 0 to 31; in each aligned block of 32 rows (0 to 31, 32 to 63, ..., all dimensions but the last counted through in order) at most 2 rows name the same one
- footprint_row: int32 [16, 1024], P('exp', 'sky'), may hold values from 0 to 15
- kernel_index: int32 [16, 1024, 2, 2], P('exp', 'sky'), may hold values from 0 to 7
- kernels: bfloat16 [8, 128, 128], replicated, may hold values from -1 to 1
Outputs:
- sky_image: float32 [16, 128, 4096], P(None, None, 'sky')
Inputs may be any that keep to these rules, and one draw needn't show every extreme that they name: `footprint_owner`: the 32 footprint tiles of one device name one tile column at most 2 times, and some tile column exactly 2 times.
All inputs are finite; a program needn't handle non-finite values.
Results may differ from a plain program's by a relative error of at most 0.0035.
Values may be sent and summed in bfloat16 or wider, within the bound.
No kernel may reach another device: no remote copies, remote signals or barrier semaphores. Data moves between devices by JAX's collectives and lax.ppermute only.
A program may use at most 128 MiB of HBM per device.

v0:
```python
import jax
import jax.numpy as jnp
from jax import lax
from jax.sharding import PartitionSpec as P

ITERS = 2


weight_ceiling = 2.0


def padded_2(cells, sides, width):
    for axis, dim in sides:
        count = lax.axis_size(axis)
        ends = count - 1
        head = lax.slice_in_dim(cells, 0, width, axis=dim)
        tail = lax.slice_in_dim(cells, cells.shape[dim] - width, cells.shape[dim], axis=dim)
        cells = jnp.concatenate(
            [
                lax.ppermute(tail, axis, [(i, (i + 1) % count) for i in range(ends)]),
                cells,
                lax.ppermute(head, axis, [((i + 1) % count, i) for i in range(ends)]),
            ],
            axis=dim,
        )
    return cells


def pick_kernels(kernel_ids, kernels):
    table_size = kernels.shape[0]
    tile_edge = kernels.shape[1]
    onehot = (kernel_ids[..., None] == jnp.arange(table_size, dtype=jnp.int32)).astype(jnp.bfloat16)
    onehot = onehot.reshape(-1, table_size)
    selected = jnp.dot(onehot, kernels.reshape(table_size, -1), preferred_element_type=jnp.float32)
    selected = selected.astype(jnp.bfloat16).reshape(kernel_ids.shape + (tile_edge, tile_edge))
    return (selected[..., 0, :, :], selected[..., 1, :, :])


def adjoint_tiles(fetched, left_kernels, right_kernels, tile_weights, observed):
    left_product = jnp.einsum(
        "fetu,fuv->fetv", left_kernels, fetched, preferred_element_type=jnp.float32
    ).astype(jnp.bfloat16)
    predicted = jnp.einsum(
        "fetv,fewv->fetw", left_product, right_kernels, preferred_element_type=jnp.float32
    )
    residual = tile_weights.astype(jnp.float32)[..., None, None] * (
        predicted - observed.astype(jnp.float32)
    )
    residual = residual.astype(jnp.bfloat16)
    back_product = jnp.einsum(
        "feut,feuw->fetw", left_kernels, residual, preferred_element_type=jnp.float32
    ).astype(jnp.bfloat16)
    summed = jnp.sum(
        jnp.einsum(
            "fetw,fewv->fetv", back_product, right_kernels, preferred_element_type=jnp.float32
        ),
        axis=1,
    )
    return summed.astype(jnp.bfloat16)


def laplace_image(padded):
    image_rows = padded.reshape(padded.shape[0] * padded.shape[1], padded.shape[2])
    center = image_rows[:, 1:-1]
    vertical = jnp.pad(center, ((1, 1), (0, 0)))
    laplacian = 4.0 * center - image_rows[:, :-2] - image_rows[:, 2:] - vertical[:-2] - vertical[2:]
    return laplacian.reshape(padded.shape[0], padded.shape[1], padded.shape[2] - 2)


def per_device(
    sky_start, exposures, weights, footprint_owner, footprint_row, kernel_index, kernels
):
    sky_rows = sky_start.shape[0]
    tile_edge = sky_start.shape[1]
    foot_tiles = footprint_row.shape[1]
    expo_count = exposures.shape[2]
    n_sky = lax.axis_size("sky")
    n_exp = lax.axis_size("exp")
    capacity = max(2, 3 * foot_tiles // (2 * n_sky))
    slot_count = n_sky * capacity
    prior_weight = n_exp * foot_tiles * expo_count / (8.0 * sky_rows)
    owner_ids = footprint_owner[0, :, 0]
    tile_rows = footprint_row[0]
    onehot_owner = (owner_ids[:, None] == jnp.arange(n_sky, dtype=jnp.int32)[None, :]).astype(
        jnp.int32
    )
    ranks = jnp.sum((jnp.cumsum(onehot_owner, axis=0) - onehot_owner) * onehot_owner, axis=1)
    slot_of = owner_ids * capacity + ranks
    packing = jnp.arange(slot_count, dtype=jnp.int32)[:, None] == slot_of[None, :]
    packing_half = packing.astype(jnp.bfloat16)
    requested = jnp.sum(jnp.where(packing, tile_rows[None, :] + 1, 0), axis=1) - 1
    observed = exposures[0]
    tile_weights = weights[0]
    kernel_ids = kernel_index[0]
    incoming = lax.all_to_all(requested, "sky", split_axis=0, concat_axis=0, tiled=True)
    left_kernels, right_kernels = pick_kernels(kernel_ids, kernels)
    receive_map = jnp.arange(sky_rows, dtype=jnp.int32)[:, None] == incoming[None, :]
    counts = float(expo_count) * jnp.sum(receive_map.astype(jnp.float32), axis=1)
    receive_half = receive_map.astype(jnp.bfloat16)
    safe_rows = jnp.maximum(incoming, 0)
    sky_now = sky_start
    for iteration in range(ITERS):
        sky_half = sky_now.astype(jnp.bfloat16)
        replies = lax.all_to_all(
            sky_half[safe_rows], "sky", split_axis=0, concat_axis=0, tiled=True
        )
        fetched = replies[slot_of]
        adjoint = adjoint_tiles(fetched, left_kernels, right_kernels, tile_weights, observed)
        outgoing = jnp.dot(
            packing_half, adjoint.reshape(foot_tiles, -1), preferred_element_type=jnp.float32
        )
        arrived = lax.all_to_all(
            outgoing.astype(jnp.bfloat16), "sky", split_axis=0, concat_axis=0, tiled=True
        )
        partial_value = jnp.dot(receive_half, arrived, preferred_element_type=jnp.float32).reshape(
            sky_rows, tile_edge, tile_edge
        )
        laplacian = laplace_image(padded_2(sky_now, (("sky", 2),), 1))
        summed, summed_counts = lax.psum((partial_value, counts), "exp")
        denominator = weight_ceiling * summed_counts[:, None, None] + 8.0 * prior_weight
        sky_now = sky_now - (summed + prior_weight * laplacian) / denominator
    return sky_now


def solution(mesh):
    in_specs = (
        P(None, None, "sky"),
        P("exp", "sky", None, None, None),
        P("exp", "sky", None),
        P("exp", "sky", None),
        P("exp", "sky"),
        P("exp", "sky", None, None),
        P(),
    )
    out_specs = P(None, None, "sky")
    return jax.shard_map(
        per_device, mesh=mesh, in_specs=in_specs, out_specs=out_specs, check_vma=False
    )
```

profile of v0, /device:TPU:6, one launch (start us, length us, event | category | flops | bytes accessed | tf_op | source)
XLA Modules:
  0.0 492.7 jit_solution(1157418583036453153)
XLA Ops:
  10.3 9.4 %all-to-all-start = ((s32[32,2,1]{1,2,0:T(1,128)}), s32[32,2,1]{1,2,0:T(1,128)S(1)}, u32[]{:S(2)}, u32[]{:S(2)}) async-start(s32[32,2,1]{1,2,0:T(1,128)} %bitcast.2), calls=%async_computation | async-start | bytes 32768 | tf_op jit(solution)/shard_map/all_to_all | solution.py:95
  21.0 4.2 all-to-all-done
  26.6 2.1 gather_fusion
  28.7 5.9 %all-to-all-start.1 = ((bf16[64,128,128]{2,1,0:T(8,128)(2,1)}), bf16[64,128,128]{2,1,0:T(8,128)(2,1)S(1)}, u32[]{:S(2)}, u32[]{:S(2)}) async-start(bf16[64,128,128]{2,1,0:T(8,128)(2,1)} %gather_fusion), calls=%async_computation.1 | async-start | bytes 4194304 | tf_op jit(solution)/shard_map/all_to_all | solution.py:104
  36.3 3.2 copy.94
  39.5 20.8 %all-to-all-done.1 = bf16[64,128,128]{2,1,0:T(8,128)(2,1)S(1)} async-done(((bf16[64,128,128]{2,1,0:T(8,128)(2,1)}), bf16[64,128,128]{2,1,0:T(8,128)(2,1)S(1)}, u32[]{:S(2)}, u32[]{:S(2)}) %all-to-all-start.1) | async-done | bytes 2097184 | tf_op jit(solution)/shard_map/all_to_all | solution.py:104
  61.0 5.0 %fusion.1 = bf16[32,2,128,128]{3,2,1,0:T(8,128)(2,1)S(1)} fusion(bf16[1,32,2,128,128]{4,3,2,1,0:T(8,128)(2,1)} %param.8, f32[32,2]{1,0:T(8,128)S(1)} %copy.56, bf16[32,2,2,128,128]{4,3,2,1,0:T(8,128)(2,1)} %bitcast.105, bf16[32,128,128]{2,1,0:T(8,128)(2,1)S(1)} %gather_fusion.1), kind=kOutput, calls=%fused_computation.10 | convolution fusion | flops 542113792 | bytes 9437440 | tf_op jit(solution)/shard_map/fetv,fewv->fetw/dot_general | solution.py:43
  66.0 3.6 bitcast_convert_fusion.1
  70.6 2.7 all_to_all.28
  73.2 9.2 %all-to-all-start.2 = ((bf16[32,2,16384]{2,1,0:T(2,128)(2,1)}), bf16[32,2,16384]{2,1,0:T(2,128)(2,1)}, u32[]{:S(2)}, u32[]{:S(2)}) async-start(bf16[32,2,16384]{2,1,0:T(2,128)(2,1)} %all_to_all.28), calls=%async_computation.2 | async-start | bytes 4194304 | tf_op jit(solution)/shard_map/all_to_all | solution.py:112
  83.2 2.5 collective-permute-start.1
  86.0 1.9 collective-permute-start
  88.2 19.9 %all-to-all-done.2 = bf16[32,2,16384]{2,1,0:T(2,128)(2,1)} async-done(((bf16[32,2,16384]{2,1,0:T(2,128)(2,1)}), bf16[32,2,16384]{2,1,0:T(2,128)(2,1)}, u32[]{:S(2)}, u32[]{:S(2)}) %all-to-all-start.2) | async-done | bytes 2097184 | tf_op jit(solution)/shard_map/all_to_all | solution.py:112
  108.1 4.1 all_to_all.30
  112.2 3.0 fusion.8
  115.3 34.8 %psum.25 = f32[16]{0:T(128)S(1)} all-reduce(f32[16]{0:T(128)S(1)} %broadcast_multiply_fusion), channel_id=1, replica_groups=mesh['exp'=16,'sky'=32] {'exp'}, use_global_device_ids=true, to_apply=%region_5.6 | all-reduce | flops 16 | bytes 128 | tf_op jit(solution)/shard_map/psum | solution.py:119
  152.6 104.0 %all-reduce.5.cloned.1.call-done = f32[16,128,128]{2,0,1:T(8,128)} async-done(((f32[16,128,128]{2,0,1:T(8,128)}), f32[16,128,128]{2,0,1:T(8,128)}) %all-reduce.5.cloned.1.call-update) | async-done | bytes 1048592 | tf_op jit(solution)/shard_map/psum | solution.py:119
  256.6 2.5 fusion.59
  259.1 2.1 gather_fusion.2
  261.3 33.3 %all_to_all.40 = bf16[64,128,128]{2,1,0:T(8,128)(2,1)S(1)} all-to-all(bf16[64,128,128]{2,1,0:T(8,128)(2,1)} %gather_fusion.2), channel_id=1, replica_groups=mesh['exp'=16,'sky'=32] {'sky'}, dimensions={0} | all-to-all | bytes 4194304 | tf_op jit(solution)/shard_map/all_to_all | solution.py:104
  294.6 1.6 gather_fusion.3
  296.2 5.3 %fusion.3 = bf16[32,2,128,128]{3,2,1,0:T(8,128)(2,1)S(1)} fusion(bf16[1,32,2,128,128]{4,3,2,1,0:T(8,128)(2,1)} %param.8, f32[32,2]{1,0:T(8,128)S(1)} %copy.56, bf16[32,2,2,128,128]{4,3,2,1,0:T(8,128)(2,1)} %bitcast.107, bf16[32,128,128]{2,1,0:T(8,128)(2,1)} %gather_fusion.3), kind=kOutput, calls=%fused_computation.12 | convolution fusion | flops 542113792 | bytes 9437440 | tf_op jit(solution)/shard_map/fetv,fewv->fetw/dot_general | solution.py:43
  301.5 4.6 bitcast_convert_fusion
  306.1 2.1 convolution_convert_fusion.1
  308.3 2.7 all_to_all.32
  310.9 33.3 %all_to_all.41 = bf16[32,2,16384]{2,1,0:T(2,128)(2,1)} all-to-all(bf16[32,2,16384]{2,1,0:T(2,128)(2,1)} %all_to_all.32), channel_id=1, replica_groups=mesh['exp'=16,'sky'=32] {'sky'}, dimensions={0} | all-to-all | bytes 4194304 | tf_op jit(solution)/shard_map/all_to_all | solution.py:112
  344.2 2.7 all_to_all.34
  349.2 3.1 collective-permute-start.3
  352.7 2.3 collective-permute-start.2
  355.6 2.1 collective-permute-done.2
  361.1 121.6 %all-reduce.7.cloned.1.call-done = f32[16,128,128]{2,0,1:T(8,128)} async-done(((f32[16,128,128]{2,0,1:T(8,128)}), f32[16,128,128]{2,0,1:T(8,128)}) %all-reduce.7.cloned.1.call-update) | async-done | bytes 1048592 | tf_op jit(solution)/shard_map/psum | solution.py:119
  482.7 1.9 fusion.44
  (63 shorter events, 21.5 us)
Async XLA Ops:
  10.3 14.9 %all-to-all-start = ((s32[32,2,1]{1,2,0:T(1,128)}), s32[32,2,1]{1,2,0:T(1,128)S(1)}, u32[]{:S(2)}, u32[]{:S(2)}) async-start(s32[32,2,1]{1,2,0:T(1,128)} %bitcast.2), calls=%async_computation | async-start | bytes 32768 | tf_op jit(solution)/shard_map/all_to_all | solution.py:95
  28.7 5.9 %copy-start.4 = (bf16[1,32,2]{1,2,0:T(2,128)(2,1)S(1)}, bf16[1,32,2]{1,2,0:T(2,128)(2,1)}, u32[]{:S(2)}) copy-start(bf16[1,32,2]{1,2,0:T(2,128)(2,1)} %param.9) | copy-start | bytes 388
  28.7 6.0 %copy-start.2 = (s32[1,32,2,2]{1,3,2,0:T(2,128)S(1)}, s32[1,32,2,2]{1,3,2,0:T(2,128)}, u32[]{:S(2)}) copy-start(s32[1,32,2,2]{1,3,2,0:T(2,128)} %param.12) | copy-start | bytes 1540
  28.7 6.3 %copy-start.1 = (bf16[8,128,128]{2,1,0:T(8,128)(2,1)S(1)}, bf16[8,128,128]{2,1,0:T(8,128)(2,1)}, u32[]{:S(2)}) copy-start(bf16[8,128,128]{2,1,0:T(8,128)(2,1)} %param.13) | copy-start | bytes 786436
  28.7 31.5 %all-to-all-start.1 = ((bf16[64,128,128]{2,1,0:T(8,128)(2,1)}), bf16[64,128,128]{2,1,0:T(8,128)(2,1)S(1)}, u32[]{:S(2)}, u32[]{:S(2)}) async-start(bf16[64,128,128]{2,1,0:T(8,128)(2,1)} %gather_fusion), calls=%async_computation.1 | async-start | bytes 4194304 | tf_op jit(solution)/shard_map/all_to_all | solution.py:104
  36.3 3.2 copy-start.3
  73.2 9.2 %copy-start = (f32[16,128,128]{2,1,0:T(8,128)S(1)}, f32[16,128,128]{2,1,0:T(8,128)}, u32[]{:S(2)}) copy-start(f32[16,128,128]{2,1,0:T(8,128)} %param.7) | copy-start | bytes 3145732
  73.2 34.9 %all-to-all-start.2 = ((bf16[32,2,16384]{2,1,0:T(2,128)(2,1)}), bf16[32,2,16384]{2,1,0:T(2,128)(2,1)}, u32[]{:S(2)}, u32[]{:S(2)}) async-start(bf16[32,2,16384]{2,1,0:T(2,128)(2,1)} %all_to_all.28), calls=%async_computation.2 | async-start | bytes 4194304 | tf_op jit(solution)/shard_map/all_to_all | solution.py:112
  82.4 174.1 %all-reduce.5.cloned.1.call-start = ((), (), s32[]{:S(2)}) async-start(), calls=%async_computation.5 | async-start | bytes 2097152 | tf_op jit(solution)/shard_map/psum | solution.py:119
  83.2 66.9 %collective-permute-start.1 = (f32[16,128,1]{1,0,2:T(8,128)S(1)}, f32[16,128,1]{1,0,2:T(8,128)S(1)}, u32[]{:S(2)}, u32[]{:S(2)}) collective-permute-start(f32[16,128,1]{1,0,2:T(8,128)S(1)} %copy.90), channel_id=1, source_target_pairs={{1,0},{2,1},{3,2},{4,3},{5,4},{6,5},{7,6},{8,7},{9,8},{10,9},{11,1... | collective-permute-start | bytes 24584 | tf_op jit(solution)/shard_map/ppermute | solution.py:22
  86.0 64.5 %collective-permute-start = (f32[16,128,1]{1,0,2:T(8,128)S(1)}, f32[16,128,1]{1,0,2:T(8,128)S(1)}, u32[]{:S(2)}, u32[]{:S(2)}) collective-permute-start(f32[16,128,1]{1,0,2:T(8,128)S(1)} %copy.89), channel_id=1, source_target_pairs={{0,1},{1,2},{2,3},{3,4},{4,5},{5,6},{6,7},{7,8},{8,9},{9,10},{10,1... | collective-permute-start | bytes 24584 | tf_op jit(solution)/shard_map/ppermute | solution.py:20
  115.2 367.5 %all-reduce.7.cloned.1.call-start = ((), (), s32[]{:S(2)}) async-start(), calls=%async_computation.6 | async-start | bytes 2097152 | tf_op jit(solution)/shard_map/psum | solution.py:119
  349.2 5.9 %collective-permute-start.3 = (f32[16,128,1]{1,0,2:T(8,128)S(1)}, f32[16,128,1]{1,0,2:T(8,128)S(1)}, u32[]{:S(2)}, u32[]{:S(2)}) collective-permute-start(f32[16,128,1]{1,0,2:T(8,128)S(1)} %copy.70), channel_id=1, source_target_pairs={{1,0},{2,1},{3,2},{4,3},{5,4},{6,5},{7,6},{8,7},{9,8},{10,9},{11,1... | collective-permute-start | bytes 24584 | tf_op jit(solution)/shard_map/ppermute | solution.py:22
  352.7 5.0 %collective-permute-start.2 = (f32[16,128,1]{1,0,2:T(8,128)S(1)}, f32[16,128,1]{1,0,2:T(8,128)S(1)}, u32[]{:S(2)}, u32[]{:S(2)}) collective-permute-start(f32[16,128,1]{1,0,2:T(8,128)S(1)} %copy.69), channel_id=1, source_target_pairs={{0,1},{1,2},{2,3},{3,4},{4,5},{5,6},{6,7},{7,8},{8,9},{9,10},{10,1... | collective-permute-start | bytes 24584 | tf_op jit(solution)/shard_map/ppermute | solution.py:20
Sparse Core Ops, SparseCore 0:
  115.3 141.1 all-reduce.4
  348.5 134.1 all-reduce.6
where the time goes:
time: 494 us; the launch traced here: 493 us
  waiting for transfers between devices  273 us (55%)
  blocking collectives  101 us (20%)
  starting transfers between devices  34.4 us (7%)
  local copies, waits for them, and re-layouts  31.2 us (6%)
  matrix products  27.2 us (6%)
  between operations  13.7 us (3%)
  other arithmetic  12.3 us (2%)
    psum x2, waiting for transfers between devices, per_device(): summed, summed_counts = lax.psum((partial_value, counts), 'exp')  226 us
    psum x1, blocking collectives, per_device(): summed, summed_counts = lax.psum((partial_value, counts), 'exp')  34.8 us
    all_to_all x1, blocking collectives, per_device(): lax.all_to_all(outgoing.astype(jnp.bfloat16), 'sky', split_axis=0, concat...  33.3 us
    all_to_all x1, blocking collectives, per_device(): lax.all_to_all(sky_half[safe_rows], 'sky', split_axis=0, concat_axis=0, t...  33.3 us
    all_to_all x1, waiting for transfers between devices, per_device(): lax.all_to_all(sky_half[safe_rows], 'sky', split_axis=0, concat_axis=0, t...  20.8 us
    all_to_all x1, waiting for transfers between devices, per_device(): lax.all_to_all(outgoing.astype(jnp.bfloat16), 'sky', split_axis=0, concat...  19.9 us
    all_to_all x4, local copies, waits for them, and re-layouts, per_device(): lax.all_to_all(outgoing.astype(jnp.bfloat16), 'sky', split_axis=0, concat...  12.2 us
    dot_general x2, matrix products, adjoint_tiles(): jnp.einsum('fetv,fewv->fetw', left_product, right_kernels, preferred_elem...  10.3 us
  transfers between devices with their start and end apart: 9, of which 6 were waited for; matrix products, arithmetic and copies ran while one was open for 4% of the time, Pallas kernels for 0%

commit v1 on v0

--- a/solution.py
+++ b/solution.py
@@ -95,9 +95,14 @@
     incoming = lax.all_to_all(requested, "sky", split_axis=0, concat_axis=0, tiled=True)
     left_kernels, right_kernels = pick_kernels(kernel_ids, kernels)
     receive_map = jnp.arange(sky_rows, dtype=jnp.int32)[:, None] == incoming[None, :]
-    counts = float(expo_count) * jnp.sum(receive_map.astype(jnp.float32), axis=1)
+    local_counts = float(expo_count) * jnp.sum(receive_map.astype(jnp.float32), axis=1)
+    counts = jnp.sum(lax.all_gather(local_counts, "exp", axis=0), axis=0)
     receive_half = receive_map.astype(jnp.bfloat16)
     safe_rows = jnp.maximum(incoming, 0)
+    rows_per = sky_rows // n_exp
+    own_rows = lax.axis_index("exp") * rows_per
+    own_counts = lax.dynamic_slice_in_dim(counts, own_rows, rows_per)
+    denominator = weight_ceiling * own_counts[:, None, None] + 8.0 * prior_weight
     sky_now = sky_start
     for iteration in range(ITERS):
         sky_half = sky_now.astype(jnp.bfloat16)
@@ -115,10 +120,17 @@
         partial_value = jnp.dot(receive_half, arrived, preferred_element_type=jnp.float32).reshape(
             sky_rows, tile_edge, tile_edge
         )
+        row_parts = lax.all_to_all(
+            partial_value.astype(jnp.bfloat16), "exp", split_axis=0, concat_axis=0, tiled=True
+        )
+        summed = jnp.sum(
+            row_parts.astype(jnp.float32).reshape(n_exp, rows_per, tile_edge, tile_edge), axis=0
+        )
         laplacian = laplace_image(padded_2(sky_now, (("sky", 2),), 1))
-        summed, summed_counts = lax.psum((partial_value, counts), "exp")
-        denominator = weight_ceiling * summed_counts[:, None, None] + 8.0 * prior_weight
-        sky_now = sky_now - (summed + prior_weight * laplacian) / denominator
+        own_laplacian = lax.dynamic_slice_in_dim(laplacian, own_rows, rows_per)
+        step = (summed + prior_weight * own_laplacian) / denominator
+        steps = lax.all_gather(step.astype(jnp.bfloat16), "exp", axis=0, tiled=True)
+        sky_now = sky_now - steps.astype(jnp.float32)
     return sky_now
 
 

time: 494 us -> 377 us (0.76)
  waiting for transfers between devices: 273 us -> 70.2 us
  blocking collectives: 101 us -> 169 us
  starting transfers between devices: 34.4 us -> 57.8 us
  between operations: 13.7 us -> 1.47 us
    psum x2 -> x0, waiting for transfers between devices: 226 us -> none  [per_device(): summed, summed_counts = lax.psum((partial_value, counts), 'exp')]
    all_gather x0 -> x2, blocking collectives: none -> 62.2 us  [per_device(): steps = lax.all_gather(step.astype(jnp.bfloat16), 'exp', axis=0, tiled=True)]
    unnamed x0 -> x1, blocking collectives: none -> 41 us
    psum x1 -> x0, blocking collectives: 34.8 us -> none  [per_device(): summed, summed_counts = lax.psum((partial_value, counts), 'exp')]
    all_to_all x0 -> x2, starting transfers between devices: none -> 23.7 us  [per_device(): lax.all_to_all(partial_value.astype(jnp.bfloat16), 'exp', split_axis=0, c...]
    all_to_all x0 -> x2, waiting for transfers between devices: none -> 17.2 us  [per_device(): lax.all_to_all(partial_value.astype(jnp.bfloat16), 'exp', split_axis=0, c...]
    all_to_all x1, waiting for transfers between devices: 19.9 us -> 25.5 us  [per_device(): lax.all_to_all(outgoing.astype(jnp.bfloat16), 'sky', split_axis=0, concat...]
  transfers between devices with their start and end apart: 9 -> 9, of which waited for: 6 -> 5; matrix products, arithmetic and copies ran while one was open for 4% -> 4% of each run, Pallas kernels for 0% -> 0%
where the time goes in v1:
time: 377 us; the launch traced here: 371 us
  blocking collectives  169 us (45%)
  waiting for transfers between devices  70.2 us (19%)
  starting transfers between devices  57.8 us (15%)
  local copies, waits for them, and re-layouts  33.6 us (9%)
  matrix products  27.7 us (7%)
  other arithmetic  11.7 us (3%)
    all_gather x2, blocking collectives, per_device(): steps = lax.all_gather(step.astype(jnp.bfloat16), 'exp', axis=0, tiled=True)  62.2 us
    unnamed x1, blocking collectives  41 us
    all_to_all x1, blocking collectives, per_device(): lax.all_to_all(outgoing.astype(jnp.bfloat16), 'sky', split_axis=0, concat...  33.3 us
    all_to_all x1, blocking collectives, per_device(): lax.all_to_all(sky_half[safe_rows], 'sky', split_axis=0, concat_axis=0, t...  32.5 us
    all_to_all x1, waiting for transfers between devices, per_device(): lax.all_to_all(outgoing.astype(jnp.bfloat16), 'sky', split_axis=0, concat...  25.5 us
    all_to_all x2, starting transfers between devices, per_device(): lax.all_to_all(partial_value.astype(jnp.bfloat16), 'exp', split_axis=0, c...  23.7 us
    all_to_all x1, waiting for transfers between devices, per_device(): lax.all_to_all(sky_half[safe_rows], 'sky', split_axis=0, concat_axis=0, t...  20.8 us
    all_to_all x2, waiting for transfers between devices, per_device(): lax.all_to_all(partial_value.astype(jnp.bfloat16), 'exp', split_axis=0, c...  17.2 us
  transfers between devices with their start and end apart: 9, of which 5 were waited for; matrix products, arithmetic and copies ran while one was open for 4% of the time, Pallas kernels for 0%

profile of v1, /device:TPU:6, one launch (start us, length us, event | category | flops | bytes accessed | tf_op | source)
XLA Modules:
  0.0 371.5 jit_solution(13441437539982861432)
XLA Ops:
  3.8 9.4 %all-to-all-start = ((s32[32,2,1]{1,2,0:T(1,128)}), s32[32,2,1]{1,2,0:T(1,128)S(1)}, u32[]{:S(2)}, u32[]{:S(2)}) async-start(s32[32,2,1]{1,2,0:T(1,128)} %bitcast.2), calls=%async_computation | async-start | bytes 32768 | tf_op jit(solution)/shard_map/all_to_all | solution.py:95
  14.5 4.2 %all-to-all-done = s32[32,2,1]{1,2,0:T(1,128)S(1)} async-done(((s32[32,2,1]{1,2,0:T(1,128)}), s32[32,2,1]{1,2,0:T(1,128)S(1)}, u32[]{:S(2)}, u32[]{:S(2)}) %all-to-all-start) | async-done | bytes 288 | tf_op jit(solution)/shard_map/all_to_all | solution.py:95
  20.0 2.1 gather_fusion
  22.2 5.9 %all-to-all-start.1 = ((bf16[64,128,128]{2,1,0:T(8,128)(2,1)}), bf16[64,128,128]{2,1,0:T(8,128)(2,1)S(1)}, u32[]{:S(2)}, u32[]{:S(2)}) async-start(bf16[64,128,128]{2,1,0:T(8,128)(2,1)} %gather_fusion), calls=%async_computation.1 | async-start | bytes 4194304 | tf_op jit(solution)/shard_map/all_to_all | solution.py:109
  29.8 3.2 copy.67
  32.9 20.8 %all-to-all-done.1 = bf16[64,128,128]{2,1,0:T(8,128)(2,1)S(1)} async-done(((bf16[64,128,128]{2,1,0:T(8,128)(2,1)}), bf16[64,128,128]{2,1,0:T(8,128)(2,1)S(1)}, u32[]{:S(2)}, u32[]{:S(2)}) %all-to-all-start.1) | async-done | bytes 2097184 | tf_op jit(solution)/shard_map/all_to_all | solution.py:109
  54.5 5.0 %fusion.1 = bf16[32,2,128,128]{3,2,1,0:T(8,128)(2,1)S(1)} fusion(bf16[1,32,2,128,128]{4,3,2,1,0:T(8,128)(2,1)} %param.8, f32[32,2]{1,0:T(8,128)S(1)} %copy.38, bf16[32,2,2,128,128]{4,3,2,1,0:T(8,128)(2,1)} %bitcast.123, bf16[32,128,128]{2,1,0:T(8,128)(2,1)S(1)} %gather_fusion.1), kind=kOutput, calls=%fused_computation.10 | convolution fusion | flops 542113792 | bytes 9437440 | tf_op jit(solution)/shard_map/fetv,fewv->fetw/dot_general | solution.py:43
  59.5 3.6 bitcast_convert_fusion.1
  64.0 2.7 all_to_all.34
  66.7 8.4 %all-to-all-start.2 = ((bf16[32,2,16384]{2,1,0:T(2,128)(2,1)}), bf16[32,2,16384]{2,1,0:T(2,128)(2,1)S(1)}, u32[]{:S(2)}, u32[]{:S(2)}) async-start(bf16[32,2,16384]{2,1,0:T(2,128)(2,1)} %all_to_all.34), calls=%async_computation.2 | async-start | bytes 4194304 | tf_op jit(solution)/shard_map/all_to_all | solution.py:117
  75.2 25.5 %all-to-all-done.2 = bf16[32,2,16384]{2,1,0:T(2,128)(2,1)S(1)} async-done(((bf16[32,2,16384]{2,1,0:T(2,128)(2,1)}), bf16[32,2,16384]{2,1,0:T(2,128)(2,1)S(1)}, u32[]{:S(2)}, u32[]{:S(2)}) %all-to-all-start.2) | async-done | bytes 2097184 | tf_op jit(solution)/shard_map/all_to_all | solution.py:117
  100.7 2.2 all_to_all.36
  105.9 13.4 %all-to-all-start.3 = ((bf16[16,128,128]{2,1,0:T(8,128)(2,1)}), bf16[16,128,128]{2,1,0:T(8,128)(2,1)}, u32[]{:S(2)}, u32[]{:S(2)}) async-start(bf16[16,128,128]{2,1,0:T(8,128)(2,1)} %copy.42), calls=%async_computation.3 | async-start | bytes 1048576 | tf_op jit(solution)/shard_map/all_to_all | solution.py:123
  120.0 3.1 collective-permute-start.1
  123.5 2.4 collective-permute-start
  127.9 41.0 %all-reduce.2 = f32[256]{0:T(256)S(1)} all-reduce(f32[256]{0:T(256)S(1)} %multiply_dynamic-update-slice_fusion), channel_id=2, replica_groups=mesh['exp'=16,'sky'=32] {'exp'}, use_global_device_ids=true, to_apply=%add.2 | all-reduce | flops 256 | bytes 2048
  173.8 29.8 %all_gather.11 = bf16[16,128,128]{2,1,0:T(8,128)(2,1)S(1)} all-gather(bf16[1,128,128]{2,1,0:T(8,128)(2,1)S(1)} %fusion.52), channel_id=1, replica_groups=mesh['exp'=16,'sky'=32] {'exp'}, dimensions={0}, use_global_device_ids=true | all-gather | bytes 557056 | tf_op jit(solution)/shard_map/all_gather | solution.py:132
  203.8 2.1 gather_fusion.2
  206.0 32.5 %all_to_all.50 = bf16[64,128,128]{2,1,0:T(8,128)(2,1)} all-to-all(bf16[64,128,128]{2,1,0:T(8,128)(2,1)} %gather_fusion.2), channel_id=1, replica_groups=mesh['exp'=16,'sky'=32] {'sky'}, dimensions={0} | all-to-all | bytes 4194304 | tf_op jit(solution)/shard_map/all_to_all | solution.py:109
  238.5 2.3 gather_fusion.3
  240.9 6.3 %fusion.3 = bf16[32,2,128,128]{3,2,1,0:T(8,128)(2,1)} fusion(bf16[1,32,2,128,128]{4,3,2,1,0:T(8,128)(2,1)} %param.8, f32[32,2]{1,0:T(8,128)S(1)} %copy.38, bf16[32,2,2,128,128]{4,3,2,1,0:T(8,128)(2,1)} %bitcast.125, bf16[32,128,128]{2,1,0:T(8,128)(2,1)S(1)} %gather_fusion.3), kind=kOutput, calls=%fused_computation.12 | convolution fusion | flops 542113792 | bytes 9437440 | tf_op jit(solution)/shard_map/fetv,fewv->fetw/dot_general | solution.py:43
  247.2 4.3 %bitcast_convert_fusion = bf16[32,128,128]{2,1,0:T(8,128)(2,1)S(1)} fusion(bf16[32,2,128,128]{3,2,1,0:T(8,128)(2,1)} %fusion.3, bf16[32,2,2,128,128]{4,3,2,1,0:T(8,128)(2,1)} %bitcast.126), kind=kOutput, calls=%fused_computation.24 | convolution fusion | flops 538443776 | bytes 7340032 | tf_op jit(solution)/shard_map/fetw,fewv->fetv/dot_general | solution.py:54
  251.5 2.2 convolution_convert_fusion.1
  253.7 4.4 %all_to_all.39 = bf16[32,2,16384]{2,1,0:T(2,128)(2,1)} reshape(bf16[64,16384]{1,0:T(8,128)(2,1)} %convolution_convert_fusion.1) | data formatting | bytes 4194304 | tf_op jit(solution)/shard_map/all_to_all | solution.py:117
  258.1 33.3 %all_to_all.51 = bf16[32,2,16384]{2,1,0:T(2,128)(2,1)} all-to-all(bf16[32,2,16384]{2,1,0:T(2,128)(2,1)} %all_to_all.39), channel_id=1, replica_groups=mesh['exp'=16,'sky'=32] {'sky'}, dimensions={0} | all-to-all | bytes 4194304 | tf_op jit(solution)/shard_map/all_to_all | solution.py:117
  291.4 4.1 %all_to_all.41 = bf16[64,16384]{1,0:T(8,128)(2,1)} reshape(bf16[32,2,16384]{2,1,0:T(2,128)(2,1)} %all_to_all.51) | data formatting | bytes 4194304 | tf_op jit(solution)/shard_map/all_to_all | solution.py:117
  298.4 10.4 %all-to-all-start.6 = ((bf16[16,128,128]{2,1,0:T(8,128)(2,1)}), bf16[16,128,128]{2,1,0:T(8,128)(2,1)}, u32[]{:S(2)}, u32[]{:S(2)}) async-start(bf16[16,128,128]{2,1,0:T(8,128)(2,1)} %copy.49), calls=%async_computation.6 | async-start | bytes 1048576 | tf_op jit(solution)/shard_map/all_to_all | solution.py:123
  309.5 2.8 collective-permute-start.3
  312.6 2.1 collective-permute-start.2
  315.1 2.5 collective-permute-done.2
  319.7 17.2 %all-to-all-done.6 = bf16[16,128,128]{2,1,0:T(8,128)(2,1)} async-done(((bf16[16,128,128]{2,1,0:T(8,128)(2,1)}), bf16[16,128,128]{2,1,0:T(8,128)(2,1)}, u32[]{:S(2)}, u32[]{:S(2)}) %all-to-all-start.6) | async-done | bytes 524320 | tf_op jit(solution)/shard_map/all_to_all | solution.py:123
  338.1 32.3 %all_gather.12 = bf16[16,128,128]{2,1,0:T(8,128)(2,1)S(1)} all-gather(bf16[1,128,128]{2,1,0:T(8,128)(2,1)S(1)} %fusion.50), channel_id=1, replica_groups=mesh['exp'=16,'sky'=32] {'exp'}, dimensions={0}, use_global_device_ids=true | all-gather | bytes 557056 | tf_op jit(solution)/shard_map/all_gather | solution.py:132
  (70 shorter events, 28.3 us)
Async XLA Ops:
  3.8 14.9 %all-to-all-start = ((s32[32,2,1]{1,2,0:T(1,128)}), s32[32,2,1]{1,2,0:T(1,128)S(1)}, u32[]{:S(2)}, u32[]{:S(2)}) async-start(s32[32,2,1]{1,2,0:T(1,128)} %bitcast.2), calls=%async_computation | async-start | bytes 32768 | tf_op jit(solution)/shard_map/all_to_all | solution.py:95
  22.2 5.9 %copy-start.4 = (bf16[1,32,2]{1,2,0:T(2,128)(2,1)S(1)}, bf16[1,32,2]{1,2,0:T(2,128)(2,1)}, u32[]{:S(2)}) copy-start(bf16[1,32,2]{1,2,0:T(2,128)(2,1)} %param.9) | copy-start | bytes 388
  22.2 6.0 %copy-start.2 = (s32[1,32,2,2]{1,3,2,0:T(2,128)S(1)}, s32[1,32,2,2]{1,3,2,0:T(2,128)}, u32[]{:S(2)}) copy-start(s32[1,32,2,2]{1,3,2,0:T(2,128)} %param.12) | copy-start | bytes 1540
  22.2 6.3 %copy-start.1 = (bf16[8,128,128]{2,1,0:T(8,128)(2,1)S(1)}, bf16[8,128,128]{2,1,0:T(8,128)(2,1)}, u32[]{:S(2)}) copy-start(bf16[8,128,128]{2,1,0:T(8,128)(2,1)} %param.13) | copy-start | bytes 786436
  22.2 31.5 %all-to-all-start.1 = ((bf16[64,128,128]{2,1,0:T(8,128)(2,1)}), bf16[64,128,128]{2,1,0:T(8,128)(2,1)S(1)}, u32[]{:S(2)}, u32[]{:S(2)}) async-start(bf16[64,128,128]{2,1,0:T(8,128)(2,1)} %gather_fusion), calls=%async_computation.1 | async-start | bytes 4194304 | tf_op jit(solution)/shard_map/all_to_all | solution.py:109
  29.7 3.2 copy-start.3
  66.7 34.0 %all-to-all-start.2 = ((bf16[32,2,16384]{2,1,0:T(2,128)(2,1)}), bf16[32,2,16384]{2,1,0:T(2,128)(2,1)S(1)}, u32[]{:S(2)}, u32[]{:S(2)}) async-start(bf16[32,2,16384]{2,1,0:T(2,128)(2,1)} %all_to_all.34), calls=%async_computation.2 | async-start | bytes 4194304 | tf_op jit(solution)/shard_map/all_to_all | solution.py:117
  102.9 16.4 %copy-start = (f32[16,128,128]{2,1,0:T(8,128)S(1)}, f32[16,128,128]{2,1,0:T(8,128)}, u32[]{:S(2)}) copy-start(f32[16,128,128]{2,1,0:T(8,128)} %param.7) | copy-start | bytes 3145732
  105.9 66.7 %all-to-all-start.3 = ((bf16[16,128,128]{2,1,0:T(8,128)(2,1)}), bf16[16,128,128]{2,1,0:T(8,128)(2,1)}, u32[]{:S(2)}, u32[]{:S(2)}) async-start(bf16[16,128,128]{2,1,0:T(8,128)(2,1)} %copy.42), calls=%async_computation.3 | async-start | bytes 1048576 | tf_op jit(solution)/shard_map/all_to_all | solution.py:123
  120.0 50.1 %collective-permute-start.1 = (f32[16,128,1]{1,0,2:T(8,128)S(1)}, f32[16,128,1]{1,0,2:T(8,128)S(1)}, u32[]{:S(2)}, u32[]{:S(2)}) collective-permute-start(f32[16,128,1]{1,0,2:T(8,128)S(1)} %copy.63), channel_id=1, source_target_pairs={{1,0},{2,1},{3,2},{4,3},{5,4},{6,5},{7,6},{8,7},{9,8},{10,9},{11,1... | collective-permute-start | bytes 24584 | tf_op jit(solution)/shard_map/ppermute | solution.py:22
  123.5 47.1 %collective-permute-start = (f32[16,128,1]{1,0,2:T(8,128)S(1)}, f32[16,128,1]{1,0,2:T(8,128)S(1)}, u32[]{:S(2)}, u32[]{:S(2)}) collective-permute-start(f32[16,128,1]{1,0,2:T(8,128)S(1)} %copy.62), channel_id=1, source_target_pairs={{0,1},{1,2},{2,3},{3,4},{4,5},{5,6},{6,7},{7,8},{8,9},{9,10},{10,1... | collective-permute-start | bytes 24584 | tf_op jit(solution)/shard_map/ppermute | solution.py:20
  298.4 38.5 %all-to-all-start.6 = ((bf16[16,128,128]{2,1,0:T(8,128)(2,1)}), bf16[16,128,128]{2,1,0:T(8,128)(2,1)}, u32[]{:S(2)}, u32[]{:S(2)}) async-start(bf16[16,128,128]{2,1,0:T(8,128)(2,1)} %copy.49), calls=%async_computation.6 | async-start | bytes 1048576 | tf_op jit(solution)/shard_map/all_to_all | solution.py:123
  309.5 5.3 %collective-permute-start.3 = (f32[16,128,1]{1,0,2:T(8,128)S(1)}, f32[16,128,1]{1,0,2:T(8,128)S(1)}, u32[]{:S(2)}, u32[]{:S(2)}) collective-permute-start(f32[16,128,1]{1,0,2:T(8,128)S(1)} %copy.51), channel_id=1, source_target_pairs={{1,0},{2,1},{3,2},{4,3},{5,4},{6,5},{7,6},{8,7},{9,8},{10,9},{11,1... | collective-permute-start | bytes 24584 | tf_op jit(solution)/shard_map/ppermute | solution.py:22
  312.6 5.0 %collective-permute-start.2 = (f32[16,128,1]{1,0,2:T(8,128)S(1)}, f32[16,128,1]{1,0,2:T(8,128)S(1)}, u32[]{:S(2)}, u32[]{:S(2)}) collective-permute-start(f32[16,128,1]{1,0,2:T(8,128)S(1)} %copy.50), channel_id=1, source_target_pairs={{0,1},{1,2},{2,3},{3,4},{4,5},{5,6},{6,7},{7,8},{8,9},{9,10},{10,1... | collective-permute-start | bytes 24584 | tf_op jit(solution)/shard_map/ppermute | solution.py:20

commit v2 on v0

--- a/solution.py
+++ b/solution.py
@@ -95,9 +95,14 @@
     incoming = lax.all_to_all(requested, "sky", split_axis=0, concat_axis=0, tiled=True)
     left_kernels, right_kernels = pick_kernels(kernel_ids, kernels)
     receive_map = jnp.arange(sky_rows, dtype=jnp.int32)[:, None] == incoming[None, :]
-    counts = float(expo_count) * jnp.sum(receive_map.astype(jnp.float32), axis=1)
+    local_counts = float(expo_count) * jnp.sum(receive_map.astype(jnp.float32), axis=1)
     receive_half = receive_map.astype(jnp.bfloat16)
     safe_rows = jnp.maximum(incoming, 0)
+    rows_per = sky_rows // n_exp
+    own_rows = lax.axis_index("exp") * rows_per
+    count_block = jnp.broadcast_to(
+        local_counts.astype(jnp.bfloat16)[None, :, None], (n_exp, sky_rows, tile_edge)
+    )
     sky_now = sky_start
     for iteration in range(ITERS):
         sky_half = sky_now.astype(jnp.bfloat16)
@@ -112,13 +117,22 @@
         arrived = lax.all_to_all(
             outgoing.astype(jnp.bfloat16), "sky", split_axis=0, concat_axis=0, tiled=True
         )
-        partial_value = jnp.dot(receive_half, arrived, preferred_element_type=jnp.float32).reshape(
-            sky_rows, tile_edge, tile_edge
-        )
+        partial_value = jnp.dot(receive_half, arrived, preferred_element_type=jnp.float32)
+        payload = partial_value.astype(jnp.bfloat16).reshape(n_exp, rows_per * tile_edge, tile_edge)
+        if iteration == 0:
+            payload = jnp.concatenate([payload, count_block], axis=1)
+        row_parts = lax.all_to_all(payload, "exp", split_axis=0, concat_axis=0, tiled=True)
+        summed = jnp.sum(row_parts.astype(jnp.float32).reshape((n_exp,) + payload.shape[1:]), axis=0)
+        if iteration == 0:
+            counts = summed[rows_per * tile_edge :, 0]
+            denominator = weight_ceiling * counts + 8.0 * prior_weight
+            own_denominator = lax.dynamic_slice_in_dim(denominator, own_rows, rows_per)
+        own_total = summed[: rows_per * tile_edge].reshape(rows_per, tile_edge, tile_edge)
+        scaled = own_total / own_denominator[:, None, None]
+        gathered = lax.all_gather(scaled.astype(jnp.bfloat16), "exp", axis=0, tiled=True)
         laplacian = laplace_image(padded_2(sky_now, (("sky", 2),), 1))
-        summed, summed_counts = lax.psum((partial_value, counts), "exp")
-        denominator = weight_ceiling * summed_counts[:, None, None] + 8.0 * prior_weight
-        sky_now = sky_now - (summed + prior_weight * laplacian) / denominator
+        smooth = prior_weight * laplacian / denominator[:, None, None]
+        sky_now = sky_now - (gathered.astype(jnp.float32) + smooth)
     return sky_now
 
 

time: 494 us -> 351 us (0.71)
  waiting for transfers between devices: 273 us -> 89.6 us
  blocking collectives: 101 us -> 135 us
  starting transfers between devices: 34.4 us -> 52.7 us
  between operations: 13.7 us -> 0.37 us
    psum x2 -> x0, waiting for transfers between devices: 226 us -> none  [per_device(): summed, summed_counts = lax.psum((partial_value, counts), 'exp')]
    all_gather x0 -> x2, blocking collectives: none -> 66.8 us  [per_device(): lax.all_gather(scaled.astype(jnp.bfloat16), 'exp', axis=0, tiled=True)]
    psum x1 -> x0, blocking collectives: 34.8 us -> none  [per_device(): summed, summed_counts = lax.psum((partial_value, counts), 'exp')]
    all_to_all x0 -> x2, waiting for transfers between devices: none -> 34.8 us  [per_device(): lax.all_to_all(payload, 'exp', split_axis=0, concat_axis=0, tiled=True)]
    all_to_all x0 -> x2, starting transfers between devices: none -> 18.4 us  [per_device(): lax.all_to_all(payload, 'exp', split_axis=0, concat_axis=0, tiled=True)]
    all_to_all x1, waiting for transfers between devices: 19.9 us -> 25.4 us  [per_device(): lax.all_to_all(outgoing.astype(jnp.bfloat16), 'sky', split_axis=0, concat...]
  transfers between devices with their start and end apart: 9 -> 9, of which waited for: 6 -> 7; matrix products, arithmetic and copies ran while one was open for 4% -> 4% of each run, Pallas kernels for 0% -> 0%
where the time goes in v2:
time: 351 us; the launch traced here: 346 us
  blocking collectives  135 us (38%)
  waiting for transfers between devices  89.6 us (26%)
  starting transfers between devices  52.7 us (15%)
  local copies, waits for them, and re-layouts  27.6 us (8%)
  matrix products  25.2 us (7%)
  other arithmetic  16.2 us (5%)
    all_gather x2, blocking collectives, per_device(): lax.all_gather(scaled.astype(jnp.bfloat16), 'exp', axis=0, tiled=True)  66.8 us
    all_to_all x2, waiting for transfers between devices, per_device(): lax.all_to_all(payload, 'exp', split_axis=0, concat_axis=0, tiled=True)  34.8 us
    all_to_all x1, blocking collectives, per_device(): lax.all_to_all(sky_half[safe_rows], 'sky', split_axis=0, concat_axis=0, t...  34.6 us
    all_to_all x1, blocking collectives, per_device(): lax.all_to_all(outgoing.astype(jnp.bfloat16), 'sky', split_axis=0, concat...  33.3 us
    all_to_all x1, waiting for transfers between devices, per_device(): lax.all_to_all(outgoing.astype(jnp.bfloat16), 'sky', split_axis=0, concat...  25.4 us
    all_to_all x1, waiting for transfers between devices, per_device(): lax.all_to_all(sky_half[safe_rows], 'sky', split_axis=0, concat_axis=0, t...  20.8 us
    all_to_all x2, starting transfers between devices, per_device(): lax.all_to_all(payload, 'exp', split_axis=0, concat_axis=0, tiled=True)  18.4 us
    dot_general x2, matrix products, adjoint_tiles(): jnp.einsum('fetv,fewv->fetw', left_product, right_kernels, preferred_elem...  10.3 us
  transfers between devices with their start and end apart: 9, of which 7 were waited for; matrix products, arithmetic and copies ran while one was open for 4% of the time, Pallas kernels for 0%

profile of v2, /device:TPU:6, one launch (start us, length us, event | category | flops | bytes accessed | tf_op | source)
XLA Modules:
  0.0 346.3 jit_solution(11392690573035063864)
XLA Ops:
  3.8 9.4 %all-to-all-start = ((s32[32,2,1]{1,2,0:T(1,128)}), s32[32,2,1]{1,2,0:T(1,128)S(1)}, u32[]{:S(2)}, u32[]{:S(2)}) async-start(s32[32,2,1]{1,2,0:T(1,128)} %bitcast.2), calls=%async_computation | async-start | bytes 32768 | tf_op jit(solution)/shard_map/all_to_all | solution.py:95
  14.5 4.2 %all-to-all-done = s32[32,2,1]{1,2,0:T(1,128)S(1)} async-done(((s32[32,2,1]{1,2,0:T(1,128)}), s32[32,2,1]{1,2,0:T(1,128)S(1)}, u32[]{:S(2)}, u32[]{:S(2)}) %all-to-all-start) | async-done | bytes 288 | tf_op jit(solution)/shard_map/all_to_all | solution.py:95
  20.0 2.1 gather_fusion
  22.2 5.9 %all-to-all-start.1 = ((bf16[64,128,128]{2,1,0:T(8,128)(2,1)}), bf16[64,128,128]{2,1,0:T(8,128)(2,1)S(1)}, u32[]{:S(2)}, u32[]{:S(2)}) async-start(bf16[64,128,128]{2,1,0:T(8,128)(2,1)} %gather_fusion), calls=%async_computation.1 | async-start | bytes 4194304 | tf_op jit(solution)/shard_map/all_to_all | solution.py:109
  29.8 3.2 copy.78
  32.9 20.8 %all-to-all-done.1 = bf16[64,128,128]{2,1,0:T(8,128)(2,1)S(1)} async-done(((bf16[64,128,128]{2,1,0:T(8,128)(2,1)}), bf16[64,128,128]{2,1,0:T(8,128)(2,1)S(1)}, u32[]{:S(2)}, u32[]{:S(2)}) %all-to-all-start.1) | async-done | bytes 2097184 | tf_op jit(solution)/shard_map/all_to_all | solution.py:109
  54.5 5.0 %fusion.1 = bf16[32,2,128,128]{3,2,1,0:T(8,128)(2,1)S(1)} fusion(bf16[1,32,2,128,128]{4,3,2,1,0:T(8,128)(2,1)} %param.8, f32[32,2]{1,0:T(8,128)S(1)} %copy.55, bf16[32,2,2,128,128]{4,3,2,1,0:T(8,128)(2,1)} %bitcast.98, bf16[32,128,128]{2,1,0:T(8,128)(2,1)S(1)} %gather_fusion.1), kind=kOutput, calls=%fused_computation.12 | convolution fusion | flops 542113792 | bytes 9437440 | tf_op jit(solution)/shard_map/fetv,fewv->fetw/dot_general | solution.py:43
  59.5 3.6 %bitcast_convert_fusion.1 = bf16[32,128,128]{2,1,0:T(8,128)(2,1)S(1)} fusion(bf16[32,2,128,128]{3,2,1,0:T(8,128)(2,1)S(1)} %fusion.1, bf16[32,2,2,128,128]{4,3,2,1,0:T(8,128)(2,1)} %bitcast.99), kind=kOutput, calls=%fused_computation.21 | convolution fusion | flops 538443776 | bytes 7340032 | tf_op jit(solution)/shard_map/fetw,fewv->fetv/dot_general | solution.py:54
  64.0 2.7 all_to_all.34
  66.7 8.4 %all-to-all-start.2 = ((bf16[32,2,16384]{2,1,0:T(2,128)(2,1)}), bf16[32,2,16384]{2,1,0:T(2,128)(2,1)S(1)}, u32[]{:S(2)}, u32[]{:S(2)}) async-start(bf16[32,2,16384]{2,1,0:T(2,128)(2,1)} %all_to_all.34), calls=%async_computation.2 | async-start | bytes 4194304 | tf_op jit(solution)/shard_map/all_to_all | solution.py:117
  75.3 25.4 %all-to-all-done.2 = bf16[32,2,16384]{2,1,0:T(2,128)(2,1)S(1)} async-done(((bf16[32,2,16384]{2,1,0:T(2,128)(2,1)}), bf16[32,2,16384]{2,1,0:T(2,128)(2,1)S(1)}, u32[]{:S(2)}, u32[]{:S(2)}) %all-to-all-start.2) | async-done | bytes 2097184 | tf_op jit(solution)/shard_map/all_to_all | solution.py:117
  100.7 2.2 all_to_all.36
  106.0 13.4 %all-to-all-start.3 = ((bf16[16,144,128]{2,1,0:T(8,128)(2,1)}), bf16[16,144,128]{2,1,0:T(8,128)(2,1)}, u32[]{:S(2)}, u32[]{:S(2)}) async-start(bf16[16,144,128]{2,1,0:T(8,128)(2,1)} %pad_maximum_fusion.2), calls=%async_computation.3 | async-start | bytes 1179648 | tf_op jit(solution)/shard_map/all_to_all | solution.py:124
  120.1 3.1 collective-permute-start.1
  123.5 2.6 collective-permute-start
  126.5 2.0 collective-permute-done
  131.6 17.5 %all-to-all-done.3 = bf16[16,144,128]{2,1,0:T(8,128)(2,1)} async-done(((bf16[16,144,128]{2,1,0:T(8,128)(2,1)}), bf16[16,144,128]{2,1,0:T(8,128)(2,1)}, u32[]{:S(2)}, u32[]{:S(2)}) %all-to-all-start.3) | async-done | bytes 589856 | tf_op jit(solution)/shard_map/all_to_all | solution.py:124
  151.5 34.5 %all-gather = bf16[2048,128]{1,0:T(8,128)(2,1)S(1)} all-gather(bf16[128,128]{1,0:T(8,128)(2,1)S(1)} %fusion.43), channel_id=2, replica_groups=mesh['exp'=16,'sky'=32] {'exp'}, dimensions={0}, use_global_device_ids=true | all-gather | bytes 557056 | tf_op jit(solution)/shard_map/all_gather | solution.py:132
  187.4 2.1 gather_fusion.2
  189.6 34.6 %all_to_all.50 = bf16[64,128,128]{2,1,0:T(8,128)(2,1)S(1)} all-to-all(bf16[64,128,128]{2,1,0:T(8,128)(2,1)} %gather_fusion.2), channel_id=1, replica_groups=mesh['exp'=16,'sky'=32] {'sky'}, dimensions={0} | all-to-all | bytes 4194304 | tf_op jit(solution)/shard_map/all_to_all | solution.py:109
  225.8 5.3 %fusion.3 = bf16[32,2,128,128]{3,2,1,0:T(8,128)(2,1)S(1)} fusion(bf16[1,32,2,128,128]{4,3,2,1,0:T(8,128)(2,1)} %param.8, f32[32,2]{1,0:T(8,128)S(1)} %copy.55, bf16[32,2,2,128,128]{4,3,2,1,0:T(8,128)(2,1)} %bitcast.100, bf16[32,128,128]{2,1,0:T(8,128)(2,1)} %gather_fusion.3), kind=kOutput, calls=%fused_computation.14 | convolution fusion | flops 542113792 | bytes 9437440 | tf_op jit(solution)/shard_map/fetv,fewv->fetw/dot_general | solution.py:43
  231.1 4.6 %bitcast_convert_fusion = bf16[32,128,128]{2,1,0:T(8,128)(2,1)} fusion(bf16[32,2,128,128]{3,2,1,0:T(8,128)(2,1)S(1)} %fusion.3, bf16[32,2,2,128,128]{4,3,2,1,0:T(8,128)(2,1)} %bitcast.101), kind=kOutput, calls=%fused_computation.20 | convolution fusion | flops 538443776 | bytes 7340032 | tf_op jit(solution)/shard_map/fetw,fewv->fetv/dot_general | solution.py:54
  235.7 2.1 convolution_convert_fusion.1
  237.9 2.7 all_to_all.39
  240.5 33.3 %all_to_all.51 = bf16[32,2,16384]{2,1,0:T(2,128)(2,1)} all-to-all(bf16[32,2,16384]{2,1,0:T(2,128)(2,1)} %all_to_all.39), channel_id=1, replica_groups=mesh['exp'=16,'sky'=32] {'sky'}, dimensions={0} | all-to-all | bytes 4194304 | tf_op jit(solution)/shard_map/all_to_all | solution.py:117
  273.8 2.7 all_to_all.41
  277.9 5.0 %all-to-all-start.6 = ((bf16[16,128,128]{2,1,0:T(8,128)(2,1)}), bf16[16,128,128]{2,1,0:T(8,128)(2,1)}, u32[]{:S(2)}, u32[]{:S(2)}) async-start(bf16[16,128,128]{2,1,0:T(8,128)(2,1)} %bitcast.47), calls=%async_computation.6 | async-start | bytes 1048576 | tf_op jit(solution)/shard_map/all_to_all | solution.py:124
  283.6 2.8 collective-permute-start.3
  286.7 2.1 collective-permute-start.2
  289.3 2.5 collective-permute-done.2
  293.8 17.3 %all-to-all-done.6 = bf16[16,128,128]{2,1,0:T(8,128)(2,1)} async-done(((bf16[16,128,128]{2,1,0:T(8,128)(2,1)}), bf16[16,128,128]{2,1,0:T(8,128)(2,1)}, u32[]{:S(2)}, u32[]{:S(2)}) %all-to-all-start.6) | async-done | bytes 524320 | tf_op jit(solution)/shard_map/all_to_all | solution.py:124
  312.8 32.3 %all-gather.1 = bf16[2048,128]{1,0:T(8,128)(2,1)S(1)} all-gather(bf16[128,128]{1,0:T(8,128)(2,1)S(1)} %divide_convert_fusion), channel_id=3, replica_groups=mesh['exp'=16,'sky'=32] {'exp'}, dimensions={0}, use_global_device_ids=true | all-gather | bytes 557056 | tf_op jit(solution)/shard_map/all_gather | solution.py:132
  (68 shorter events, 30.7 us)
Async XLA Ops:
  3.8 14.9 %all-to-all-start = ((s32[32,2,1]{1,2,0:T(1,128)}), s32[32,2,1]{1,2,0:T(1,128)S(1)}, u32[]{:S(2)}, u32[]{:S(2)}) async-start(s32[32,2,1]{1,2,0:T(1,128)} %bitcast.2), calls=%async_computation | async-start | bytes 32768 | tf_op jit(solution)/shard_map/all_to_all | solution.py:95
  22.2 5.9 %copy-start.4 = (bf16[1,32,2]{1,2,0:T(2,128)(2,1)S(1)}, bf16[1,32,2]{1,2,0:T(2,128)(2,1)}, u32[]{:S(2)}) copy-start(bf16[1,32,2]{1,2,0:T(2,128)(2,1)} %param.9) | copy-start | bytes 388
  22.2 6.0 %copy-start.2 = (s32[1,32,2,2]{1,3,2,0:T(2,128)S(1)}, s32[1,32,2,2]{1,3,2,0:T(2,128)}, u32[]{:S(2)}) copy-start(s32[1,32,2,2]{1,3,2,0:T(2,128)} %param.12) | copy-start | bytes 1540
  22.2 6.3 %copy-start.1 = (bf16[8,128,128]{2,1,0:T(8,128)(2,1)S(1)}, bf16[8,128,128]{2,1,0:T(8,128)(2,1)}, u32[]{:S(2)}) copy-start(bf16[8,128,128]{2,1,0:T(8,128)(2,1)} %param.13) | copy-start | bytes 786436
  22.2 31.5 %all-to-all-start.1 = ((bf16[64,128,128]{2,1,0:T(8,128)(2,1)}), bf16[64,128,128]{2,1,0:T(8,128)(2,1)S(1)}, u32[]{:S(2)}, u32[]{:S(2)}) async-start(bf16[64,128,128]{2,1,0:T(8,128)(2,1)} %gather_fusion), calls=%async_computation.1 | async-start | bytes 4194304 | tf_op jit(solution)/shard_map/all_to_all | solution.py:109
  29.7 3.2 copy-start.3
  66.7 34.0 %all-to-all-start.2 = ((bf16[32,2,16384]{2,1,0:T(2,128)(2,1)}), bf16[32,2,16384]{2,1,0:T(2,128)(2,1)S(1)}, u32[]{:S(2)}, u32[]{:S(2)}) async-start(bf16[32,2,16384]{2,1,0:T(2,128)(2,1)} %all_to_all.34), calls=%async_computation.2 | async-start | bytes 4194304 | tf_op jit(solution)/shard_map/all_to_all | solution.py:117
  104.9 14.5 %copy-start = (f32[16,128,128]{2,1,0:T(8,128)S(1)}, f32[16,128,128]{2,1,0:T(8,128)}, u32[]{:S(2)}) copy-start(f32[16,128,128]{2,1,0:T(8,128)} %param.7) | copy-start | bytes 3145732
  106.0 43.1 %all-to-all-start.3 = ((bf16[16,144,128]{2,1,0:T(8,128)(2,1)}), bf16[16,144,128]{2,1,0:T(8,128)(2,1)}, u32[]{:S(2)}, u32[]{:S(2)}) async-start(bf16[16,144,128]{2,1,0:T(8,128)(2,1)} %pad_maximum_fusion.2), calls=%async_computation.3 | async-start | bytes 1179648 | tf_op jit(solution)/shard_map/all_to_all | solution.py:124
  120.1 6.0 %collective-permute-start.1 = (f32[16,128,1]{1,0,2:T(8,128)S(1)}, f32[16,128,1]{1,0,2:T(8,128)S(1)}, u32[]{:S(2)}, u32[]{:S(2)}) collective-permute-start(f32[16,128,1]{1,0,2:T(8,128)S(1)} %copy.76), channel_id=1, source_target_pairs={{1,0},{2,1},{3,2},{4,3},{5,4},{6,5},{7,6},{8,7},{9,8},{10,9},{11,1... | collective-permute-start | bytes 24584 | tf_op jit(solution)/shard_map/ppermute | solution.py:22
  123.5 5.0 %collective-permute-start = (f32[16,128,1]{1,0,2:T(8,128)S(1)}, f32[16,128,1]{1,0,2:T(8,128)S(1)}, u32[]{:S(2)}, u32[]{:S(2)}) collective-permute-start(f32[16,128,1]{1,0,2:T(8,128)S(1)} %copy.75), channel_id=1, source_target_pairs={{0,1},{1,2},{2,3},{3,4},{4,5},{5,6},{6,7},{7,8},{8,9},{9,10},{10,1... | collective-permute-start | bytes 24584 | tf_op jit(solution)/shard_map/ppermute | solution.py:20
  277.9 33.2 %all-to-all-start.6 = ((bf16[16,128,128]{2,1,0:T(8,128)(2,1)}), bf16[16,128,128]{2,1,0:T(8,128)(2,1)}, u32[]{:S(2)}, u32[]{:S(2)}) async-start(bf16[16,128,128]{2,1,0:T(8,128)(2,1)} %bitcast.47), calls=%async_computation.6 | async-start | bytes 1048576 | tf_op jit(solution)/shard_map/all_to_all | solution.py:124
  283.6 5.3 %collective-permute-start.3 = (f32[16,128,1]{1,0,2:T(8,128)S(1)}, f32[16,128,1]{1,0,2:T(8,128)S(1)}, u32[]{:S(2)}, u32[]{:S(2)}) collective-permute-start(f32[16,128,1]{1,0,2:T(8,128)S(1)} %copy.64), channel_id=1, source_target_pairs={{1,0},{2,1},{3,2},{4,3},{5,4},{6,5},{7,6},{8,7},{9,8},{10,9},{11,1... | collective-permute-start | bytes 24584 | tf_op jit(solution)/shard_map/ppermute | solution.py:22
  286.7 5.0 %collective-permute-start.2 = (f32[16,128,1]{1,0,2:T(8,128)S(1)}, f32[16,128,1]{1,0,2:T(8,128)S(1)}, u32[]{:S(2)}, u32[]{:S(2)}) collective-permute-start(f32[16,128,1]{1,0,2:T(8,128)S(1)} %copy.63), channel_id=1, source_target_pairs={{0,1},{1,2},{2,3},{3,4},{4,5},{5,6},{6,7},{7,8},{8,9},{9,10},{10,1... | collective-permute-start | bytes 24584 | tf_op jit(solution)/shard_map/ppermute | solution.py:20

commit v3 on v2

--- a/solution.py
+++ b/solution.py
@@ -87,8 +87,9 @@
     ranks = jnp.sum((jnp.cumsum(onehot_owner, axis=0) - onehot_owner) * onehot_owner, axis=1)
     slot_of = owner_ids * capacity + ranks
     packing = jnp.arange(slot_count, dtype=jnp.int32)[:, None] == slot_of[None, :]
-    packing_half = packing.astype(jnp.bfloat16)
     requested = jnp.sum(jnp.where(packing, tile_rows[None, :] + 1, 0), axis=1) - 1
+    slot_source = jnp.sum(jnp.where(packing, jnp.arange(foot_tiles)[None, :] + 1, 0), axis=1) - 1
+    slot_source = jnp.where(slot_source < 0, foot_tiles, slot_source)
     observed = exposures[0]
     tile_weights = weights[0]
     kernel_ids = kernel_index[0]
@@ -111,13 +112,14 @@
         )
         fetched = replies[slot_of]
         adjoint = adjoint_tiles(fetched, left_kernels, right_kernels, tile_weights, observed)
-        outgoing = jnp.dot(
-            packing_half, adjoint.reshape(foot_tiles, -1), preferred_element_type=jnp.float32
+        padded_adjoint = jnp.concatenate(
+            [adjoint, jnp.zeros((1, tile_edge, tile_edge), adjoint.dtype)], axis=0
         )
-        arrived = lax.all_to_all(
-            outgoing.astype(jnp.bfloat16), "sky", split_axis=0, concat_axis=0, tiled=True
+        outgoing = padded_adjoint[slot_source]
+        arrived = lax.all_to_all(outgoing, "sky", split_axis=0, concat_axis=0, tiled=True)
+        partial_value = jnp.einsum(
+            "rj,juv->ruv", receive_half, arrived, preferred_element_type=jnp.float32
         )
-        partial_value = jnp.dot(receive_half, arrived, preferred_element_type=jnp.float32)
         payload = partial_value.astype(jnp.bfloat16).reshape(n_exp, rows_per * tile_edge, tile_edge)
         if iteration == 0:
             payload = jnp.concatenate([payload, count_block], axis=1)

time: 351 us -> 346 us (0.986)
  local copies, waits for them, and re-layouts: 27.6 us -> 23.4 us
    all_to_all x4 -> x0, local copies, waits for them, and re-layouts: 10.3 us -> none  [per_device(): lax.all_to_all(outgoing.astype(jnp.bfloat16), 'sky', split_axis=0, concat...]
    gather x0 -> x2, local copies, waits for them, and re-layouts: none -> 4.32 us  [per_device(): outgoing = padded_adjoint[slot_source]]
where the time goes in v3:
time: 346 us; the launch traced here: 341 us
  blocking collectives  134 us (39%)
  waiting for transfers between devices  89.5 us (26%)
  starting transfers between devices  52.7 us (15%)
  matrix products  25 us (7%)
  local copies, waits for them, and re-layouts  23.4 us (7%)
  other arithmetic  15.5 us (4%)
    all_gather x2, blocking collectives, per_device(): lax.all_gather(scaled.astype(jnp.bfloat16), 'exp', axis=0, tiled=True)  66.8 us
    all_to_all x2, waiting for transfers between devices, per_device(): lax.all_to_all(payload, 'exp', split_axis=0, concat_axis=0, tiled=True)  34.8 us
    all_to_all x1, blocking collectives, per_device(): lax.all_to_all(sky_half[safe_rows], 'sky', split_axis=0, concat_axis=0, t...  34.7 us
    all_to_all x1, blocking collectives, per_device(): lax.all_to_all(outgoing, 'sky', split_axis=0, concat_axis=0, tiled=True)  32.6 us
    all_to_all x1, waiting for transfers between devices, per_device(): lax.all_to_all(outgoing, 'sky', split_axis=0, concat_axis=0, tiled=True)  25.4 us
    all_to_all x1, waiting for transfers between devices, per_device(): lax.all_to_all(sky_half[safe_rows], 'sky', split_axis=0, concat_axis=0, t...  20.7 us
    all_to_all x2, starting transfers between devices, per_device(): lax.all_to_all(payload, 'exp', split_axis=0, concat_axis=0, tiled=True)  18.4 us
    dot_general x2, matrix products, adjoint_tiles(): jnp.einsum('fetv,fewv->fetw', left_product, right_kernels, preferred_elem...  12.7 us
  transfers between devices with their start and end apart: 9, of which 7 were waited for; matrix products, arithmetic and copies ran while one was open for 4% of the time, Pallas kernels for 0%

profile of v3, /device:TPU:6, one launch (start us, length us, event | category | flops | bytes accessed | tf_op | source)
XLA Modules:
  0.0 340.5 jit_solution(9868937879238891678)
XLA Ops:
  3.8 9.4 %all-to-all-start = ((s32[32,2,1]{1,2,0:T(1,128)}), s32[32,2,1]{1,2,0:T(1,128)S(1)}, u32[]{:S(2)}, u32[]{:S(2)}) async-start(s32[32,2,1]{1,2,0:T(1,128)} %bitcast.2), calls=%async_computation | async-start | bytes 32768 | tf_op jit(solution)/shard_map/all_to_all | solution.py:96
  14.5 4.2 %all-to-all-done = s32[32,2,1]{1,2,0:T(1,128)S(1)} async-done(((s32[32,2,1]{1,2,0:T(1,128)}), s32[32,2,1]{1,2,0:T(1,128)S(1)}, u32[]{:S(2)}, u32[]{:S(2)}) %all-to-all-start) | async-done | bytes 288 | tf_op jit(solution)/shard_map/all_to_all | solution.py:96
  20.0 2.1 gather_fusion
  22.2 5.9 %all-to-all-start.1 = ((bf16[64,128,128]{2,1,0:T(8,128)(2,1)}), bf16[64,128,128]{2,1,0:T(8,128)(2,1)S(1)}, u32[]{:S(2)}, u32[]{:S(2)}) async-start(bf16[64,128,128]{2,1,0:T(8,128)(2,1)} %gather_fusion), calls=%async_computation.1 | async-start | bytes 4194304 | tf_op jit(solution)/shard_map/all_to_all | solution.py:110
  29.8 3.2 copy.100
  33.0 20.7 %all-to-all-done.1 = bf16[64,128,128]{2,1,0:T(8,128)(2,1)S(1)} async-done(((bf16[64,128,128]{2,1,0:T(8,128)(2,1)}), bf16[64,128,128]{2,1,0:T(8,128)(2,1)S(1)}, u32[]{:S(2)}, u32[]{:S(2)}) %all-to-all-start.1) | async-done | bytes 2097184 | tf_op jit(solution)/shard_map/all_to_all | solution.py:110
  54.5 6.3 %fusion.1 = bf16[32,2,128,128]{3,2,1,0:T(8,128)(2,1)} fusion(bf16[1,32,2,128,128]{4,3,2,1,0:T(8,128)(2,1)} %param.8, f32[32,2]{1,0:T(8,128)S(1)} %copy.67, bf16[32,2,2,128,128]{4,3,2,1,0:T(8,128)(2,1)} %bitcast.90, bf16[32,128,128]{2,1,0:T(8,128)(2,1)S(1)} %gather_fusion.1), kind=kOutput, calls=%fused_computation.10 | convolution fusion | flops 542113792 | bytes 9437440 | tf_op jit(solution)/shard_map/fetv,fewv->fetw/dot_general | solution.py:43
  60.8 4.3 %bitcast_convert_fusion.1 = bf16[32,128,128]{2,1,0:T(8,128)(2,1)S(1)} fusion(bf16[32,2,128,128]{3,2,1,0:T(8,128)(2,1)} %fusion.1, bf16[32,2,2,128,128]{4,3,2,1,0:T(8,128)(2,1)} %bitcast.91), kind=kOutput, calls=%fused_computation.19 | convolution fusion | flops 538443776 | bytes 7340032 | tf_op jit(solution)/shard_map/fetw,fewv->fetv/dot_general | solution.py:54
  65.2 2.1 gather_fusion.2
  67.4 8.4 %all-to-all-start.2 = ((bf16[64,128,128]{2,1,0:T(8,128)(2,1)}), bf16[64,128,128]{2,1,0:T(8,128)(2,1)S(1)}, u32[]{:S(2)}, u32[]{:S(2)}) async-start(bf16[64,128,128]{2,1,0:T(8,128)(2,1)} %gather_fusion.2), calls=%async_computation.2 | async-start | bytes 4194304 | tf_op jit(solution)/shard_map/all_to_all | solution.py:119
  76.0 25.4 %all-to-all-done.2 = bf16[64,128,128]{2,1,0:T(8,128)(2,1)S(1)} async-done(((bf16[64,128,128]{2,1,0:T(8,128)(2,1)}), bf16[64,128,128]{2,1,0:T(8,128)(2,1)S(1)}, u32[]{:S(2)}, u32[]{:S(2)}) %all-to-all-start.2) | async-done | bytes 2097184 | tf_op jit(solution)/shard_map/all_to_all | solution.py:119
  103.8 13.4 %all-to-all-start.3 = ((bf16[16,144,128]{2,1,0:T(8,128)(2,1)}), bf16[16,144,128]{2,1,0:T(8,128)(2,1)}, u32[]{:S(2)}, u32[]{:S(2)}) async-start(bf16[16,144,128]{2,1,0:T(8,128)(2,1)} %copy.71), calls=%async_computation.3 | async-start | bytes 1179648 | tf_op jit(solution)/shard_map/all_to_all | solution.py:126
  117.9 3.1 collective-permute-start.1
  121.3 2.6 collective-permute-start
  124.3 2.0 collective-permute-done
  127.9 1.5 fusion.38
  129.4 17.5 %all-to-all-done.3 = bf16[16,144,128]{2,1,0:T(8,128)(2,1)} async-done(((bf16[16,144,128]{2,1,0:T(8,128)(2,1)}), bf16[16,144,128]{2,1,0:T(8,128)(2,1)}, u32[]{:S(2)}, u32[]{:S(2)}) %all-to-all-start.3) | async-done | bytes 589856 | tf_op jit(solution)/shard_map/all_to_all | solution.py:126
  149.2 34.5 %all-gather = bf16[2048,128]{1,0:T(8,128)(2,1)S(1)} all-gather(bf16[128,128]{1,0:T(8,128)(2,1)S(1)} %fusion.47), channel_id=2, replica_groups=mesh['exp'=16,'sky'=32] {'exp'}, dimensions={0}, use_global_device_ids=true | all-gather | bytes 557056 | tf_op jit(solution)/shard_map/all_gather | solution.py:134
  183.7 1.5 fusion.60
  185.2 2.1 gather_fusion.3
  187.4 34.7 %all_to_all.36 = bf16[64,128,128]{2,1,0:T(8,128)(2,1)} all-to-all(bf16[64,128,128]{2,1,0:T(8,128)(2,1)} %gather_fusion.3), channel_id=1, replica_groups=mesh['exp'=16,'sky'=32] {'sky'}, dimensions={0} | all-to-all | bytes 4194304 | tf_op jit(solution)/shard_map/all_to_all | solution.py:110
  222.0 2.3 gather_fusion.4
  224.4 6.3 %fusion.3 = bf16[32,2,128,128]{3,2,1,0:T(8,128)(2,1)} fusion(bf16[1,32,2,128,128]{4,3,2,1,0:T(8,128)(2,1)} %param.8, f32[32,2]{1,0:T(8,128)S(1)} %copy.67, bf16[32,2,2,128,128]{4,3,2,1,0:T(8,128)(2,1)} %bitcast.92, bf16[32,128,128]{2,1,0:T(8,128)(2,1)S(1)} %gather_fusion.4), kind=kOutput, calls=%fused_computation.12 | convolution fusion | flops 542113792 | bytes 9437440 | tf_op jit(solution)/shard_map/fetv,fewv->fetw/dot_general | solution.py:43
  230.7 4.3 %bitcast_convert_fusion = bf16[32,128,128]{2,1,0:T(8,128)(2,1)S(1)} fusion(bf16[32,2,128,128]{3,2,1,0:T(8,128)(2,1)} %fusion.3, bf16[32,2,2,128,128]{4,3,2,1,0:T(8,128)(2,1)} %bitcast.93), kind=kOutput, calls=%fused_computation.18 | convolution fusion | flops 538443776 | bytes 7340032 | tf_op jit(solution)/shard_map/fetw,fewv->fetv/dot_general | solution.py:54
  235.1 2.2 gather_fusion.5
  237.3 32.6 %all_to_all.37 = bf16[64,128,128]{2,1,0:T(8,128)(2,1)S(1)} all-to-all(bf16[64,128,128]{2,1,0:T(8,128)(2,1)} %gather_fusion.5), channel_id=1, replica_groups=mesh['exp'=16,'sky'=32] {'sky'}, dimensions={0} | all-to-all | bytes 4194304 | tf_op jit(solution)/shard_map/all_to_all | solution.py:119
  272.1 5.1 %all-to-all-start.6 = ((bf16[16,128,128]{2,1,0:T(8,128)(2,1)}), bf16[16,128,128]{2,1,0:T(8,128)(2,1)}, u32[]{:S(2)}, u32[]{:S(2)}) async-start(bf16[16,128,128]{2,1,0:T(8,128)(2,1)} %copy.79), calls=%async_computation.6 | async-start | bytes 1048576 | tf_op jit(solution)/shard_map/all_to_all | solution.py:126
  277.8 2.8 collective-permute-start.3
  280.9 2.1 collective-permute-start.2
  283.5 2.5 collective-permute-done.2
  288.0 17.3 %all-to-all-done.6 = bf16[16,128,128]{2,1,0:T(8,128)(2,1)} async-done(((bf16[16,128,128]{2,1,0:T(8,128)(2,1)}), bf16[16,128,128]{2,1,0:T(8,128)(2,1)}, u32[]{:S(2)}, u32[]{:S(2)}) %all-to-all-start.6) | async-done | bytes 524320 | tf_op jit(solution)/shard_map/all_to_all | solution.py:126
  307.0 32.3 %all-gather.1 = bf16[2048,128]{1,0:T(8,128)(2,1)S(1)} all-gather(bf16[128,128]{1,0:T(8,128)(2,1)S(1)} %divide_convert_fusion), channel_id=3, replica_groups=mesh['exp'=16,'sky'=32] {'exp'}, dimensions={0}, use_global_device_ids=true | all-gather | bytes 557056 | tf_op jit(solution)/shard_map/all_gather | solution.py:134
  (68 shorter events, 25.6 us)
Async XLA Ops:
  3.8 14.9 %all-to-all-start = ((s32[32,2,1]{1,2,0:T(1,128)}), s32[32,2,1]{1,2,0:T(1,128)S(1)}, u32[]{:S(2)}, u32[]{:S(2)}) async-start(s32[32,2,1]{1,2,0:T(1,128)} %bitcast.2), calls=%async_computation | async-start | bytes 32768 | tf_op jit(solution)/shard_map/all_to_all | solution.py:96
  22.2 5.9 %copy-start.4 = (bf16[1,32,2]{1,2,0:T(2,128)(2,1)S(1)}, bf16[1,32,2]{1,2,0:T(2,128)(2,1)}, u32[]{:S(2)}) copy-start(bf16[1,32,2]{1,2,0:T(2,128)(2,1)} %param.9) | copy-start | bytes 388
  22.2 6.0 %copy-start.3 = (s32[1,32,2,2]{1,3,2,0:T(2,128)S(1)}, s32[1,32,2,2]{1,3,2,0:T(2,128)}, u32[]{:S(2)}) copy-start(s32[1,32,2,2]{1,3,2,0:T(2,128)} %param.12) | copy-start | bytes 1540
  22.2 6.3 %copy-start.1 = (bf16[8,128,128]{2,1,0:T(8,128)(2,1)S(1)}, bf16[8,128,128]{2,1,0:T(8,128)(2,1)}, u32[]{:S(2)}) copy-start(bf16[8,128,128]{2,1,0:T(8,128)(2,1)} %param.13) | copy-start | bytes 786436
  22.2 31.5 %all-to-all-start.1 = ((bf16[64,128,128]{2,1,0:T(8,128)(2,1)}), bf16[64,128,128]{2,1,0:T(8,128)(2,1)S(1)}, u32[]{:S(2)}, u32[]{:S(2)}) async-start(bf16[64,128,128]{2,1,0:T(8,128)(2,1)} %gather_fusion), calls=%async_computation.1 | async-start | bytes 4194304 | tf_op jit(solution)/shard_map/all_to_all | solution.py:110
  29.8 3.2 copy-start.2
  67.4 34.0 %all-to-all-start.2 = ((bf16[64,128,128]{2,1,0:T(8,128)(2,1)}), bf16[64,128,128]{2,1,0:T(8,128)(2,1)S(1)}, u32[]{:S(2)}, u32[]{:S(2)}) async-start(bf16[64,128,128]{2,1,0:T(8,128)(2,1)} %gather_fusion.2), calls=%async_computation.2 | async-start | bytes 4194304 | tf_op jit(solution)/shard_map/all_to_all | solution.py:119
  102.6 14.6 %copy-start = (f32[16,128,128]{2,1,0:T(8,128)S(1)}, f32[16,128,128]{2,1,0:T(8,128)}, u32[]{:S(2)}) copy-start(f32[16,128,128]{2,1,0:T(8,128)} %param.7) | copy-start | bytes 3145732
  103.8 43.1 %all-to-all-start.3 = ((bf16[16,144,128]{2,1,0:T(8,128)(2,1)}), bf16[16,144,128]{2,1,0:T(8,128)(2,1)}, u32[]{:S(2)}, u32[]{:S(2)}) async-start(bf16[16,144,128]{2,1,0:T(8,128)(2,1)} %copy.71), calls=%async_computation.3 | async-start | bytes 1179648 | tf_op jit(solution)/shard_map/all_to_all | solution.py:126
  117.9 6.0 %collective-permute-start.1 = (f32[16,128,1]{1,0,2:T(8,128)S(1)}, f32[16,128,1]{1,0,2:T(8,128)S(1)}, u32[]{:S(2)}, u32[]{:S(2)}) collective-permute-start(f32[16,128,1]{1,0,2:T(8,128)S(1)} %copy.98), channel_id=1, source_target_pairs={{1,0},{2,1},{3,2},{4,3},{5,4},{6,5},{7,6},{8,7},{9,8},{10,9},{11,1... | collective-permute-start | bytes 24584 | tf_op jit(solution)/shard_map/ppermute | solution.py:22
  121.3 5.0 %collective-permute-start = (f32[16,128,1]{1,0,2:T(8,128)S(1)}, f32[16,128,1]{1,0,2:T(8,128)S(1)}, u32[]{:S(2)}, u32[]{:S(2)}) collective-permute-start(f32[16,128,1]{1,0,2:T(8,128)S(1)} %copy.97), channel_id=1, source_target_pairs={{0,1},{1,2},{2,3},{3,4},{4,5},{5,6},{6,7},{7,8},{8,9},{9,10},{10,1... | collective-permute-start | bytes 24584 | tf_op jit(solution)/shard_map/ppermute | solution.py:20
  272.1 33.2 %all-to-all-start.6 = ((bf16[16,128,128]{2,1,0:T(8,128)(2,1)}), bf16[16,128,128]{2,1,0:T(8,128)(2,1)}, u32[]{:S(2)}, u32[]{:S(2)}) async-start(bf16[16,128,128]{2,1,0:T(8,128)(2,1)} %copy.79), calls=%async_computation.6 | async-start | bytes 1048576 | tf_op jit(solution)/shard_map/all_to_all | solution.py:126
  277.8 5.3 %collective-permute-start.3 = (f32[16,128,1]{1,0,2:T(8,128)S(1)}, f32[16,128,1]{1,0,2:T(8,128)S(1)}, u32[]{:S(2)}, u32[]{:S(2)}) collective-permute-start(f32[16,128,1]{1,0,2:T(8,128)S(1)} %copy.82), channel_id=1, source_target_pairs={{1,0},{2,1},{3,2},{4,3},{5,4},{6,5},{7,6},{8,7},{9,8},{10,9},{11,1... | collective-permute-start | bytes 24584 | tf_op jit(solution)/shard_map/ppermute | solution.py:22
  280.9 5.0 %collective-permute-start.2 = (f32[16,128,1]{1,0,2:T(8,128)S(1)}, f32[16,128,1]{1,0,2:T(8,128)S(1)}, u32[]{:S(2)}, u32[]{:S(2)}) collective-permute-start(f32[16,128,1]{1,0,2:T(8,128)S(1)} %copy.81), channel_id=1, source_target_pairs={{0,1},{1,2},{2,3},{3,4},{4,5},{5,6},{6,7},{7,8},{8,9},{9,10},{10,1... | collective-permute-start | bytes 24584 | tf_op jit(solution)/shard_map/ppermute | solution.py:20

commit v4 on v3

--- a/solution.py
+++ b/solution.py
@@ -131,7 +131,15 @@
             own_denominator = lax.dynamic_slice_in_dim(denominator, own_rows, rows_per)
         own_total = summed[: rows_per * tile_edge].reshape(rows_per, tile_edge, tile_edge)
         scaled = own_total / own_denominator[:, None, None]
-        gathered = lax.all_gather(scaled.astype(jnp.bfloat16), "exp", axis=0, tiled=True)
+        gathered = lax.all_to_all(
+            jnp.broadcast_to(scaled.astype(jnp.bfloat16)[None], (n_exp,) + scaled.shape).reshape(
+                sky_rows, tile_edge, tile_edge
+            ),
+            "exp",
+            split_axis=0,
+            concat_axis=0,
+            tiled=True,
+        )
         laplacian = laplace_image(padded_2(sky_now, (("sky", 2),), 1))
         smooth = prior_weight * laplacian / denominator[:, None, None]
         sky_now = sky_now - (gathered.astype(jnp.float32) + smooth)

time: 346 us -> 352 us (1.017)
  blocking collectives: 134 us -> 99.5 us
  waiting for transfers between devices: 89.5 us -> 119 us
  starting transfers between devices: 52.7 us -> 66.9 us
    all_gather x2 -> x0, blocking collectives: 66.8 us -> none  [per_device(): lax.all_gather(scaled.astype(jnp.bfloat16), 'exp', axis=0, tiled=True)]
    all_to_all x0 -> x2, waiting for transfers between devices: none -> 37.6 us  [per_device(): lax.all_to_all(jnp.broadcast_to(scaled.astype(jnp.bfloat16)[None], (n_exp...]
    all_to_all x0 -> x1, blocking collectives: none -> 34.3 us  [per_device(): lax.all_to_all(payload, 'exp', split_axis=0, concat_axis=0, tiled=True)]
    all_to_all x0 -> x2, starting transfers between devices: none -> 18.7 us  [per_device(): lax.all_to_all(jnp.broadcast_to(scaled.astype(jnp.bfloat16)[None], (n_exp...]
    all_to_all x2 -> x1, waiting for transfers between devices: 34.8 us -> 29.6 us  [per_device(): lax.all_to_all(payload, 'exp', split_axis=0, concat_axis=0, tiled=True)]
    all_to_all x2 -> x1, starting transfers between devices: 18.4 us -> 13.3 us  [per_device(): lax.all_to_all(payload, 'exp', split_axis=0, concat_axis=0, tiled=True)]
    ppermute x2, waiting for transfers between devices: 4.45 us -> 0.01 us  [padded_2(): lax.ppermute(tail, axis, [(i, (i + 1) % count) for i in range(ends)])]
  transfers between devices with their start and end apart: 9 -> 10, of which waited for: 7 -> 8; matrix products, arithmetic and copies ran while one was open for 4% -> 4% of each run, Pallas kernels for 0% -> 0%
where the time goes in v4:
time: 352 us; the launch traced here: 350 us
  waiting for transfers between devices  119 us (34%)
  blocking collectives  99.5 us (28%)
  starting transfers between devices  66.9 us (19%)
  matrix products  25 us (7%)
  local copies, waits for them, and re-layouts  24.5 us (7%)
  other arithmetic  14.5 us (4%)
    all_to_all x2, waiting for transfers between devices, per_device(): lax.all_to_all(jnp.broadcast_to(scaled.astype(jnp.bfloat16)[None], (n_exp...  37.6 us
    all_to_all x1, blocking collectives, per_device(): lax.all_to_all(payload, 'exp', split_axis=0, concat_axis=0, tiled=True)  34.3 us
    all_to_all x1, blocking collectives, per_device(): lax.all_to_all(sky_half[safe_rows], 'sky', split_axis=0, concat_axis=0, t...  32.6 us
    all_to_all x1, blocking collectives, per_device(): lax.all_to_all(outgoing, 'sky', split_axis=0, concat_axis=0, tiled=True)  32.6 us
    all_to_all x1, waiting for transfers between devices, per_device(): lax.all_to_all(payload, 'exp', split_axis=0, concat_axis=0, tiled=True)  29.6 us
    all_to_all x1, waiting for transfers between devices, per_device(): lax.all_to_all(outgoing, 'sky', split_axis=0, concat_axis=0, tiled=True)  25.4 us
    all_to_all x1, waiting for transfers between devices, per_device(): lax.all_to_all(sky_half[safe_rows], 'sky', split_axis=0, concat_axis=0, t...  20.7 us
    all_to_all x2, starting transfers between devices, per_device(): lax.all_to_all(jnp.broadcast_to(scaled.astype(jnp.bfloat16)[None], (n_exp...  18.7 us
  transfers between devices with their start and end apart: 10, of which 8 were waited for; matrix products, arithmetic and copies ran while one was open for 4% of the time, Pallas kernels for 0%

profile of v4, /device:TPU:6, one launch (start us, length us, event | category | flops | bytes accessed | tf_op | source)
XLA Modules:
  0.0 350.0 jit_solution(12505673563416578064)
XLA Ops:
  3.8 9.4 %all-to-all-start = ((s32[32,2,1]{1,2,0:T(1,128)}), s32[32,2,1]{1,2,0:T(1,128)S(1)}, u32[]{:S(2)}, u32[]{:S(2)}) async-start(s32[32,2,1]{1,2,0:T(1,128)} %bitcast.2), calls=%async_computation | async-start | bytes 32768 | tf_op jit(solution)/shard_map/all_to_all | solution.py:96
  14.5 4.2 %all-to-all-done = s32[32,2,1]{1,2,0:T(1,128)S(1)} async-done(((s32[32,2,1]{1,2,0:T(1,128)}), s32[32,2,1]{1,2,0:T(1,128)S(1)}, u32[]{:S(2)}, u32[]{:S(2)}) %all-to-all-start) | async-done | bytes 288 | tf_op jit(solution)/shard_map/all_to_all | solution.py:96
  20.0 2.1 gather_fusion
  22.2 5.9 %all-to-all-start.1 = ((bf16[64,128,128]{2,1,0:T(8,128)(2,1)}), bf16[64,128,128]{2,1,0:T(8,128)(2,1)S(1)}, u32[]{:S(2)}, u32[]{:S(2)}) async-start(bf16[64,128,128]{2,1,0:T(8,128)(2,1)} %gather_fusion), calls=%async_computation.1 | async-start | bytes 4194304 | tf_op jit(solution)/shard_map/all_to_all | solution.py:110
  29.7 3.2 copy.100
  33.0 20.7 %all-to-all-done.1 = bf16[64,128,128]{2,1,0:T(8,128)(2,1)S(1)} async-done(((bf16[64,128,128]{2,1,0:T(8,128)(2,1)}), bf16[64,128,128]{2,1,0:T(8,128)(2,1)S(1)}, u32[]{:S(2)}, u32[]{:S(2)}) %all-to-all-start.1) | async-done | bytes 2097184 | tf_op jit(solution)/shard_map/all_to_all | solution.py:110
  54.5 6.3 %fusion.1 = bf16[32,2,128,128]{3,2,1,0:T(8,128)(2,1)} fusion(bf16[1,32,2,128,128]{4,3,2,1,0:T(8,128)(2,1)} %param.8, f32[32,2]{1,0:T(8,128)S(1)} %copy.67, bf16[32,2,2,128,128]{4,3,2,1,0:T(8,128)(2,1)} %bitcast.86, bf16[32,128,128]{2,1,0:T(8,128)(2,1)S(1)} %gather_fusion.1), kind=kOutput, calls=%fused_computation.10 | convolution fusion | flops 542113792 | bytes 9437440 | tf_op jit(solution)/shard_map/fetv,fewv->fetw/dot_general | solution.py:43
  60.8 4.3 %bitcast_convert_fusion.1 = bf16[32,128,128]{2,1,0:T(8,128)(2,1)S(1)} fusion(bf16[32,2,128,128]{3,2,1,0:T(8,128)(2,1)} %fusion.1, bf16[32,2,2,128,128]{4,3,2,1,0:T(8,128)(2,1)} %bitcast.87), kind=kOutput, calls=%fused_computation.19 | convolution fusion | flops 538443776 | bytes 7340032 | tf_op jit(solution)/shard_map/fetw,fewv->fetv/dot_general | solution.py:54
  65.2 2.1 gather_fusion.2
  67.4 8.4 %all-to-all-start.2 = ((bf16[64,128,128]{2,1,0:T(8,128)(2,1)}), bf16[64,128,128]{2,1,0:T(8,128)(2,1)S(1)}, u32[]{:S(2)}, u32[]{:S(2)}) async-start(bf16[64,128,128]{2,1,0:T(8,128)(2,1)} %gather_fusion.2), calls=%async_computation.2 | async-start | bytes 4194304 | tf_op jit(solution)/shard_map/all_to_all | solution.py:119
  76.0 25.4 %all-to-all-done.2 = bf16[64,128,128]{2,1,0:T(8,128)(2,1)S(1)} async-done(((bf16[64,128,128]{2,1,0:T(8,128)(2,1)}), bf16[64,128,128]{2,1,0:T(8,128)(2,1)S(1)}, u32[]{:S(2)}, u32[]{:S(2)}) %all-to-all-start.2) | async-done | bytes 2097184 | tf_op jit(solution)/shard_map/all_to_all | solution.py:119
  103.8 13.3 %all-to-all-start.3 = ((bf16[16,144,128]{2,1,0:T(8,128)(2,1)}), bf16[16,144,128]{2,1,0:T(8,128)(2,1)S(1)}, u32[]{:S(2)}, u32[]{:S(2)}) async-start(bf16[16,144,128]{2,1,0:T(8,128)(2,1)} %copy.71), calls=%async_computation.3 | async-start | bytes 1179648 | tf_op jit(solution)/shard_map/all_to_all | solution.py:126
  117.1 29.6 %all-to-all-done.3 = bf16[16,144,128]{2,1,0:T(8,128)(2,1)S(1)} async-done(((bf16[16,144,128]{2,1,0:T(8,128)(2,1)}), bf16[16,144,128]{2,1,0:T(8,128)(2,1)S(1)}, u32[]{:S(2)}, u32[]{:S(2)}) %all-to-all-start.3) | async-done | bytes 589856 | tf_op jit(solution)/shard_map/all_to_all | solution.py:126
  149.0 9.9 %all-to-all-start.4 = ((bf16[16,128,128]{2,1,0:T(8,128)(2,1)}), bf16[16,128,128]{2,1,0:T(8,128)(2,1)}, u32[]{:S(2)}, u32[]{:S(2)}) async-start(bf16[16,128,128]{2,1,0:T(8,128)(2,1)} %reshape.169), calls=%async_computation.4 | async-start | bytes 1048576 | tf_op jit(solution)/shard_map/all_to_all | solution.py:134
  159.6 1.9 collective-permute-start
  161.9 3.8 %collective-permute-start.1 = (f32[16,128,1]{1,0,2:T(8,128)S(1)}, f32[16,128,1]{1,0,2:T(8,128)S(1)}, u32[]{:S(2)}, u32[]{:S(2)}) collective-permute-start(f32[16,128,1]{1,0,2:T(8,128)S(1)} %copy.98), channel_id=1, source_target_pairs={{1,0},{2,1},{3,2},{4,3},{5,4},{6,5},{7,6},{8,7},{9,8},{10,9},{11,1... | collective-permute-start | bytes 24584 | tf_op jit(solution)/shard_map/ppermute | solution.py:22
  168.4 1.5 fusion.38
  169.9 18.3 %all-to-all-done.4 = bf16[16,128,128]{2,1,0:T(8,128)(2,1)} async-done(((bf16[16,128,128]{2,1,0:T(8,128)(2,1)}), bf16[16,128,128]{2,1,0:T(8,128)(2,1)}, u32[]{:S(2)}, u32[]{:S(2)}) %all-to-all-start.4) | async-done | bytes 524320 | tf_op jit(solution)/shard_map/all_to_all | solution.py:134
  188.2 1.6 fusion.58
  189.9 2.1 gather_fusion.3
  192.0 32.6 %all_to_all.46 = bf16[64,128,128]{2,1,0:T(8,128)(2,1)} all-to-all(bf16[64,128,128]{2,1,0:T(8,128)(2,1)} %gather_fusion.3), channel_id=1, replica_groups=mesh['exp'=16,'sky'=32] {'sky'}, dimensions={0} | all-to-all | bytes 4194304 | tf_op jit(solution)/shard_map/all_to_all | solution.py:110
  224.6 2.3 gather_fusion.4
  226.9 6.3 %fusion.3 = bf16[32,2,128,128]{3,2,1,0:T(8,128)(2,1)} fusion(bf16[1,32,2,128,128]{4,3,2,1,0:T(8,128)(2,1)} %param.8, f32[32,2]{1,0:T(8,128)S(1)} %copy.67, bf16[32,2,2,128,128]{4,3,2,1,0:T(8,128)(2,1)} %bitcast.88, bf16[32,128,128]{2,1,0:T(8,128)(2,1)S(1)} %gather_fusion.4), kind=kOutput, calls=%fused_computation.12 | convolution fusion | flops 542113792 | bytes 9437440 | tf_op jit(solution)/shard_map/fetv,fewv->fetw/dot_general | solution.py:43
  233.3 4.3 %bitcast_convert_fusion = bf16[32,128,128]{2,1,0:T(8,128)(2,1)S(1)} fusion(bf16[32,2,128,128]{3,2,1,0:T(8,128)(2,1)} %fusion.3, bf16[32,2,2,128,128]{4,3,2,1,0:T(8,128)(2,1)} %bitcast.89), kind=kOutput, calls=%fused_computation.18 | convolution fusion | flops 538443776 | bytes 7340032 | tf_op jit(solution)/shard_map/fetw,fewv->fetv/dot_general | solution.py:54
  237.7 2.2 gather_fusion.5
  239.8 32.6 %all_to_all.47 = bf16[64,128,128]{2,1,0:T(8,128)(2,1)S(1)} all-to-all(bf16[64,128,128]{2,1,0:T(8,128)(2,1)} %gather_fusion.5), channel_id=1, replica_groups=mesh['exp'=16,'sky'=32] {'sky'}, dimensions={0} | all-to-all | bytes 4194304 | tf_op jit(solution)/shard_map/all_to_all | solution.py:119
  273.8 34.3 %all_to_all.48 = bf16[16,128,128]{2,1,0:T(8,128)(2,1)S(1)} all-to-all(bf16[16,128,128]{2,1,0:T(8,128)(2,1)S(1)} %copy.79), channel_id=1, replica_groups=mesh['exp'=16,'sky'=32] {'exp'}, dimensions={0} | all-to-all | bytes 1048576 | tf_op jit(solution)/shard_map/all_to_all | solution.py:126
  309.7 8.7 %all-to-all-start.8 = ((bf16[16,128,128]{2,1,0:T(8,128)(2,1)}), bf16[16,128,128]{2,1,0:T(8,128)(2,1)}, u32[]{:S(2)}, u32[]{:S(2)}) async-start(bf16[16,128,128]{2,1,0:T(8,128)(2,1)} %reshape.171), calls=%async_computation.8 | async-start | bytes 1048576 | tf_op jit(solution)/shard_map/all_to_all | solution.py:134
  319.1 1.9 collective-permute-start.2
  321.4 3.6 %collective-permute-start.3 = (f32[16,128,1]{1,0,2:T(8,128)S(1)}, f32[16,128,1]{1,0,2:T(8,128)S(1)}, u32[]{:S(2)}, u32[]{:S(2)}) collective-permute-start(f32[16,128,1]{1,0,2:T(8,128)S(1)} %copy.82), channel_id=1, source_target_pairs={{1,0},{2,1},{3,2},{4,3},{5,4},{6,5},{7,6},{8,7},{9,8},{10,9},{11,1... | collective-permute-start | bytes 24584 | tf_op jit(solution)/shard_map/ppermute | solution.py:22
  328.5 19.3 %all-to-all-done.8 = bf16[16,128,128]{2,1,0:T(8,128)(2,1)} async-done(((bf16[16,128,128]{2,1,0:T(8,128)(2,1)}), bf16[16,128,128]{2,1,0:T(8,128)(2,1)}, u32[]{:S(2)}, u32[]{:S(2)}) %all-to-all-start.8) | async-done | bytes 524320 | tf_op jit(solution)/shard_map/all_to_all | solution.py:134
  347.7 2.3 add_subtract_fusion
  (71 shorter events, 25.0 us)
Async XLA Ops:
  3.8 14.9 %all-to-all-start = ((s32[32,2,1]{1,2,0:T(1,128)}), s32[32,2,1]{1,2,0:T(1,128)S(1)}, u32[]{:S(2)}, u32[]{:S(2)}) async-start(s32[32,2,1]{1,2,0:T(1,128)} %bitcast.2), calls=%async_computation | async-start | bytes 32768 | tf_op jit(solution)/shard_map/all_to_all | solution.py:96
  22.2 5.9 %copy-start.3 = (s32[1,32,2,2]{1,3,2,0:T(2,128)S(1)}, s32[1,32,2,2]{1,3,2,0:T(2,128)}, u32[]{:S(2)}) copy-start(s32[1,32,2,2]{1,3,2,0:T(2,128)} %param.12) | copy-start | bytes 1540
  22.2 6.2 %copy-start.1 = (bf16[8,128,128]{2,1,0:T(8,128)(2,1)S(1)}, bf16[8,128,128]{2,1,0:T(8,128)(2,1)}, u32[]{:S(2)}) copy-start(bf16[8,128,128]{2,1,0:T(8,128)(2,1)} %param.13) | copy-start | bytes 786436
  22.2 31.5 %all-to-all-start.1 = ((bf16[64,128,128]{2,1,0:T(8,128)(2,1)}), bf16[64,128,128]{2,1,0:T(8,128)(2,1)S(1)}, u32[]{:S(2)}, u32[]{:S(2)}) async-start(bf16[64,128,128]{2,1,0:T(8,128)(2,1)} %gather_fusion), calls=%async_computation.1 | async-start | bytes 4194304 | tf_op jit(solution)/shard_map/all_to_all | solution.py:110
  29.7 3.2 copy-start.4
  29.7 3.3 copy-start.2
  67.4 34.0 %all-to-all-start.2 = ((bf16[64,128,128]{2,1,0:T(8,128)(2,1)}), bf16[64,128,128]{2,1,0:T(8,128)(2,1)S(1)}, u32[]{:S(2)}, u32[]{:S(2)}) async-start(bf16[64,128,128]{2,1,0:T(8,128)(2,1)} %gather_fusion.2), calls=%async_computation.2 | async-start | bytes 4194304 | tf_op jit(solution)/shard_map/all_to_all | solution.py:119
  102.8 56.1 %copy-start = (f32[16,128,128]{2,1,0:T(8,128)S(1)}, f32[16,128,128]{2,1,0:T(8,128)}, u32[]{:S(2)}) copy-start(f32[16,128,128]{2,1,0:T(8,128)} %param.7) | copy-start | bytes 3145732
  103.8 42.9 %all-to-all-start.3 = ((bf16[16,144,128]{2,1,0:T(8,128)(2,1)}), bf16[16,144,128]{2,1,0:T(8,128)(2,1)S(1)}, u32[]{:S(2)}, u32[]{:S(2)}) async-start(bf16[16,144,128]{2,1,0:T(8,128)(2,1)} %copy.71), calls=%async_computation.3 | async-start | bytes 1179648 | tf_op jit(solution)/shard_map/all_to_all | solution.py:126
  149.0 39.2 %all-to-all-start.4 = ((bf16[16,128,128]{2,1,0:T(8,128)(2,1)}), bf16[16,128,128]{2,1,0:T(8,128)(2,1)}, u32[]{:S(2)}, u32[]{:S(2)}) async-start(bf16[16,128,128]{2,1,0:T(8,128)(2,1)} %reshape.169), calls=%async_computation.4 | async-start | bytes 1048576 | tf_op jit(solution)/shard_map/all_to_all | solution.py:134
  159.6 6.1 %collective-permute-start = (f32[16,128,1]{1,0,2:T(8,128)S(1)}, f32[16,128,1]{1,0,2:T(8,128)S(1)}, u32[]{:S(2)}, u32[]{:S(2)}) collective-permute-start(f32[16,128,1]{1,0,2:T(8,128)S(1)} %copy.97), channel_id=1, source_target_pairs={{0,1},{1,2},{2,3},{3,4},{4,5},{5,6},{6,7},{7,8},{8,9},{9,10},{10,1... | collective-permute-start | bytes 24584 | tf_op jit(solution)/shard_map/ppermute | solution.py:20
  161.9 5.0 %collective-permute-start.1 = (f32[16,128,1]{1,0,2:T(8,128)S(1)}, f32[16,128,1]{1,0,2:T(8,128)S(1)}, u32[]{:S(2)}, u32[]{:S(2)}) collective-permute-start(f32[16,128,1]{1,0,2:T(8,128)S(1)} %copy.98), channel_id=1, source_target_pairs={{1,0},{2,1},{3,2},{4,3},{5,4},{6,5},{7,6},{8,7},{9,8},{10,9},{11,1... | collective-permute-start | bytes 24584 | tf_op jit(solution)/shard_map/ppermute | solution.py:22
  309.7 38.1 %all-to-all-start.8 = ((bf16[16,128,128]{2,1,0:T(8,128)(2,1)}), bf16[16,128,128]{2,1,0:T(8,128)(2,1)}, u32[]{:S(2)}, u32[]{:S(2)}) async-start(bf16[16,128,128]{2,1,0:T(8,128)(2,1)} %reshape.171), calls=%async_computation.8 | async-start | bytes 1048576 | tf_op jit(solution)/shard_map/all_to_all | solution.py:134
  319.1 5.9 %collective-permute-start.2 = (f32[16,128,1]{1,0,2:T(8,128)S(1)}, f32[16,128,1]{1,0,2:T(8,128)S(1)}, u32[]{:S(2)}, u32[]{:S(2)}) collective-permute-start(f32[16,128,1]{1,0,2:T(8,128)S(1)} %copy.81), channel_id=1, source_target_pairs={{0,1},{1,2},{2,3},{3,4},{4,5},{5,6},{6,7},{7,8},{8,9},{9,10},{10,1... | collective-permute-start | bytes 24584 | tf_op jit(solution)/shard_map/ppermute | solution.py:20
  321.4 5.0 %collective-permute-start.3 = (f32[16,128,1]{1,0,2:T(8,128)S(1)}, f32[16,128,1]{1,0,2:T(8,128)S(1)}, u32[]{:S(2)}, u32[]{:S(2)}) collective-permute-start(f32[16,128,1]{1,0,2:T(8,128)S(1)} %copy.82), channel_id=1, source_target_pairs={{1,0},{2,1},{3,2},{4,3},{5,4},{6,5},{7,6},{8,7},{9,8},{10,9},{11,1... | collective-permute-start | bytes 24584 | tf_op jit(solution)/shard_map/ppermute | solution.py:22

commit v5 on v3

--- a/solution.py
+++ b/solution.py
@@ -104,37 +104,91 @@
     count_block = jnp.broadcast_to(
         local_counts.astype(jnp.bfloat16)[None, :, None], (n_exp, sky_rows, tile_edge)
     )
+    half_edge = tile_edge // 2
+
+    def exchange(outgoing_rows, extra, arrived_already=False):
+        arrived = outgoing_rows
+        if not arrived_already:
+            arrived = lax.all_to_all(outgoing_rows, "sky", split_axis=0, concat_axis=0, tiled=True)
+        partial_value = jnp.einsum(
+            "rj,juv->ruv", receive_half, arrived, preferred_element_type=jnp.float32
+        )
+        payload = partial_value.astype(jnp.bfloat16).reshape(
+            n_exp, rows_per * outgoing_rows.shape[1], tile_edge
+        )
+        if extra is not None:
+            payload = jnp.concatenate([payload, extra], axis=1)
+        row_parts = lax.all_to_all(payload, "exp", split_axis=0, concat_axis=0, tiled=True)
+        return jnp.sum(row_parts.astype(jnp.float32).reshape((n_exp,) + payload.shape[1:]), axis=0)
+
+    def fetch(part):
+        replies = lax.all_to_all(
+            part.astype(jnp.bfloat16)[safe_rows], "sky", split_axis=0, concat_axis=0, tiled=True
+        )
+        return replies[slot_of]
+
+    def gather_scaled(summed, own_denominator):
+        piece_edge = summed.shape[0] // rows_per
+        own_total = summed.reshape(rows_per, piece_edge, tile_edge)
+        scaled = (own_total / own_denominator[:, None, None]).astype(jnp.bfloat16)
+        return scaled
+
     sky_now = sky_start
+    fetched = None
     for iteration in range(ITERS):
-        sky_half = sky_now.astype(jnp.bfloat16)
-        replies = lax.all_to_all(
-            sky_half[safe_rows], "sky", split_axis=0, concat_axis=0, tiled=True
-        )
-        fetched = replies[slot_of]
+        if fetched is None:
+            fetched = fetch(sky_now)
         adjoint = adjoint_tiles(fetched, left_kernels, right_kernels, tile_weights, observed)
         padded_adjoint = jnp.concatenate(
             [adjoint, jnp.zeros((1, tile_edge, tile_edge), adjoint.dtype)], axis=0
         )
         outgoing = padded_adjoint[slot_source]
-        arrived = lax.all_to_all(outgoing, "sky", split_axis=0, concat_axis=0, tiled=True)
-        partial_value = jnp.einsum(
-            "rj,juv->ruv", receive_half, arrived, preferred_element_type=jnp.float32
-        )
-        payload = partial_value.astype(jnp.bfloat16).reshape(n_exp, rows_per * tile_edge, tile_edge)
+        laplacian = laplace_image(padded_2(sky_now, (("sky", 2),), 1))
         if iteration == 0:
-            payload = jnp.concatenate([payload, count_block], axis=1)
-        row_parts = lax.all_to_all(payload, "exp", split_axis=0, concat_axis=0, tiled=True)
-        summed = jnp.sum(row_parts.astype(jnp.float32).reshape((n_exp,) + payload.shape[1:]), axis=0)
-        if iteration == 0:
-            counts = summed[rows_per * tile_edge :, 0]
+            summed = exchange(outgoing[:, :half_edge], count_block)
+            counts = summed[rows_per * half_edge :, 0]
             denominator = weight_ceiling * counts + 8.0 * prior_weight
             own_denominator = lax.dynamic_slice_in_dim(denominator, own_rows, rows_per)
-        own_total = summed[: rows_per * tile_edge].reshape(rows_per, tile_edge, tile_edge)
-        scaled = own_total / own_denominator[:, None, None]
-        gathered = lax.all_gather(scaled.astype(jnp.bfloat16), "exp", axis=0, tiled=True)
-        laplacian = laplace_image(padded_2(sky_now, (("sky", 2),), 1))
-        smooth = prior_weight * laplacian / denominator[:, None, None]
-        sky_now = sky_now - (gathered.astype(jnp.float32) + smooth)
+            summed_head = summed[: rows_per * half_edge]
+            smooth = prior_weight * laplacian / denominator[:, None, None]
+        else:
+            smooth = prior_weight * laplacian / denominator[:, None, None]
+            if iteration + 1 == ITERS:
+                scaled = gather_scaled(exchange(outgoing, None), own_denominator)
+                gathered = lax.all_gather(scaled, "exp", axis=0, tiled=True)
+                sky_now = sky_now - (gathered.astype(jnp.float32) + smooth)
+                continue
+            summed_head = exchange(outgoing[:, :half_edge], None)
+        scaled_head = gather_scaled(summed_head, own_denominator)
+        scaled_head, outgoing_tail = lax.optimization_barrier(
+            (scaled_head, outgoing[:, half_edge:])
+        )
+        gathered_head = lax.all_gather(scaled_head, "exp", axis=0, tiled=True)
+        arrived_tail = lax.all_to_all(outgoing_tail, "sky", split_axis=0, concat_axis=0, tiled=True)
+        gathered_head, arrived_tail = lax.optimization_barrier((gathered_head, arrived_tail))
+        scaled_tail = gather_scaled(exchange(arrived_tail, None, True), own_denominator)
+        sky_head = sky_now[:, :half_edge] - (
+            gathered_head.astype(jnp.float32) + smooth[:, :half_edge]
+        )
+        if iteration + 1 == ITERS:
+            gathered_tail = lax.all_gather(scaled_tail, "exp", axis=0, tiled=True)
+            sky_tail = sky_now[:, half_edge:] - (
+                gathered_tail.astype(jnp.float32) + smooth[:, half_edge:]
+            )
+            sky_now = jnp.concatenate([sky_head, sky_tail], axis=1)
+            continue
+        request_head = sky_head.astype(jnp.bfloat16)[safe_rows]
+        request_head, scaled_tail = lax.optimization_barrier((request_head, scaled_tail))
+        gathered_tail = lax.all_gather(scaled_tail, "exp", axis=0, tiled=True)
+        fetched_head = lax.all_to_all(
+            request_head, "sky", split_axis=0, concat_axis=0, tiled=True
+        )[slot_of]
+        gathered_tail, fetched_head = lax.optimization_barrier((gathered_tail, fetched_head))
+        sky_tail = sky_now[:, half_edge:] - (
+            gathered_tail.astype(jnp.float32) + smooth[:, half_edge:]
+        )
+        fetched = jnp.concatenate([fetched_head, fetch(sky_tail)], axis=1)
+        sky_now = jnp.concatenate([sky_head, sky_tail], axis=1)
     return sky_now
 
 

time: 346 us -> 393 us (1.14)
  blocking collectives: 134 us -> 153 us
  starting transfers between devices: 52.7 us -> 71.2 us
    all_gather x2 -> x3, blocking collectives: 66.8 us -> 99.6 us  [the longest x1 34.8 us: per_device(): gathered = lax.all_gather(scaled, 'exp', axis=0, tiled=True)]
    all_to_all x4 -> x7, starting transfers between devices: 32.7 us -> 51.8 us  [the longest x3 22.1 us: exchange(): lax.all_to_all(payload, 'exp', split_axis=0, concat_axis=0, tiled=True)]
    all_to_all x2, blocking collectives: 67.2 us -> 53.9 us  [the longest x1 31.9 us: exchange(): lax.all_to_all(outgoing_rows, 'sky', split_axis=0, concat_axis=0, tiled=T...]
    ppermute x2, waiting for transfers between devices: 0.01 us -> 6.27 us  [padded_2(): lax.ppermute(head, axis, [((i + 1) % count, i) for i in range(ends)])]
    all_to_all x4 -> x7, waiting for transfers between devices: 80.9 us -> 80.1 us  [the longest x3 45 us: exchange(): lax.all_to_all(payload, 'exp', split_axis=0, concat_axis=0, tiled=True)]
  transfers between devices with their start and end apart: 9 -> 12, of which waited for: 7 -> 8; matrix products, arithmetic and copies ran while one was open for 4% -> 6% of each run, Pallas kernels for 0% -> 0%
where the time goes in v5:
time: 393 us; the launch traced here: 389 us
  blocking collectives  153 us (39%)
  waiting for transfers between devices  92.8 us (24%)
  starting transfers between devices  71.2 us (18%)
  local copies, waits for them, and re-layouts  26.6 us (7%)
  matrix products  26.3 us (7%)
  other arithmetic  18.5 us (5%)
    all_to_all x3, waiting for transfers between devices, exchange(): lax.all_to_all(payload, 'exp', split_axis=0, concat_axis=0, tiled=True)  45 us
    all_gather x1, blocking collectives, per_device(): gathered = lax.all_gather(scaled, 'exp', axis=0, tiled=True)  34.8 us
    all_gather x1, blocking collectives, per_device(): gathered_head = lax.all_gather(scaled_head, 'exp', axis=0, tiled=True)  33.8 us
    all_to_all x1, blocking collectives, exchange(): lax.all_to_all(outgoing_rows, 'sky', split_axis=0, concat_axis=0, tiled=T...  31.9 us
    all_gather x1, blocking collectives, per_device(): gathered_tail = lax.all_gather(scaled_tail, 'exp', axis=0, tiled=True)  31.1 us
    all_to_all x3, starting transfers between devices, exchange(): lax.all_to_all(payload, 'exp', split_axis=0, concat_axis=0, tiled=True)  22.1 us
    all_to_all x1, blocking collectives, fetch(): lax.all_to_all(part.astype(jnp.bfloat16)[safe_rows], 'sky', split_axis=0,...  21.9 us
    all_to_all x1, waiting for transfers between devices, fetch(): lax.all_to_all(part.astype(jnp.bfloat16)[safe_rows], 'sky', split_axis=0,...  20.7 us
  transfers between devices with their start and end apart: 12, of which 8 were waited for; matrix products, arithmetic and copies ran while one was open for 6% of the time, Pallas kernels for 0%

profile of v5, /device:TPU:6, one launch (start us, length us, event | category | flops | bytes accessed | tf_op | source)
XLA Modules:
  0.0 389.3 jit_solution(12822003709473119195)
XLA Ops:
  3.8 9.4 %all-to-all-start = ((s32[32,2,1]{1,2,0:T(1,128)}), s32[32,2,1]{1,2,0:T(1,128)S(1)}, u32[]{:S(2)}, u32[]{:S(2)}) async-start(s32[32,2,1]{1,2,0:T(1,128)} %bitcast.2), calls=%async_computation | async-start | bytes 32768 | tf_op jit(solution)/shard_map/all_to_all | solution.py:96
  14.5 4.2 %all-to-all-done = s32[32,2,1]{1,2,0:T(1,128)S(1)} async-done(((s32[32,2,1]{1,2,0:T(1,128)}), s32[32,2,1]{1,2,0:T(1,128)S(1)}, u32[]{:S(2)}, u32[]{:S(2)}) %all-to-all-start) | async-done | bytes 288 | tf_op jit(solution)/shard_map/all_to_all | solution.py:96
  20.0 2.1 gather_fusion
  22.2 5.9 %all-to-all-start.1 = ((bf16[64,128,128]{2,1,0:T(8,128)(2,1)}), bf16[64,128,128]{2,1,0:T(8,128)(2,1)S(1)}, u32[]{:S(2)}, u32[]{:S(2)}) async-start(bf16[64,128,128]{2,1,0:T(8,128)(2,1)} %gather_fusion), calls=%async_computation.1 | async-start | bytes 4194304 | tf_op jit(solution)/shard_map/all_to_all | solution.py:125
  29.8 3.2 copy.72
  33.0 20.7 %all-to-all-done.1 = bf16[64,128,128]{2,1,0:T(8,128)(2,1)S(1)} async-done(((bf16[64,128,128]{2,1,0:T(8,128)(2,1)}), bf16[64,128,128]{2,1,0:T(8,128)(2,1)S(1)}, u32[]{:S(2)}, u32[]{:S(2)}) %all-to-all-start.1) | async-done | bytes 2097184 | tf_op jit(solution)/shard_map/all_to_all | solution.py:125
  54.5 6.3 %fusion.1 = bf16[32,2,128,128]{3,2,1,0:T(8,128)(2,1)} fusion(bf16[1,32,2,128,128]{4,3,2,1,0:T(8,128)(2,1)} %param.8, f32[32,2]{1,0:T(8,128)S(1)} %copy.43, bf16[32,2,2,128,128]{4,3,2,1,0:T(8,128)(2,1)} %bitcast.93, bf16[32,128,128]{2,1,0:T(8,128)(2,1)S(1)} %gather_fusion.1), kind=kOutput, calls=%fused_computation.12 | convolution fusion | flops 542113792 | bytes 9437440 | tf_op jit(solution)/shard_map/fetv,fewv->fetw/dot_general | solution.py:43
  60.8 4.3 %bitcast_convert_fusion.1 = bf16[32,128,128]{2,1,0:T(8,128)(2,1)S(1)} fusion(bf16[32,2,128,128]{3,2,1,0:T(8,128)(2,1)} %fusion.1, bf16[32,2,2,128,128]{4,3,2,1,0:T(8,128)(2,1)} %bitcast.94), kind=kOutput, calls=%fused_computation.21 | convolution fusion | flops 538443776 | bytes 7340032 | tf_op jit(solution)/shard_map/fetw,fewv->fetv/dot_general | solution.py:54
  67.7 8.3 %all-to-all-start.2 = ((bf16[64,64,128]{2,1,0:T(8,128)(2,1)}), bf16[64,64,128]{2,1,0:T(8,128)(2,1)S(1)}, u32[]{:S(2)}, u32[]{:S(2)}) async-start(bf16[64,64,128]{2,1,0:T(8,128)(2,1)} %get-tuple-element.30), calls=%async_computation.2 | async-start | bytes 2097152 | tf_op jit(solution)/shard_map/all_to_all | solution.py:112
  76.3 14.4 %all-to-all-done.2 = bf16[64,64,128]{2,1,0:T(8,128)(2,1)S(1)} async-done(((bf16[64,64,128]{2,1,0:T(8,128)(2,1)}), bf16[64,64,128]{2,1,0:T(8,128)(2,1)S(1)}, u32[]{:S(2)}, u32[]{:S(2)}) %all-to-all-start.2) | async-done | bytes 1048608 | tf_op jit(solution)/shard_map/all_to_all | solution.py:112
  92.3 13.3 %all-to-all-start.3 = ((bf16[16,80,128]{2,1,0:T(8,128)(2,1)}), bf16[16,80,128]{2,1,0:T(8,128)(2,1)S(1)}, u32[]{:S(2)}, u32[]{:S(2)}) async-start(bf16[16,80,128]{2,1,0:T(8,128)(2,1)} %copy.47), calls=%async_computation.3 | async-start | bytes 655360 | tf_op jit(solution)/shard_map/all_to_all | solution.py:121
  105.6 21.0 %all-to-all-done.3 = bf16[16,80,128]{2,1,0:T(8,128)(2,1)S(1)} async-done(((bf16[16,80,128]{2,1,0:T(8,128)(2,1)}), bf16[16,80,128]{2,1,0:T(8,128)(2,1)S(1)}, u32[]{:S(2)}, u32[]{:S(2)}) %all-to-all-start.3) | async-done | bytes 327712 | tf_op jit(solution)/shard_map/all_to_all | solution.py:121
  128.0 7.6 %all-to-all-start.4 = ((bf16[64,64,128]{2,1,0:T(8,128)(2,1)}), bf16[64,64,128]{2,1,0:T(8,128)(2,1)}, u32[]{:S(2)}, u32[]{:S(2)}) async-start(bf16[64,64,128]{2,1,0:T(8,128)(2,1)} %get-tuple-element.14), calls=%async_computation.4 | async-start | bytes 2097152 | tf_op jit(solution)/shard_map/all_to_all | solution.py:167
  136.2 2.5 collective-permute-start.1
  141.2 6.3 %collective-permute-done.1 = f32[16,128,1]{1,0,2:T(8,128)S(1)} collective-permute-done((f32[16,128,1]{1,0,2:T(8,128)S(1)}, f32[16,128,1]{1,0,2:T(8,128)S(1)}, u32[]{:S(2)}, u32[]{:S(2)}) %collective-permute-start.1) | collective-permute-done | bytes 8224 | tf_op jit(solution)/shard_map/ppermute | solution.py:22
  150.2 2.4 pad_maximum_fusion
  153.9 33.8 %all_gather.9 = bf16[16,64,128]{2,1,0:T(8,128)(2,1)} all-gather(bf16[1,64,128]{2,1,0:T(8,128)(2,1)S(1)} %fusion.53), channel_id=1, replica_groups=mesh['exp'=16,'sky'=32] {'exp'}, dimensions={0}, use_global_device_ids=true | all-gather | bytes 278528 | tf_op jit(solution)/shard_map/all_gather | solution.py:166
  190.3 4.5 %all-to-all-start.5 = ((bf16[16,64,128]{2,1,0:T(8,128)(2,1)}), bf16[16,64,128]{2,1,0:T(8,128)(2,1)S(1)}, u32[]{:S(2)}, u32[]{:S(2)}) async-start(bf16[16,64,128]{2,1,0:T(8,128)(2,1)} %copy.53), calls=%async_computation.5 | async-start | bytes 524288 | tf_op jit(solution)/shard_map/all_to_all | solution.py:121
  194.8 2.5 fusion.36
  200.9 8.2 %all-to-all-done.5 = bf16[16,64,128]{2,1,0:T(8,128)(2,1)S(1)} async-done(((bf16[16,64,128]{2,1,0:T(8,128)(2,1)}), bf16[16,64,128]{2,1,0:T(8,128)(2,1)S(1)}, u32[]{:S(2)}, u32[]{:S(2)}) %all-to-all-start.5) | async-done | bytes 262176 | tf_op jit(solution)/shard_map/all_to_all | solution.py:121
  209.7 8.0 %all-to-all-start.6 = ((bf16[64,64,128]{2,1,0:T(8,128)(2,1)}), bf16[64,64,128]{2,1,0:T(8,128)(2,1)S(1)}, u32[]{:S(2)}, u32[]{:S(2)}) async-start(bf16[64,64,128]{2,1,0:T(8,128)(2,1)} %gather_fusion.3), calls=%async_computation.6 | async-start | bytes 2097152 | tf_op jit(solution)/shard_map/all_to_all | solution.py:183
  217.7 31.1 %all_gather.10 = bf16[16,64,128]{2,1,0:T(8,128)(2,1)S(1)} all-gather(bf16[1,64,128]{2,1,0:T(8,128)(2,1)S(1)} %fusion.52), channel_id=1, replica_groups=mesh['exp'=16,'sky'=32] {'exp'}, dimensions={0}, use_global_device_ids=true | all-gather | bytes 278528 | tf_op jit(solution)/shard_map/all_gather | solution.py:182
  251.8 21.9 %all_to_all.51 = bf16[64,64,128]{2,1,0:T(8,128)(2,1)S(1)} all-to-all(bf16[64,64,128]{2,1,0:T(8,128)(2,1)S(1)} %gather_fusion.5), channel_id=1, replica_groups=mesh['exp'=16,'sky'=32] {'sky'}, dimensions={0} | all-to-all | bytes 2097152 | tf_op jit(solution)/shard_map/all_to_all | solution.py:125
  274.4 6.3 %fusion.3 = bf16[32,2,128,128]{3,2,1,0:T(8,128)(2,1)} fusion(bf16[1,32,2,128,128]{4,3,2,1,0:T(8,128)(2,1)} %param.8, f32[32,2]{1,0:T(8,128)S(1)} %copy.43, bf16[32,2,2,128,128]{4,3,2,1,0:T(8,128)(2,1)} %bitcast.95, bf16[32,64,128]{2,1,0:T(8,128)(2,1)S(1)} %gather_fusion.6, bf16[32,64,128]{2,1,0:T(8,128)(2,1)S(1)} %copy-done.4), kind=kOutput, calls=%fused_computation.14 | convolution fusion | flops 544210944 | bytes 9437440 | tf_op jit(solution)/shard_map/fetv,fewv->fetw/dot_general | solution.py:43
  280.7 4.3 %bitcast_convert_fusion = bf16[32,128,128]{2,1,0:T(8,128)(2,1)S(1)} fusion(bf16[32,2,128,128]{3,2,1,0:T(8,128)(2,1)} %fusion.3, bf16[32,2,2,128,128]{4,3,2,1,0:T(8,128)(2,1)} %bitcast.96), kind=kOutput, calls=%fused_computation.20 | convolution fusion | flops 538443776 | bytes 7340032 | tf_op jit(solution)/shard_map/fetw,fewv->fetv/dot_general | solution.py:54
  286.1 31.9 %all_to_all.52 = bf16[64,128,128]{2,1,0:T(8,128)(2,1)S(1)} all-to-all(bf16[64,128,128]{2,1,0:T(8,128)(2,1)S(1)} %gather_fusion.7), channel_id=1, replica_groups=mesh['exp'=16,'sky'=32] {'sky'}, dimensions={0} | all-to-all | bytes 4194304 | tf_op jit(solution)/shard_map/all_to_all | solution.py:112
  320.2 4.3 %all-to-all-start.9 = ((bf16[16,128,128]{2,1,0:T(8,128)(2,1)}), bf16[16,128,128]{2,1,0:T(8,128)(2,1)}, u32[]{:S(2)}, u32[]{:S(2)}) async-start(bf16[16,128,128]{2,1,0:T(8,128)(2,1)} %copy.56), calls=%async_computation.9 | async-start | bytes 1048576 | tf_op jit(solution)/shard_map/all_to_all | solution.py:121
  325.2 3.1 collective-permute-start.3
  328.6 2.3 collective-permute-start.2
  331.4 2.2 collective-permute-done.2
  335.7 15.8 %all-to-all-done.9 = bf16[16,128,128]{2,1,0:T(8,128)(2,1)} async-done(((bf16[16,128,128]{2,1,0:T(8,128)(2,1)}), bf16[16,128,128]{2,1,0:T(8,128)(2,1)}, u32[]{:S(2)}, u32[]{:S(2)}) %all-to-all-start.9) | async-done | bytes 524320 | tf_op jit(solution)/shard_map/all_to_all | solution.py:121
  353.3 34.8 %all-gather = bf16[2048,128]{1,0:T(8,128)(2,1)S(1)} all-gather(bf16[128,128]{1,0:T(8,128)(2,1)S(1)} %divide_convert_fusion), channel_id=2, replica_groups=mesh['exp'=16,'sky'=32] {'exp'}, dimensions={0}, use_global_device_ids=true | all-gather | bytes 557056 | tf_op jit(solution)/shard_map/all_gather | solution.py:158
  (92 shorter events, 42.1 us)
Async XLA Ops:
  3.8 14.9 %all-to-all-start = ((s32[32,2,1]{1,2,0:T(1,128)}), s32[32,2,1]{1,2,0:T(1,128)S(1)}, u32[]{:S(2)}, u32[]{:S(2)}) async-start(s32[32,2,1]{1,2,0:T(1,128)} %bitcast.2), calls=%async_computation | async-start | bytes 32768 | tf_op jit(solution)/shard_map/all_to_all | solution.py:96
  22.2 5.9 %copy-start.8 = (bf16[1,32,2]{1,2,0:T(2,128)(2,1)S(1)}, bf16[1,32,2]{1,2,0:T(2,128)(2,1)}, u32[]{:S(2)}) copy-start(bf16[1,32,2]{1,2,0:T(2,128)(2,1)} %param.9) | copy-start | bytes 388
  22.2 6.0 %copy-start.7 = (s32[1,32,2,2]{1,3,2,0:T(2,128)S(1)}, s32[1,32,2,2]{1,3,2,0:T(2,128)}, u32[]{:S(2)}) copy-start(s32[1,32,2,2]{1,3,2,0:T(2,128)} %param.12) | copy-start | bytes 1540
  22.2 6.3 %copy-start.5 = (bf16[8,128,128]{2,1,0:T(8,128)(2,1)S(1)}, bf16[8,128,128]{2,1,0:T(8,128)(2,1)}, u32[]{:S(2)}) copy-start(bf16[8,128,128]{2,1,0:T(8,128)(2,1)} %param.13) | copy-start | bytes 786436
  22.2 31.5 %all-to-all-start.1 = ((bf16[64,128,128]{2,1,0:T(8,128)(2,1)}), bf16[64,128,128]{2,1,0:T(8,128)(2,1)S(1)}, u32[]{:S(2)}, u32[]{:S(2)}) async-start(bf16[64,128,128]{2,1,0:T(8,128)(2,1)} %gather_fusion), calls=%async_computation.1 | async-start | bytes 4194304 | tf_op jit(solution)/shard_map/all_to_all | solution.py:125
  29.7 3.2 copy-start.6
  67.7 23.0 %all-to-all-start.2 = ((bf16[64,64,128]{2,1,0:T(8,128)(2,1)}), bf16[64,64,128]{2,1,0:T(8,128)(2,1)S(1)}, u32[]{:S(2)}, u32[]{:S(2)}) async-start(bf16[64,64,128]{2,1,0:T(8,128)(2,1)} %get-tuple-element.30), calls=%async_computation.2 | async-start | bytes 2097152 | tf_op jit(solution)/shard_map/all_to_all | solution.py:112
  91.4 44.2 %copy-start = (f32[16,128,128]{2,1,0:T(8,128)S(1)}, f32[16,128,128]{2,1,0:T(8,128)}, u32[]{:S(2)}) copy-start(f32[16,128,128]{2,1,0:T(8,128)} %param.7) | copy-start | bytes 3145732
  92.3 34.3 %all-to-all-start.3 = ((bf16[16,80,128]{2,1,0:T(8,128)(2,1)}), bf16[16,80,128]{2,1,0:T(8,128)(2,1)S(1)}, u32[]{:S(2)}, u32[]{:S(2)}) async-start(bf16[16,80,128]{2,1,0:T(8,128)(2,1)} %copy.47), calls=%async_computation.3 | async-start | bytes 655360 | tf_op jit(solution)/shard_map/all_to_all | solution.py:121
  128.0 59.7 %all-to-all-start.4 = ((bf16[64,64,128]{2,1,0:T(8,128)(2,1)}), bf16[64,64,128]{2,1,0:T(8,128)(2,1)}, u32[]{:S(2)}, u32[]{:S(2)}) async-start(bf16[64,64,128]{2,1,0:T(8,128)(2,1)} %get-tuple-element.14), calls=%async_computation.4 | async-start | bytes 2097152 | tf_op jit(solution)/shard_map/all_to_all | solution.py:167
  136.2 11.2 %collective-permute-start.1 = (f32[16,128,1]{1,0,2:T(8,128)S(1)}, f32[16,128,1]{1,0,2:T(8,128)S(1)}, u32[]{:S(2)}, u32[]{:S(2)}) collective-permute-start(f32[16,128,1]{1,0,2:T(8,128)S(1)} %copy.70), channel_id=1, source_target_pairs={{1,0},{2,1},{3,2},{4,3},{5,4},{6,5},{7,6},{8,7},{9,8},{10,9},{11,1... | collective-permute-start | bytes 24584 | tf_op jit(solution)/shard_map/ppermute | solution.py:22
  139.1 9.7 %collective-permute-start = (f32[16,128,1]{1,0,2:T(8,128)S(1)}, f32[16,128,1]{1,0,2:T(8,128)S(1)}, u32[]{:S(2)}, u32[]{:S(2)}) collective-permute-start(f32[16,128,1]{1,0,2:T(8,128)S(1)} %copy.69), channel_id=1, source_target_pairs={{0,1},{1,2},{2,3},{3,4},{4,5},{5,6},{6,7},{7,8},{8,9},{9,10},{10,1... | collective-permute-start | bytes 24584 | tf_op jit(solution)/shard_map/ppermute | solution.py:20
  190.3 18.7 %all-to-all-start.5 = ((bf16[16,64,128]{2,1,0:T(8,128)(2,1)}), bf16[16,64,128]{2,1,0:T(8,128)(2,1)S(1)}, u32[]{:S(2)}, u32[]{:S(2)}) async-start(bf16[16,64,128]{2,1,0:T(8,128)(2,1)} %copy.53), calls=%async_computation.5 | async-start | bytes 524288 | tf_op jit(solution)/shard_map/all_to_all | solution.py:121
  197.3 1.0 copy-start.3
  209.7 39.0 %all-to-all-start.6 = ((bf16[64,64,128]{2,1,0:T(8,128)(2,1)}), bf16[64,64,128]{2,1,0:T(8,128)(2,1)S(1)}, u32[]{:S(2)}, u32[]{:S(2)}) async-start(bf16[64,64,128]{2,1,0:T(8,128)(2,1)} %gather_fusion.3), calls=%async_computation.6 | async-start | bytes 2097152 | tf_op jit(solution)/shard_map/all_to_all | solution.py:183
  251.8 22.6 %copy-start.4 = (bf16[32,64,128]{2,1,0:T(8,128)(2,1)S(1)}, bf16[32,64,128]{2,1,0:T(8,128)(2,1)}, u32[]{:S(2)}) copy-start(bf16[32,64,128]{2,1,0:T(8,128)(2,1)} %gather_fusion.4) | copy-start | bytes 1572868
  318.0 6.5 %copy-start.1 = (f32[16,64,128]{2,1,0:T(8,128)S(1)}, f32[16,64,128]{2,1,0:T(8,128)}, u32[]{:S(2)}) copy-start(f32[16,64,128]{2,1,0:T(8,128)} %get-tuple-element.28) | copy-start | bytes 1572868
  318.0 6.5 %copy-start.2 = (f32[16,64,128]{2,1,0:T(8,128)S(1)}, f32[16,64,128]{2,1,0:T(8,128)}, u32[]{:S(2)}) copy-start(f32[16,64,128]{2,1,0:T(8,128)} %get-tuple-element.26) | copy-start | bytes 1572868
  320.2 31.3 %all-to-all-start.9 = ((bf16[16,128,128]{2,1,0:T(8,128)(2,1)}), bf16[16,128,128]{2,1,0:T(8,128)(2,1)}, u32[]{:S(2)}, u32[]{:S(2)}) async-start(bf16[16,128,128]{2,1,0:T(8,128)(2,1)} %copy.56), calls=%async_computation.9 | async-start | bytes 1048576 | tf_op jit(solution)/shard_map/all_to_all | solution.py:121
  325.2 5.8 %collective-permute-start.3 = (f32[16,128,1]{1,0,2:T(8,128)S(1)}, f32[16,128,1]{1,0,2:T(8,128)S(1)}, u32[]{:S(2)}, u32[]{:S(2)}) collective-permute-start(f32[16,128,1]{1,0,2:T(8,128)S(1)} %copy.58), channel_id=1, source_target_pairs={{1,0},{2,1},{3,2},{4,3},{5,4},{6,5},{7,6},{8,7},{9,8},{10,9},{11,1... | collective-permute-start | bytes 24584 | tf_op jit(solution)/shard_map/ppermute | solution.py:22
  328.6 5.0 %collective-permute-start.2 = (f32[16,128,1]{1,0,2:T(8,128)S(1)}, f32[16,128,1]{1,0,2:T(8,128)S(1)}, u32[]{:S(2)}, u32[]{:S(2)}) collective-permute-start(f32[16,128,1]{1,0,2:T(8,128)S(1)} %copy.57), channel_id=1, source_target_pairs={{0,1},{1,2},{2,3},{3,4},{4,5},{5,6},{6,7},{7,8},{8,9},{9,10},{10,1... | collective-permute-start | bytes 24584 | tf_op jit(solution)/shard_map/ppermute | solution.py:20

commit v6 on v3

--- a/solution.py
+++ b/solution.py
@@ -2,6 +2,8 @@
 import jax.numpy as jnp
 from jax import lax
 from jax.sharding import PartitionSpec as P
+from jax.experimental import pallas as pl
+from jax.experimental.pallas import tpu as pltpu
 
 ITERS = 2
 
@@ -57,6 +59,67 @@
         axis=1,
     )
     return summed.astype(jnp.bfloat16)
+
+
+def chain_kernel(ids_ref, weight_ref, fetched_ref, observed_ref, table_ref, flipped_ref, out_ref):
+    block = fetched_ref.shape[0]
+    expo_count = observed_ref.shape[1]
+    base = pl.program_id(0) * block
+    for j in range(block):
+        sky_tile = fetched_ref[j]
+        total = None
+        for e in range(expo_count):
+            slot = (base + j) * expo_count + e
+            left_id = ids_ref[2 * slot]
+            right_id = ids_ref[2 * slot + 1]
+            left_product = jnp.dot(
+                table_ref[left_id], sky_tile, preferred_element_type=jnp.float32
+            ).astype(jnp.bfloat16)
+            predicted = jnp.dot(
+                left_product, flipped_ref[right_id], preferred_element_type=jnp.float32
+            )
+            residual = weight_ref[slot] * (predicted - observed_ref[j, e].astype(jnp.float32))
+            back_product = jnp.dot(
+                flipped_ref[left_id],
+                residual.astype(jnp.bfloat16),
+                preferred_element_type=jnp.float32,
+            ).astype(jnp.bfloat16)
+            term = jnp.dot(back_product, table_ref[right_id], preferred_element_type=jnp.float32)
+            total = term if total is None else total + term
+        out_ref[j] = total.astype(jnp.bfloat16)
+
+
+def adjoint_chain(fetched, kernel_ids, kernels, tile_weights, observed):
+    foot_tiles, tile_edge = fetched.shape[0], fetched.shape[1]
+    expo_count = observed.shape[1]
+    table_size = kernels.shape[0]
+    block = 8 if foot_tiles % 8 == 0 else 1
+    flipped = jnp.swapaxes(kernels, 1, 2)
+    return pl.pallas_call(
+        chain_kernel,
+        grid_spec=pltpu.PrefetchScalarGridSpec(
+            num_scalar_prefetch=1,
+            grid=(foot_tiles // block,),
+            in_specs=[
+                pl.BlockSpec(memory_space=pltpu.SMEM),
+                pl.BlockSpec((block, tile_edge, tile_edge), lambda i, ids: (i, 0, 0)),
+                pl.BlockSpec(
+                    (block, expo_count, tile_edge, tile_edge), lambda i, ids: (i, 0, 0, 0)
+                ),
+                pl.BlockSpec((table_size, tile_edge, tile_edge), lambda i, ids: (0, 0, 0)),
+                pl.BlockSpec((table_size, tile_edge, tile_edge), lambda i, ids: (0, 0, 0)),
+            ],
+            out_specs=pl.BlockSpec((block, tile_edge, tile_edge), lambda i, ids: (i, 0, 0)),
+        ),
+        out_shape=jax.ShapeDtypeStruct((foot_tiles, tile_edge, tile_edge), jnp.bfloat16),
+    )(
+        kernel_ids.reshape(-1),
+        tile_weights.astype(jnp.float32).reshape(-1),
+        fetched,
+        observed,
+        kernels,
+        flipped,
+    )
 
 
 def laplace_image(padded):
@@ -94,7 +157,6 @@
     tile_weights = weights[0]
     kernel_ids = kernel_index[0]
     incoming = lax.all_to_all(requested, "sky", split_axis=0, concat_axis=0, tiled=True)
-    left_kernels, right_kernels = pick_kernels(kernel_ids, kernels)
     receive_map = jnp.arange(sky_rows, dtype=jnp.int32)[:, None] == incoming[None, :]
     local_counts = float(expo_count) * jnp.sum(receive_map.astype(jnp.float32), axis=1)
     receive_half = receive_map.astype(jnp.bfloat16)
@@ -111,7 +173,7 @@
             sky_half[safe_rows], "sky", split_axis=0, concat_axis=0, tiled=True
         )
         fetched = replies[slot_of]
-        adjoint = adjoint_tiles(fetched, left_kernels, right_kernels, tile_weights, observed)
+        adjoint = adjoint_chain(fetched, kernel_ids, kernels, tile_weights, observed)
         padded_adjoint = jnp.concatenate(
             [adjoint, jnp.zeros((1, tile_edge, tile_edge), adjoint.dtype)], axis=0
         )

time: 346 us -> 364 us (1.052)
  Pallas kernels: 0 us -> 35.3 us
  matrix products: 25 us -> 2.51 us
    pallas_call x0 -> x2, Pallas kernels: none -> 35.3 us  [adjoint_chain(): pl.pallas_call(chain_kernel, grid_spec=pltpu.PrefetchScalarGridSpec(num_s...]
    dot_general x5 -> x0, matrix products: 22.5 us -> none  [the longest x2 12.7 us: adjoint_tiles(): jnp.einsum('fetv,fewv->fetw', left_product, right_kernels, preferred_elem...]
    ppermute x2, waiting for transfers between devices: 4.45 us -> 0.01 us  [padded_2(): lax.ppermute(tail, axis, [(i, (i + 1) % count) for i in range(ends)])]
  transfers between devices with their start and end apart: 9 -> 9, of which waited for: 7 -> 7; matrix products, arithmetic and copies ran while one was open for 4% -> 3% of each run, Pallas kernels for 0% -> 0%
where the time goes in v6:
time: 364 us; the launch traced here: 359 us
  blocking collectives  134 us (37%)
  waiting for transfers between devices  91.5 us (25%)
  starting transfers between devices  53.2 us (15%)
  Pallas kernels  35.3 us (10%)
  local copies, waits for them, and re-layouts  26.6 us (7%)
  other arithmetic  15.6 us (4%)
    all_gather x2, blocking collectives, per_device(): lax.all_gather(scaled.astype(jnp.bfloat16), 'exp', axis=0, tiled=True)  66.8 us
    all_to_all x2, waiting for transfers between devices, per_device(): lax.all_to_all(payload, 'exp', split_axis=0, concat_axis=0, tiled=True)  36.8 us
    pallas_call x2, Pallas kernels, adjoint_chain(): pl.pallas_call(chain_kernel, grid_spec=pltpu.PrefetchScalarGridSpec(num_s...  35.3 us
    all_to_all x1, blocking collectives, per_device(): lax.all_to_all(sky_half[safe_rows], 'sky', split_axis=0, concat_axis=0, t...  34.7 us
    all_to_all x1, blocking collectives, per_device(): lax.all_to_all(outgoing, 'sky', split_axis=0, concat_axis=0, tiled=True)  32.6 us
    all_to_all x1, waiting for transfers between devices, per_device(): lax.all_to_all(outgoing, 'sky', split_axis=0, concat_axis=0, tiled=True)  25.4 us
    all_to_all x1, waiting for transfers between devices, per_device(): lax.all_to_all(sky_half[safe_rows], 'sky', split_axis=0, concat_axis=0, t...  23.2 us
    all_to_all x2, starting transfers between devices, per_device(): lax.all_to_all(payload, 'exp', split_axis=0, concat_axis=0, tiled=True)  18.4 us
  transfers between devices with their start and end apart: 9, of which 7 were waited for; matrix products, arithmetic and copies ran while one was open for 3% of the time, Pallas kernels for 0%

profile of v6, /device:TPU:6, one launch (start us, length us, event | category | flops | bytes accessed | tf_op | source)
XLA Modules:
  0.0 359.0 jit_solution(16422523755861536406)
XLA Ops:
  3.8 9.4 %all-to-all-start = ((s32[32,2,1]{1,2,0:T(1,128)}), s32[32,2,1]{1,2,0:T(1,128)S(1)}, u32[]{:S(2)}, u32[]{:S(2)}) async-start(s32[32,2,1]{1,2,0:T(1,128)} %bitcast.2), calls=%async_computation | async-start | bytes 32768 | tf_op jit(solution)/shard_map/all_to_all | solution.py:159
  13.1 1.3 convert_element_type.72
  14.5 4.2 %all-to-all-done = s32[32,2,1]{1,2,0:T(1,128)S(1)} async-done(((s32[32,2,1]{1,2,0:T(1,128)}), s32[32,2,1]{1,2,0:T(1,128)S(1)}, u32[]{:S(2)}, u32[]{:S(2)}) %all-to-all-start) | async-done | bytes 288 | tf_op jit(solution)/shard_map/all_to_all | solution.py:159
  20.0 2.2 gather_fusion
  22.2 5.9 %all-to-all-start.1 = ((bf16[64,128,128]{2,1,0:T(8,128)(2,1)}), bf16[64,128,128]{2,1,0:T(8,128)(2,1)S(1)}, u32[]{:S(2)}, u32[]{:S(2)}) async-start(bf16[64,128,128]{2,1,0:T(8,128)(2,1)} %gather_fusion), calls=%async_computation.1 | async-start | bytes 4194304 | tf_op jit(solution)/shard_map/all_to_all | solution.py:172
  30.6 23.2 %all-to-all-done.1 = bf16[64,128,128]{2,1,0:T(8,128)(2,1)S(1)} async-done(((bf16[64,128,128]{2,1,0:T(8,128)(2,1)}), bf16[64,128,128]{2,1,0:T(8,128)(2,1)S(1)}, u32[]{:S(2)}, u32[]{:S(2)}) %all-to-all-start.1) | async-done | bytes 2097184 | tf_op jit(solution)/shard_map/all_to_all | solution.py:172
  53.8 1.6 gather_fusion.1
  55.4 17.7 %shard_map.73 = bf16[32,128,128]{2,1,0:T(8,128)(2,1)} custom-call(s32[128]{0:T(128)} %reshape_squeeze.4.ids_ref, f32[64]{0:T(128)} %reshape.151.weight_ref, bf16[32,128,128]{2,1,0:T(8,128)(2,1)} %gather_fusion.1, bf16[32,2,128,128]{3,2,1,0:T(8,128)(2,1)} %bitcast.37, bf16[8,128,128]{2,1,0:T(8,128)(2,1)} %table_ref.3, bf16[8,128,128]{2,1,0:T(8,128)(2,1)} %bitcast.41), custom_call_target="tpu_custom_call" | custom-call | tf_op jit(solution)/shard_map/pallas_call | solution.py:98
  73.1 1.3 concatenate.15
  74.4 2.2 gather_fusion.2
  76.5 8.4 %all-to-all-start.2 = ((bf16[64,128,128]{2,1,0:T(8,128)(2,1)}), bf16[64,128,128]{2,1,0:T(8,128)(2,1)S(1)}, u32[]{:S(2)}, u32[]{:S(2)}) async-start(bf16[64,128,128]{2,1,0:T(8,128)(2,1)} %gather_fusion.2), calls=%async_computation.2 | async-start | bytes 4194304 | tf_op jit(solution)/shard_map/all_to_all | solution.py:181
  85.2 25.4 %all-to-all-done.2 = bf16[64,128,128]{2,1,0:T(8,128)(2,1)S(1)} async-done(((bf16[64,128,128]{2,1,0:T(8,128)(2,1)}), bf16[64,128,128]{2,1,0:T(8,128)(2,1)S(1)}, u32[]{:S(2)}, u32[]{:S(2)}) %all-to-all-start.2) | async-done | bytes 2097184 | tf_op jit(solution)/shard_map/all_to_all | solution.py:181
  110.5 1.3 fusion.4
  113.0 13.4 %all-to-all-start.3 = ((bf16[16,144,128]{2,1,0:T(8,128)(2,1)}), bf16[16,144,128]{2,1,0:T(8,128)(2,1)}, u32[]{:S(2)}, u32[]{:S(2)}) async-start(bf16[16,144,128]{2,1,0:T(8,128)(2,1)} %copy.66), calls=%async_computation.3 | async-start | bytes 1179648 | tf_op jit(solution)/shard_map/all_to_all | solution.py:188
  127.1 3.6 %collective-permute-start = (f32[16,128,1]{1,0,2:T(8,128)S(1)}, f32[16,128,1]{1,0,2:T(8,128)S(1)}, u32[]{:S(2)}, u32[]{:S(2)}) collective-permute-start(f32[16,128,1]{1,0,2:T(8,128)S(1)} %copy.83), channel_id=1, source_target_pairs={{0,1},{1,2},{2,3},{3,4},{4,5},{5,6},{6,7},{7,8},{8,9},{9,10},{10,1... | collective-permute-start | bytes 24584 | tf_op jit(solution)/shard_map/ppermute | solution.py:22
  131.0 2.0 collective-permute-start.1
  135.9 1.5 fusion.15
  137.4 18.6 %all-to-all-done.3 = bf16[16,144,128]{2,1,0:T(8,128)(2,1)} async-done(((bf16[16,144,128]{2,1,0:T(8,128)(2,1)}), bf16[16,144,128]{2,1,0:T(8,128)(2,1)}, u32[]{:S(2)}, u32[]{:S(2)}) %all-to-all-start.3) | async-done | bytes 589856 | tf_op jit(solution)/shard_map/all_to_all | solution.py:188
  158.5 34.5 %all-gather = bf16[2048,128]{1,0:T(8,128)(2,1)S(1)} all-gather(bf16[128,128]{1,0:T(8,128)(2,1)S(1)} %fusion.18), channel_id=2, replica_groups=mesh['exp'=16,'sky'=32] {'exp'}, dimensions={0}, use_global_device_ids=true | all-gather | bytes 557056 | tf_op jit(solution)/shard_map/all_gather | solution.py:196
  193.0 1.5 fusion.30
  194.5 2.2 gather_fusion.3
  196.7 34.7 %all_to_all.36 = bf16[64,128,128]{2,1,0:T(8,128)(2,1)} all-to-all(bf16[64,128,128]{2,1,0:T(8,128)(2,1)} %gather_fusion.3), channel_id=1, replica_groups=mesh['exp'=16,'sky'=32] {'sky'}, dimensions={0} | all-to-all | bytes 4194304 | tf_op jit(solution)/shard_map/all_to_all | solution.py:172
  231.3 3.2 gather_fusion.4
  234.6 17.7 %shard_map.74 = bf16[32,128,128]{2,1,0:T(8,128)(2,1)} custom-call(s32[128]{0:T(128)} %reshape_squeeze.4.ids_ref, f32[64]{0:T(128)} %reshape.151.weight_ref, bf16[32,128,128]{2,1,0:T(8,128)(2,1)} %gather_fusion.4, bf16[32,2,128,128]{3,2,1,0:T(8,128)(2,1)} %bitcast.38, bf16[8,128,128]{2,1,0:T(8,128)(2,1)} %table_ref.3, bf16[8,128,128]{2,1,0:T(8,128)(2,1)} %bitcast.42), custom_call_target="tpu_custom_call" | custom-call | tf_op jit(solution)/shard_map/pallas_call | solution.py:98
  252.2 1.3 concatenate.18
  253.6 2.2 gather_fusion.5
  255.7 32.6 %all_to_all.37 = bf16[64,128,128]{2,1,0:T(8,128)(2,1)S(1)} all-to-all(bf16[64,128,128]{2,1,0:T(8,128)(2,1)} %gather_fusion.5), channel_id=1, replica_groups=mesh['exp'=16,'sky'=32] {'sky'}, dimensions={0} | all-to-all | bytes 4194304 | tf_op jit(solution)/shard_map/all_to_all | solution.py:181
  290.5 5.1 %all-to-all-start.6 = ((bf16[16,128,128]{2,1,0:T(8,128)(2,1)}), bf16[16,128,128]{2,1,0:T(8,128)(2,1)}, u32[]{:S(2)}, u32[]{:S(2)}) async-start(bf16[16,128,128]{2,1,0:T(8,128)(2,1)} %copy.73), calls=%async_computation.6 | async-start | bytes 1048576 | tf_op jit(solution)/shard_map/all_to_all | solution.py:188
  296.2 3.0 collective-permute-start.2
  299.6 2.5 collective-permute-start.3
  305.6 18.1 %all-to-all-done.6 = bf16[16,128,128]{2,1,0:T(8,128)(2,1)} async-done(((bf16[16,128,128]{2,1,0:T(8,128)(2,1)}), bf16[16,128,128]{2,1,0:T(8,128)(2,1)}, u32[]{:S(2)}, u32[]{:S(2)}) %all-to-all-start.6) | async-done | bytes 524320 | tf_op jit(solution)/shard_map/all_to_all | solution.py:188
  325.5 32.3 %all-gather.1 = bf16[2048,128]{1,0:T(8,128)(2,1)S(1)} all-gather(bf16[128,128]{1,0:T(8,128)(2,1)S(1)} %divide_convert_fusion), channel_id=3, replica_groups=mesh['exp'=16,'sky'=32] {'exp'}, dimensions={0}, use_global_device_ids=true | all-gather | bytes 557056 | tf_op jit(solution)/shard_map/all_gather | solution.py:196
  (65 shorter events, 24.9 us)
Async XLA Ops:
  3.8 14.9 %all-to-all-start = ((s32[32,2,1]{1,2,0:T(1,128)}), s32[32,2,1]{1,2,0:T(1,128)S(1)}, u32[]{:S(2)}, u32[]{:S(2)}) async-start(s32[32,2,1]{1,2,0:T(1,128)} %bitcast.2), calls=%async_computation | async-start | bytes 32768 | tf_op jit(solution)/shard_map/all_to_all | solution.py:159
  22.2 5.9 %copy-start.4 = (bf16[1,32,2]{1,2,0:T(2,128)(2,1)S(1)}, bf16[1,32,2]{1,2,0:T(2,128)(2,1)}, u32[]{:S(2)}) copy-start(bf16[1,32,2]{1,2,0:T(2,128)(2,1)} %param.9) | copy-start | bytes 388
  22.2 6.7 %copy-start.3 = (s32[1,32,2,2]{1,3,2,0:T(2,128)S(1)}, s32[1,32,2,2]{1,3,2,0:T(2,128)}, u32[]{:S(2)}) copy-start(s32[1,32,2,2]{1,3,2,0:T(2,128)} %param.12) | copy-start | bytes 1540
  22.2 7.5 %copy-start.1 = (bf16[8,128,128]{2,1,0:T(8,128)(2,1)S(1)}, bf16[8,128,128]{2,1,0:T(8,128)(2,1)}, u32[]{:S(2)}) copy-start(bf16[8,128,128]{2,1,0:T(8,128)(2,1)} %table_ref.3) | copy-start | bytes 786436
  22.2 8.3 %copy-start.2 = (s32[1,32,1]{1,2,0:T(1,128)S(1)}, s32[1,32,1]{1,2,0:T(1,128)}, u32[]{:S(2)}) copy-start(s32[1,32,1]{1,2,0:T(1,128)} %param.10) | copy-start | bytes 388
  22.2 31.5 %all-to-all-start.1 = ((bf16[64,128,128]{2,1,0:T(8,128)(2,1)}), bf16[64,128,128]{2,1,0:T(8,128)(2,1)S(1)}, u32[]{:S(2)}, u32[]{:S(2)}) async-start(bf16[64,128,128]{2,1,0:T(8,128)(2,1)} %gather_fusion), calls=%async_computation.1 | async-start | bytes 4194304 | tf_op jit(solution)/shard_map/all_to_all | solution.py:172
  76.5 34.0 %all-to-all-start.2 = ((bf16[64,128,128]{2,1,0:T(8,128)(2,1)}), bf16[64,128,128]{2,1,0:T(8,128)(2,1)S(1)}, u32[]{:S(2)}, u32[]{:S(2)}) async-start(bf16[64,128,128]{2,1,0:T(8,128)(2,1)} %gather_fusion.2), calls=%async_computation.2 | async-start | bytes 4194304 | tf_op jit(solution)/shard_map/all_to_all | solution.py:181
  111.8 14.6 %copy-start = (f32[16,128,128]{2,1,0:T(8,128)S(1)}, f32[16,128,128]{2,1,0:T(8,128)}, u32[]{:S(2)}) copy-start(f32[16,128,128]{2,1,0:T(8,128)} %param.7) | copy-start | bytes 3145732
  113.0 43.1 %all-to-all-start.3 = ((bf16[16,144,128]{2,1,0:T(8,128)(2,1)}), bf16[16,144,128]{2,1,0:T(8,128)(2,1)}, u32[]{:S(2)}, u32[]{:S(2)}) async-start(bf16[16,144,128]{2,1,0:T(8,128)(2,1)} %copy.66), calls=%async_computation.3 | async-start | bytes 1179648 | tf_op jit(solution)/shard_map/all_to_all | solution.py:188
  127.1 5.9 %collective-permute-start = (f32[16,128,1]{1,0,2:T(8,128)S(1)}, f32[16,128,1]{1,0,2:T(8,128)S(1)}, u32[]{:S(2)}, u32[]{:S(2)}) collective-permute-start(f32[16,128,1]{1,0,2:T(8,128)S(1)} %copy.83), channel_id=1, source_target_pairs={{0,1},{1,2},{2,3},{3,4},{4,5},{5,6},{6,7},{7,8},{8,9},{9,10},{10,1... | collective-permute-start | bytes 24584 | tf_op jit(solution)/shard_map/ppermute | solution.py:22
  131.0 3.4 collective-permute-start.1
  290.5 33.2 %all-to-all-start.6 = ((bf16[16,128,128]{2,1,0:T(8,128)(2,1)}), bf16[16,128,128]{2,1,0:T(8,128)(2,1)}, u32[]{:S(2)}, u32[]{:S(2)}) async-start(bf16[16,128,128]{2,1,0:T(8,128)(2,1)} %copy.73), calls=%async_computation.6 | async-start | bytes 1048576 | tf_op jit(solution)/shard_map/all_to_all | solution.py:188
  296.2 5.9 %collective-permute-start.2 = (f32[16,128,1]{1,0,2:T(8,128)S(1)}, f32[16,128,1]{1,0,2:T(8,128)S(1)}, u32[]{:S(2)}, u32[]{:S(2)}) collective-permute-start(f32[16,128,1]{1,0,2:T(8,128)S(1)} %copy.75), channel_id=1, source_target_pairs={{0,1},{1,2},{2,3},{3,4},{4,5},{5,6},{6,7},{7,8},{8,9},{9,10},{10,1... | collective-permute-start | bytes 24584 | tf_op jit(solution)/shard_map/ppermute | solution.py:22
  299.6 3.9 %collective-permute-start.3 = (f32[16,128,1]{1,0,2:T(8,128)S(1)}, f32[16,128,1]{1,0,2:T(8,128)S(1)}, u32[]{:S(2)}, u32[]{:S(2)}) collective-permute-start(f32[16,128,1]{1,0,2:T(8,128)S(1)} %copy.76), channel_id=1, source_target_pairs={{1,0},{2,1},{3,2},{4,3},{5,4},{6,5},{7,6},{8,7},{9,8},{10,9},{11,1... | collective-permute-start | bytes 24584 | tf_op jit(solution)/shard_map/ppermute | solution.py:24

commit v7 on v3

--- a/solution.py
+++ b/solution.py
@@ -101,8 +101,8 @@
     safe_rows = jnp.maximum(incoming, 0)
     rows_per = sky_rows // n_exp
     own_rows = lax.axis_index("exp") * rows_per
-    count_block = jnp.broadcast_to(
-        local_counts.astype(jnp.bfloat16)[None, :, None], (n_exp, sky_rows, tile_edge)
+    count_tile = jnp.broadcast_to(
+        local_counts[:, None], (sky_rows, tile_edge)
     )
     sky_now = sky_start
     for iteration in range(ITERS):
@@ -110,6 +110,14 @@
         replies = lax.all_to_all(
             sky_half[safe_rows], "sky", split_axis=0, concat_axis=0, tiled=True
         )
+        if iteration == 0:
+            count_tiles = lax.all_gather(count_tile, "exp", axis=0, tiled=True)
+            count_tiles, replies = lax.optimization_barrier((count_tiles, replies))
+            counts = jnp.sum(
+                count_tiles.astype(jnp.float32).reshape(n_exp, sky_rows, tile_edge)[:, :, 0], axis=0
+            )
+            denominator = weight_ceiling * counts + 8.0 * prior_weight
+            own_denominator = lax.dynamic_slice_in_dim(denominator, own_rows, rows_per)
         fetched = replies[slot_of]
         adjoint = adjoint_tiles(fetched, left_kernels, right_kernels, tile_weights, observed)
         padded_adjoint = jnp.concatenate(
@@ -121,14 +129,8 @@
             "rj,juv->ruv", receive_half, arrived, preferred_element_type=jnp.float32
         )
         payload = partial_value.astype(jnp.bfloat16).reshape(n_exp, rows_per * tile_edge, tile_edge)
-        if iteration == 0:
-            payload = jnp.concatenate([payload, count_block], axis=1)
         row_parts = lax.all_to_all(payload, "exp", split_axis=0, concat_axis=0, tiled=True)
         summed = jnp.sum(row_parts.astype(jnp.float32).reshape((n_exp,) + payload.shape[1:]), axis=0)
-        if iteration == 0:
-            counts = summed[rows_per * tile_edge :, 0]
-            denominator = weight_ceiling * counts + 8.0 * prior_weight
-            own_denominator = lax.dynamic_slice_in_dim(denominator, own_rows, rows_per)
         own_total = summed[: rows_per * tile_edge].reshape(rows_per, tile_edge, tile_edge)
         scaled = own_total / own_denominator[:, None, None]
         gathered = lax.all_gather(scaled.astype(jnp.bfloat16), "exp", axis=0, tiled=True)

time: 346 us -> 349 us (level)
  blocking collectives: 134 us -> 201 us
  waiting for transfers between devices: 89.5 us -> 40.5 us
  starting transfers between devices: 52.7 us -> 38 us
    unnamed x0 -> x1, blocking collectives: none -> 34.6 us
    all_to_all x1 -> x2, blocking collectives: 32.6 us -> 65.7 us  [per_device(): lax.all_to_all(outgoing, 'sky', split_axis=0, concat_axis=0, tiled=True)]
    all_to_all x1 -> x0, waiting for transfers between devices: 25.4 us -> none  [per_device(): lax.all_to_all(outgoing, 'sky', split_axis=0, concat_axis=0, tiled=True)]
    all_to_all x1, waiting for transfers between devices: 20.7 us -> 0.01 us  [per_device(): lax.all_to_all(sky_half[safe_rows], 'sky', split_axis=0, concat_axis=0, t...]
    all_to_all x1 -> x0, starting transfers between devices: 8.35 us -> none  [per_device(): lax.all_to_all(outgoing, 'sky', split_axis=0, concat_axis=0, tiled=True)]
    all_to_all x2, starting transfers between devices: 18.4 us -> 11.4 us  [per_device(): lax.all_to_all(payload, 'exp', split_axis=0, concat_axis=0, tiled=True)]
    ppermute x2, waiting for transfers between devices: 4.45 us -> 0.01 us  [padded_2(): lax.ppermute(tail, axis, [(i, (i + 1) % count) for i in range(ends)])]
  transfers between devices with their start and end apart: 9 -> 8, of which waited for: 7 -> 5; matrix products, arithmetic and copies ran while one was open for 4% -> 5% of each run, Pallas kernels for 0% -> 0%
where the time goes in v7:
time: 349 us; the launch traced here: 344 us
  blocking collectives  201 us (58%)
  waiting for transfers between devices  40.5 us (12%)
  starting transfers between devices  38 us (11%)
  matrix products  25 us (7%)
  local copies, waits for them, and re-layouts  23.7 us (7%)
  other arithmetic  15.3 us (4%)
    all_to_all x2, blocking collectives, per_device(): lax.all_to_all(outgoing, 'sky', split_axis=0, concat_axis=0, tiled=True)  65.7 us
    all_gather x2, blocking collectives, per_device(): lax.all_gather(scaled.astype(jnp.bfloat16), 'exp', axis=0, tiled=True)  64.7 us
    all_to_all x1, blocking collectives, per_device(): lax.all_to_all(sky_half[safe_rows], 'sky', split_axis=0, concat_axis=0, t...  35.6 us
    unnamed x1, blocking collectives  34.6 us
    all_to_all x2, waiting for transfers between devices, per_device(): lax.all_to_all(payload, 'exp', split_axis=0, concat_axis=0, tiled=True)  34.5 us
    dot_general x2, matrix products, adjoint_tiles(): jnp.einsum('fetv,fewv->fetw', left_product, right_kernels, preferred_elem...  12.7 us
    all_to_all x2, starting transfers between devices, per_device(): lax.all_to_all(payload, 'exp', split_axis=0, concat_axis=0, tiled=True)  11.4 us
    all_to_all x1, starting transfers between devices, per_device(): lax.all_to_all(requested, 'sky', split_axis=0, concat_axis=0, tiled=True)  9.36 us
  transfers between devices with their start and end apart: 8, of which 5 were waited for; matrix products, arithmetic and copies ran while one was open for 5% of the time, Pallas kernels for 0%

profile of v7, /device:TPU:6, one launch (start us, length us, event | category | flops | bytes accessed | tf_op | source)
XLA Modules:
  0.0 344.2 jit_solution(7054661665493111888)
XLA Ops:
  3.8 9.4 %all-to-all-start = ((s32[32,2,1]{1,2,0:T(1,128)}), s32[32,2,1]{1,2,0:T(1,128)S(1)}, u32[]{:S(2)}, u32[]{:S(2)}) async-start(s32[32,2,1]{1,2,0:T(1,128)} %bitcast.2), calls=%async_computation | async-start | bytes 32768 | tf_op jit(solution)/shard_map/all_to_all | solution.py:96
  13.1 1.3 convert_element_type.113
  14.5 4.2 %all-to-all-done = s32[32,2,1]{1,2,0:T(1,128)S(1)} async-done(((s32[32,2,1]{1,2,0:T(1,128)}), s32[32,2,1]{1,2,0:T(1,128)S(1)}, u32[]{:S(2)}, u32[]{:S(2)}) %all-to-all-start) | async-done | bytes 288 | tf_op jit(solution)/shard_map/all_to_all | solution.py:96
  20.0 2.1 gather_fusion
  22.2 5.9 %all-to-all-start.1 = ((bf16[64,128,128]{2,1,0:T(8,128)(2,1)}), bf16[64,128,128]{2,1,0:T(8,128)(2,1)S(1)}, u32[]{:S(2)}, u32[]{:S(2)}) async-start(bf16[64,128,128]{2,1,0:T(8,128)(2,1)} %gather_fusion), calls=%async_computation.1 | async-start | bytes 4194304 | tf_op jit(solution)/shard_map/all_to_all | solution.py:110
  28.5 1.3 fusion.4
  29.8 3.2 copy.105
  32.9 1.3 dynamic-slice
  35.3 34.6 %all-reduce.4 = f32[256]{0:T(256)S(1)} all-reduce(f32[256]{0:T(256)S(1)} %multiply_dynamic-update-slice_fusion), channel_id=2, replica_groups=mesh['exp'=16,'sky'=32] {'exp'}, use_global_device_ids=true, to_apply=%add.4 | all-reduce | flops 256 | bytes 2048
  70.7 6.3 %fusion.1 = bf16[32,2,128,128]{3,2,1,0:T(8,128)(2,1)} fusion(bf16[1,32,2,128,128]{4,3,2,1,0:T(8,128)(2,1)} %param.8, f32[32,2]{1,0:T(8,128)S(1)} %copy.76, bf16[32,2,2,128,128]{4,3,2,1,0:T(8,128)(2,1)} %bitcast.92, bf16[32,128,128]{2,1,0:T(8,128)(2,1)S(1)} %gather_fusion.1), kind=kOutput, calls=%fused_computation.10 | convolution fusion | flops 542113792 | bytes 9437440 | tf_op jit(solution)/shard_map/fetv,fewv->fetw/dot_general | solution.py:43
  77.1 4.3 %bitcast_convert_fusion.1 = bf16[32,128,128]{2,1,0:T(8,128)(2,1)S(1)} fusion(bf16[32,2,128,128]{3,2,1,0:T(8,128)(2,1)} %fusion.1, bf16[32,2,2,128,128]{4,3,2,1,0:T(8,128)(2,1)} %bitcast.93), kind=kOutput, calls=%fused_computation.19 | convolution fusion | flops 538443776 | bytes 7340032 | tf_op jit(solution)/shard_map/fetw,fewv->fetv/dot_general | solution.py:54
  82.4 33.1 %all_to_all.36 = bf16[64,128,128]{2,1,0:T(8,128)(2,1)S(1)} all-to-all(bf16[64,128,128]{2,1,0:T(8,128)(2,1)S(1)} %gather_fusion.2), channel_id=1, replica_groups=mesh['exp'=16,'sky'=32] {'sky'}, dimensions={0} | all-to-all | bytes 4194304 | tf_op jit(solution)/shard_map/all_to_all | solution.py:127
  115.6 1.3 fusion.27
  117.8 6.8 %all-to-all-start.3 = ((bf16[16,128,128]{2,1,0:T(8,128)(2,1)}), bf16[16,128,128]{2,1,0:T(8,128)(2,1)}, u32[]{:S(2)}, u32[]{:S(2)}) async-start(bf16[16,128,128]{2,1,0:T(8,128)(2,1)} %copy.80), calls=%async_computation.3 | async-start | bytes 1048576 | tf_op jit(solution)/shard_map/all_to_all | solution.py:132
  125.3 3.0 collective-permute-start
  128.6 2.7 collective-permute-start.1
  134.1 1.5 fusion.38
  136.3 16.4 %all-to-all-done.3 = bf16[16,128,128]{2,1,0:T(8,128)(2,1)} async-done(((bf16[16,128,128]{2,1,0:T(8,128)(2,1)}), bf16[16,128,128]{2,1,0:T(8,128)(2,1)}, u32[]{:S(2)}, u32[]{:S(2)}) %all-to-all-start.3) | async-done | bytes 524320 | tf_op jit(solution)/shard_map/all_to_all | solution.py:132
  154.4 32.4 %all-gather = bf16[2048,128]{1,0:T(8,128)(2,1)S(1)} all-gather(bf16[128,128]{1,0:T(8,128)(2,1)S(1)} %divide_convert_fusion.1), channel_id=3, replica_groups=mesh['exp'=16,'sky'=32] {'exp'}, dimensions={0}, use_global_device_ids=true | all-gather | bytes 557056 | tf_op jit(solution)/shard_map/all_gather | solution.py:136
  186.8 1.5 fusion.56
  188.3 2.1 gather_fusion.3
  190.4 35.6 %all_to_all.37 = bf16[64,128,128]{2,1,0:T(8,128)(2,1)} all-to-all(bf16[64,128,128]{2,1,0:T(8,128)(2,1)} %gather_fusion.3), channel_id=1, replica_groups=mesh['exp'=16,'sky'=32] {'sky'}, dimensions={0} | all-to-all | bytes 4194304 | tf_op jit(solution)/shard_map/all_to_all | solution.py:110
  226.1 2.3 gather_fusion.4
  228.4 6.3 %fusion.3 = bf16[32,2,128,128]{3,2,1,0:T(8,128)(2,1)} fusion(bf16[1,32,2,128,128]{4,3,2,1,0:T(8,128)(2,1)} %param.8, f32[32,2]{1,0:T(8,128)S(1)} %copy.76, bf16[32,2,2,128,128]{4,3,2,1,0:T(8,128)(2,1)} %bitcast.94, bf16[32,128,128]{2,1,0:T(8,128)(2,1)S(1)} %gather_fusion.4), kind=kOutput, calls=%fused_computation.12 | convolution fusion | flops 542113792 | bytes 9437440 | tf_op jit(solution)/shard_map/fetv,fewv->fetw/dot_general | solution.py:43
  234.7 4.3 %bitcast_convert_fusion = bf16[32,128,128]{2,1,0:T(8,128)(2,1)S(1)} fusion(bf16[32,2,128,128]{3,2,1,0:T(8,128)(2,1)} %fusion.3, bf16[32,2,2,128,128]{4,3,2,1,0:T(8,128)(2,1)} %bitcast.95), kind=kOutput, calls=%fused_computation.18 | convolution fusion | flops 538443776 | bytes 7340032 | tf_op jit(solution)/shard_map/fetw,fewv->fetv/dot_general | solution.py:54
  239.2 2.2 gather_fusion.5
  241.3 32.6 %all_to_all.38 = bf16[64,128,128]{2,1,0:T(8,128)(2,1)S(1)} all-to-all(bf16[64,128,128]{2,1,0:T(8,128)(2,1)} %gather_fusion.5), channel_id=1, replica_groups=mesh['exp'=16,'sky'=32] {'sky'}, dimensions={0} | all-to-all | bytes 4194304 | tf_op jit(solution)/shard_map/all_to_all | solution.py:127
  276.1 4.6 %all-to-all-start.6 = ((bf16[16,128,128]{2,1,0:T(8,128)(2,1)}), bf16[16,128,128]{2,1,0:T(8,128)(2,1)}, u32[]{:S(2)}, u32[]{:S(2)}) async-start(bf16[16,128,128]{2,1,0:T(8,128)(2,1)} %copy.88), calls=%async_computation.6 | async-start | bytes 1048576 | tf_op jit(solution)/shard_map/all_to_all | solution.py:132
  281.4 3.0 collective-permute-start.2
  284.8 2.5 collective-permute-start.3
  290.8 18.1 %all-to-all-done.6 = bf16[16,128,128]{2,1,0:T(8,128)(2,1)} async-done(((bf16[16,128,128]{2,1,0:T(8,128)(2,1)}), bf16[16,128,128]{2,1,0:T(8,128)(2,1)}, u32[]{:S(2)}, u32[]{:S(2)}) %all-to-all-start.6) | async-done | bytes 524320 | tf_op jit(solution)/shard_map/all_to_all | solution.py:132
  310.6 32.3 %all-gather.1 = bf16[2048,128]{1,0:T(8,128)(2,1)S(1)} all-gather(bf16[128,128]{1,0:T(8,128)(2,1)S(1)} %divide_convert_fusion), channel_id=4, replica_groups=mesh['exp'=16,'sky'=32] {'exp'}, dimensions={0}, use_global_device_ids=true | all-gather | bytes 557056 | tf_op jit(solution)/shard_map/all_gather | solution.py:136
  (70 shorter events, 24.5 us)
Async XLA Ops:
  3.8 14.9 %all-to-all-start = ((s32[32,2,1]{1,2,0:T(1,128)}), s32[32,2,1]{1,2,0:T(1,128)S(1)}, u32[]{:S(2)}, u32[]{:S(2)}) async-start(s32[32,2,1]{1,2,0:T(1,128)} %bitcast.2), calls=%async_computation | async-start | bytes 32768 | tf_op jit(solution)/shard_map/all_to_all | solution.py:96
  22.2 5.9 %copy-start.4 = (bf16[1,32,2]{1,2,0:T(2,128)(2,1)S(1)}, bf16[1,32,2]{1,2,0:T(2,128)(2,1)}, u32[]{:S(2)}) copy-start(bf16[1,32,2]{1,2,0:T(2,128)(2,1)} %param.9) | copy-start | bytes 388
  22.2 6.0 %copy-start.3 = (s32[1,32,2,2]{1,3,2,0:T(2,128)S(1)}, s32[1,32,2,2]{1,3,2,0:T(2,128)}, u32[]{:S(2)}) copy-start(s32[1,32,2,2]{1,3,2,0:T(2,128)} %param.12) | copy-start | bytes 1540
  22.2 6.3 %copy-start.1 = (bf16[8,128,128]{2,1,0:T(8,128)(2,1)S(1)}, bf16[8,128,128]{2,1,0:T(8,128)(2,1)}, u32[]{:S(2)}) copy-start(bf16[8,128,128]{2,1,0:T(8,128)(2,1)} %param.13) | copy-start | bytes 786436
  22.2 47.7 %all-to-all-start.1 = ((bf16[64,128,128]{2,1,0:T(8,128)(2,1)}), bf16[64,128,128]{2,1,0:T(8,128)(2,1)S(1)}, u32[]{:S(2)}, u32[]{:S(2)}) async-start(bf16[64,128,128]{2,1,0:T(8,128)(2,1)} %gather_fusion), calls=%async_computation.1 | async-start | bytes 4194304 | tf_op jit(solution)/shard_map/all_to_all | solution.py:110
  29.8 5.1 %copy-start.2 = (s32[1,32,1]{1,2,0:T(1,128)S(1)}, s32[1,32,1]{1,2,0:T(1,128)}, u32[]{:S(2)}) copy-start(s32[1,32,1]{1,2,0:T(1,128)} %param.10) | copy-start | bytes 388
  115.6 9.0 %copy-start = (f32[16,128,128]{2,1,0:T(8,128)S(1)}, f32[16,128,128]{2,1,0:T(8,128)}, u32[]{:S(2)}) copy-start(f32[16,128,128]{2,1,0:T(8,128)} %param.7) | copy-start | bytes 3145732
  117.8 34.9 %all-to-all-start.3 = ((bf16[16,128,128]{2,1,0:T(8,128)(2,1)}), bf16[16,128,128]{2,1,0:T(8,128)(2,1)}, u32[]{:S(2)}, u32[]{:S(2)}) async-start(bf16[16,128,128]{2,1,0:T(8,128)(2,1)} %copy.80), calls=%async_computation.3 | async-start | bytes 1048576 | tf_op jit(solution)/shard_map/all_to_all | solution.py:132
  125.3 6.1 %collective-permute-start = (f32[16,128,1]{1,0,2:T(8,128)S(1)}, f32[16,128,1]{1,0,2:T(8,128)S(1)}, u32[]{:S(2)}, u32[]{:S(2)}) collective-permute-start(f32[16,128,1]{1,0,2:T(8,128)S(1)} %copy.102), channel_id=1, source_target_pairs={{0,1},{1,2},{2,3},{3,4},{4,5},{5,6},{6,7},{7,8},{8,9},{9,10},{10,1... | collective-permute-start | bytes 24584 | tf_op jit(solution)/shard_map/ppermute | solution.py:20
  128.6 3.9 %collective-permute-start.1 = (f32[16,128,1]{1,0,2:T(8,128)S(1)}, f32[16,128,1]{1,0,2:T(8,128)S(1)}, u32[]{:S(2)}, u32[]{:S(2)}) collective-permute-start(f32[16,128,1]{1,0,2:T(8,128)S(1)} %copy.103), channel_id=1, source_target_pairs={{1,0},{2,1},{3,2},{4,3},{5,4},{6,5},{7,6},{8,7},{9,8},{10,9},{11,1... | collective-permute-start | bytes 24584 | tf_op jit(solution)/shard_map/ppermute | solution.py:22
  276.1 32.8 %all-to-all-start.6 = ((bf16[16,128,128]{2,1,0:T(8,128)(2,1)}), bf16[16,128,128]{2,1,0:T(8,128)(2,1)}, u32[]{:S(2)}, u32[]{:S(2)}) async-start(bf16[16,128,128]{2,1,0:T(8,128)(2,1)} %copy.88), calls=%async_computation.6 | async-start | bytes 1048576 | tf_op jit(solution)/shard_map/all_to_all | solution.py:132
  281.4 5.9 %collective-permute-start.2 = (f32[16,128,1]{1,0,2:T(8,128)S(1)}, f32[16,128,1]{1,0,2:T(8,128)S(1)}, u32[]{:S(2)}, u32[]{:S(2)}) collective-permute-start(f32[16,128,1]{1,0,2:T(8,128)S(1)} %copy.89), channel_id=1, source_target_pairs={{0,1},{1,2},{2,3},{3,4},{4,5},{5,6},{6,7},{7,8},{8,9},{9,10},{10,1... | collective-permute-start | bytes 24584 | tf_op jit(solution)/shard_map/ppermute | solution.py:20
  284.8 3.9 %collective-permute-start.3 = (f32[16,128,1]{1,0,2:T(8,128)S(1)}, f32[16,128,1]{1,0,2:T(8,128)S(1)}, u32[]{:S(2)}, u32[]{:S(2)}) collective-permute-start(f32[16,128,1]{1,0,2:T(8,128)S(1)} %copy.90), channel_id=1, source_target_pairs={{1,0},{2,1},{3,2},{4,3},{5,4},{6,5},{7,6},{8,7},{9,8},{10,9},{11,1... | collective-permute-start | bytes 24584 | tf_op jit(solution)/shard_map/ppermute | solution.py:22

commit v8 on v7

--- a/solution.py
+++ b/solution.py
@@ -110,14 +110,6 @@
         replies = lax.all_to_all(
             sky_half[safe_rows], "sky", split_axis=0, concat_axis=0, tiled=True
         )
-        if iteration == 0:
-            count_tiles = lax.all_gather(count_tile, "exp", axis=0, tiled=True)
-            count_tiles, replies = lax.optimization_barrier((count_tiles, replies))
-            counts = jnp.sum(
-                count_tiles.astype(jnp.float32).reshape(n_exp, sky_rows, tile_edge)[:, :, 0], axis=0
-            )
-            denominator = weight_ceiling * counts + 8.0 * prior_weight
-            own_denominator = lax.dynamic_slice_in_dim(denominator, own_rows, rows_per)
         fetched = replies[slot_of]
         adjoint = adjoint_tiles(fetched, left_kernels, right_kernels, tile_weights, observed)
         padded_adjoint = jnp.concatenate(
@@ -125,6 +117,14 @@
         )
         outgoing = padded_adjoint[slot_source]
         arrived = lax.all_to_all(outgoing, "sky", split_axis=0, concat_axis=0, tiled=True)
+        if iteration == 0:
+            count_tiles = lax.all_gather(count_tile, "exp", axis=0, tiled=True)
+            count_tiles, arrived = lax.optimization_barrier((count_tiles, arrived))
+            counts = jnp.sum(
+                count_tiles.astype(jnp.float32).reshape(n_exp, sky_rows, tile_edge)[:, :, 0], axis=0
+            )
+            denominator = weight_ceiling * counts + 8.0 * prior_weight
+            own_denominator = lax.dynamic_slice_in_dim(denominator, own_rows, rows_per)
         partial_value = jnp.einsum(
             "rj,juv->ruv", receive_half, arrived, preferred_element_type=jnp.float32
         )

time: 349 us -> 342 us (0.980)
  blocking collectives: 201 us -> 163 us
  waiting for transfers between devices: 40.5 us -> 60.7 us
  starting transfers between devices: 38 us -> 46.5 us
    all_to_all x2 -> x1, blocking collectives: 65.7 us -> 32.6 us  [per_device(): lax.all_to_all(outgoing, 'sky', split_axis=0, concat_axis=0, tiled=True)]
    all_to_all x1, waiting for transfers between devices: 0.01 us -> 20.7 us  [per_device(): lax.all_to_all(sky_half[safe_rows], 'sky', split_axis=0, concat_axis=0, t...]
    all_to_all x0 -> x1, starting transfers between devices: none -> 8.35 us  [per_device(): lax.all_to_all(outgoing, 'sky', split_axis=0, concat_axis=0, tiled=True)]
    ppermute x2, waiting for transfers between devices: 0.01 us -> 4.44 us  [padded_2(): lax.ppermute(tail, axis, [(i, (i + 1) % count) for i in range(ends)])]
    all_to_all x1, blocking collectives: 35.6 us -> 31.7 us  [per_device(): lax.all_to_all(sky_half[safe_rows], 'sky', split_axis=0, concat_axis=0, t...]
  transfers between devices with their start and end apart: 8 -> 9, of which waited for: 5 -> 6; matrix products, arithmetic and copies ran while one was open for 5% -> 5% of each run, Pallas kernels for 0% -> 0%
where the time goes in v8:
time: 342 us; the launch traced here: 337 us
  blocking collectives  163 us (48%)
  waiting for transfers between devices  60.7 us (18%)
  starting transfers between devices  46.5 us (14%)
  matrix products  25 us (7%)
  local copies, waits for them, and re-layouts  24.9 us (7%)
  other arithmetic  15.3 us (4%)
    all_gather x2, blocking collectives, per_device(): lax.all_gather(scaled.astype(jnp.bfloat16), 'exp', axis=0, tiled=True)  64.4 us
    unnamed x1, blocking collectives  34.6 us
    all_to_all x1, blocking collectives, per_device(): lax.all_to_all(outgoing, 'sky', split_axis=0, concat_axis=0, tiled=True)  32.6 us
    all_to_all x1, blocking collectives, per_device(): lax.all_to_all(sky_half[safe_rows], 'sky', split_axis=0, concat_axis=0, t...  31.7 us
    all_to_all x2, waiting for transfers between devices, per_device(): lax.all_to_all(payload, 'exp', split_axis=0, concat_axis=0, tiled=True)  31.4 us
    all_to_all x1, waiting for transfers between devices, per_device(): lax.all_to_all(sky_half[safe_rows], 'sky', split_axis=0, concat_axis=0, t...  20.7 us
    all_to_all x2, starting transfers between devices, per_device(): lax.all_to_all(payload, 'exp', split_axis=0, concat_axis=0, tiled=True)  13.4 us
    dot_general x2, matrix products, adjoint_tiles(): jnp.einsum('fetv,fewv->fetw', left_product, right_kernels, preferred_elem...  12.7 us
  transfers between devices with their start and end apart: 9, of which 6 were waited for; matrix products, arithmetic and copies ran while one was open for 5% of the time, Pallas kernels for 0%

profile of v8, /device:TPU:6, one launch (start us, length us, event | category | flops | bytes accessed | tf_op | source)
XLA Modules:
  0.0 336.7 jit_solution(4286768661950795832)
XLA Ops:
  3.8 9.4 %all-to-all-start = ((s32[32,2,1]{1,2,0:T(1,128)}), s32[32,2,1]{1,2,0:T(1,128)S(1)}, u32[]{:S(2)}, u32[]{:S(2)}) async-start(s32[32,2,1]{1,2,0:T(1,128)} %bitcast.2), calls=%async_computation | async-start | bytes 32768 | tf_op jit(solution)/shard_map/all_to_all | solution.py:96
  14.5 4.2 %all-to-all-done = s32[32,2,1]{1,2,0:T(1,128)S(1)} async-done(((s32[32,2,1]{1,2,0:T(1,128)}), s32[32,2,1]{1,2,0:T(1,128)S(1)}, u32[]{:S(2)}, u32[]{:S(2)}) %all-to-all-start) | async-done | bytes 288 | tf_op jit(solution)/shard_map/all_to_all | solution.py:96
  20.0 2.1 gather_fusion
  22.2 5.9 %all-to-all-start.1 = ((bf16[64,128,128]{2,1,0:T(8,128)(2,1)}), bf16[64,128,128]{2,1,0:T(8,128)(2,1)S(1)}, u32[]{:S(2)}, u32[]{:S(2)}) async-start(bf16[64,128,128]{2,1,0:T(8,128)(2,1)} %gather_fusion), calls=%async_computation.1 | async-start | bytes 4194304 | tf_op jit(solution)/shard_map/all_to_all | solution.py:110
  29.8 3.2 copy.108
  33.0 20.7 %all-to-all-done.1 = bf16[64,128,128]{2,1,0:T(8,128)(2,1)S(1)} async-done(((bf16[64,128,128]{2,1,0:T(8,128)(2,1)}), bf16[64,128,128]{2,1,0:T(8,128)(2,1)S(1)}, u32[]{:S(2)}, u32[]{:S(2)}) %all-to-all-start.1) | async-done | bytes 2097184 | tf_op jit(solution)/shard_map/all_to_all | solution.py:110
  54.5 6.3 %fusion.1 = bf16[32,2,128,128]{3,2,1,0:T(8,128)(2,1)} fusion(bf16[1,32,2,128,128]{4,3,2,1,0:T(8,128)(2,1)} %param.8, f32[32,2]{1,0:T(8,128)S(1)} %copy.79, bf16[32,2,2,128,128]{4,3,2,1,0:T(8,128)(2,1)} %bitcast.92, bf16[32,128,128]{2,1,0:T(8,128)(2,1)S(1)} %gather_fusion.1), kind=kOutput, calls=%fused_computation.10 | convolution fusion | flops 542113792 | bytes 9437440 | tf_op jit(solution)/shard_map/fetv,fewv->fetw/dot_general | solution.py:43
  60.8 4.3 %bitcast_convert_fusion.1 = bf16[32,128,128]{2,1,0:T(8,128)(2,1)S(1)} fusion(bf16[32,2,128,128]{3,2,1,0:T(8,128)(2,1)} %fusion.1, bf16[32,2,2,128,128]{4,3,2,1,0:T(8,128)(2,1)} %bitcast.93), kind=kOutput, calls=%fused_computation.19 | convolution fusion | flops 538443776 | bytes 7340032 | tf_op jit(solution)/shard_map/fetw,fewv->fetv/dot_general | solution.py:54
  65.2 2.1 gather_fusion.2
  67.4 8.4 %all-to-all-start.2 = ((bf16[64,128,128]{2,1,0:T(8,128)(2,1)}), bf16[64,128,128]{2,1,0:T(8,128)(2,1)S(1)}, u32[]{:S(2)}, u32[]{:S(2)}) async-start(bf16[64,128,128]{2,1,0:T(8,128)(2,1)} %gather_fusion.2), calls=%async_computation.2 | async-start | bytes 4194304 | tf_op jit(solution)/shard_map/all_to_all | solution.py:119
  78.0 34.6 %all-reduce.4 = f32[256]{0:T(256)S(1)} all-reduce(f32[256]{0:T(256)S(1)} %multiply_dynamic-update-slice_fusion), channel_id=2, replica_groups=mesh['exp'=16,'sky'=32] {'exp'}, use_global_device_ids=true, to_apply=%add.4 | all-reduce | flops 256 | bytes 2048
  114.9 6.8 %all-to-all-start.3 = ((bf16[16,128,128]{2,1,0:T(8,128)(2,1)}), bf16[16,128,128]{2,1,0:T(8,128)(2,1)}, u32[]{:S(2)}, u32[]{:S(2)}) async-start(bf16[16,128,128]{2,1,0:T(8,128)(2,1)} %copy.83), calls=%async_computation.3 | async-start | bytes 1048576 | tf_op jit(solution)/shard_map/all_to_all | solution.py:132
  122.4 1.9 collective-permute-start.1
  124.7 2.6 collective-permute-start
  127.7 2.0 collective-permute-done
  131.2 1.5 fusion.38
  133.4 14.1 %all-to-all-done.3 = bf16[16,128,128]{2,1,0:T(8,128)(2,1)} async-done(((bf16[16,128,128]{2,1,0:T(8,128)(2,1)}), bf16[16,128,128]{2,1,0:T(8,128)(2,1)}, u32[]{:S(2)}, u32[]{:S(2)}) %all-to-all-start.3) | async-done | bytes 524320 | tf_op jit(solution)/shard_map/all_to_all | solution.py:132
  149.2 32.0 %all-gather = bf16[2048,128]{1,0:T(8,128)(2,1)S(1)} all-gather(bf16[128,128]{1,0:T(8,128)(2,1)S(1)} %divide_convert_fusion.1), channel_id=3, replica_groups=mesh['exp'=16,'sky'=32] {'exp'}, dimensions={0}, use_global_device_ids=true | all-gather | bytes 557056 | tf_op jit(solution)/shard_map/all_gather | solution.py:136
  181.3 1.5 fusion.56
  182.8 2.1 gather_fusion.3
  184.9 31.7 %all_to_all.36 = bf16[64,128,128]{2,1,0:T(8,128)(2,1)} all-to-all(bf16[64,128,128]{2,1,0:T(8,128)(2,1)} %gather_fusion.3), channel_id=1, replica_groups=mesh['exp'=16,'sky'=32] {'sky'}, dimensions={0} | all-to-all | bytes 4194304 | tf_op jit(solution)/shard_map/all_to_all | solution.py:110
  216.6 2.3 gather_fusion.4
  218.9 6.3 %fusion.3 = bf16[32,2,128,128]{3,2,1,0:T(8,128)(2,1)} fusion(bf16[1,32,2,128,128]{4,3,2,1,0:T(8,128)(2,1)} %param.8, f32[32,2]{1,0:T(8,128)S(1)} %copy.79, bf16[32,2,2,128,128]{4,3,2,1,0:T(8,128)(2,1)} %bitcast.94, bf16[32,128,128]{2,1,0:T(8,128)(2,1)S(1)} %gather_fusion.4), kind=kOutput, calls=%fused_computation.12 | convolution fusion | flops 542113792 | bytes 9437440 | tf_op jit(solution)/shard_map/fetv,fewv->fetw/dot_general | solution.py:43
  225.3 4.3 %bitcast_convert_fusion = bf16[32,128,128]{2,1,0:T(8,128)(2,1)S(1)} fusion(bf16[32,2,128,128]{3,2,1,0:T(8,128)(2,1)} %fusion.3, bf16[32,2,2,128,128]{4,3,2,1,0:T(8,128)(2,1)} %bitcast.95), kind=kOutput, calls=%fused_computation.18 | convolution fusion | flops 538443776 | bytes 7340032 | tf_op jit(solution)/shard_map/fetw,fewv->fetv/dot_general | solution.py:54
  229.7 2.2 gather_fusion.5
  231.9 32.6 %all_to_all.37 = bf16[64,128,128]{2,1,0:T(8,128)(2,1)S(1)} all-to-all(bf16[64,128,128]{2,1,0:T(8,128)(2,1)} %gather_fusion.5), channel_id=1, replica_groups=mesh['exp'=16,'sky'=32] {'sky'}, dimensions={0} | all-to-all | bytes 4194304 | tf_op jit(solution)/shard_map/all_to_all | solution.py:119
  266.6 6.7 %all-to-all-start.6 = ((bf16[16,128,128]{2,1,0:T(8,128)(2,1)}), bf16[16,128,128]{2,1,0:T(8,128)(2,1)}, u32[]{:S(2)}, u32[]{:S(2)}) async-start(bf16[16,128,128]{2,1,0:T(8,128)(2,1)} %copy.91), calls=%async_computation.6 | async-start | bytes 1048576 | tf_op jit(solution)/shard_map/all_to_all | solution.py:132
  274.0 2.8 collective-permute-start.3
  277.2 2.1 collective-permute-start.2
  279.7 2.5 collective-permute-done.2
  284.2 17.3 %all-to-all-done.6 = bf16[16,128,128]{2,1,0:T(8,128)(2,1)} async-done(((bf16[16,128,128]{2,1,0:T(8,128)(2,1)}), bf16[16,128,128]{2,1,0:T(8,128)(2,1)}, u32[]{:S(2)}, u32[]{:S(2)}) %all-to-all-start.6) | async-done | bytes 524320 | tf_op jit(solution)/shard_map/all_to_all | solution.py:132
  303.2 32.3 %all-gather.1 = bf16[2048,128]{1,0:T(8,128)(2,1)S(1)} all-gather(bf16[128,128]{1,0:T(8,128)(2,1)S(1)} %divide_convert_fusion), channel_id=4, replica_groups=mesh['exp'=16,'sky'=32] {'exp'}, dimensions={0}, use_global_device_ids=true | all-gather | bytes 557056 | tf_op jit(solution)/shard_map/all_gather | solution.py:136
  (71 shorter events, 26.9 us)
Async XLA Ops:
  3.8 14.9 %all-to-all-start = ((s32[32,2,1]{1,2,0:T(1,128)}), s32[32,2,1]{1,2,0:T(1,128)S(1)}, u32[]{:S(2)}, u32[]{:S(2)}) async-start(s32[32,2,1]{1,2,0:T(1,128)} %bitcast.2), calls=%async_computation | async-start | bytes 32768 | tf_op jit(solution)/shard_map/all_to_all | solution.py:96
  22.2 5.9 %copy-start.4 = (bf16[1,32,2]{1,2,0:T(2,128)(2,1)S(1)}, bf16[1,32,2]{1,2,0:T(2,128)(2,1)}, u32[]{:S(2)}) copy-start(bf16[1,32,2]{1,2,0:T(2,128)(2,1)} %param.9) | copy-start | bytes 388
  22.2 6.0 %copy-start.3 = (s32[1,32,2,2]{1,3,2,0:T(2,128)S(1)}, s32[1,32,2,2]{1,3,2,0:T(2,128)}, u32[]{:S(2)}) copy-start(s32[1,32,2,2]{1,3,2,0:T(2,128)} %param.12) | copy-start | bytes 1540
  22.2 6.3 %copy-start.1 = (bf16[8,128,128]{2,1,0:T(8,128)(2,1)S(1)}, bf16[8,128,128]{2,1,0:T(8,128)(2,1)}, u32[]{:S(2)}) copy-start(bf16[8,128,128]{2,1,0:T(8,128)(2,1)} %param.13) | copy-start | bytes 786436
  22.2 31.5 %all-to-all-start.1 = ((bf16[64,128,128]{2,1,0:T(8,128)(2,1)}), bf16[64,128,128]{2,1,0:T(8,128)(2,1)S(1)}, u32[]{:S(2)}, u32[]{:S(2)}) async-start(bf16[64,128,128]{2,1,0:T(8,128)(2,1)} %gather_fusion), calls=%async_computation.1 | async-start | bytes 4194304 | tf_op jit(solution)/shard_map/all_to_all | solution.py:110
  29.8 3.2 copy-start.2
  67.4 45.2 %all-to-all-start.2 = ((bf16[64,128,128]{2,1,0:T(8,128)(2,1)}), bf16[64,128,128]{2,1,0:T(8,128)(2,1)S(1)}, u32[]{:S(2)}, u32[]{:S(2)}) async-start(bf16[64,128,128]{2,1,0:T(8,128)(2,1)} %gather_fusion.2), calls=%async_computation.2 | async-start | bytes 4194304 | tf_op jit(solution)/shard_map/all_to_all | solution.py:119
  112.7 9.0 %copy-start = (f32[16,128,128]{2,1,0:T(8,128)S(1)}, f32[16,128,128]{2,1,0:T(8,128)}, u32[]{:S(2)}) copy-start(f32[16,128,128]{2,1,0:T(8,128)} %param.7) | copy-start | bytes 3145732
  114.9 32.6 %all-to-all-start.3 = ((bf16[16,128,128]{2,1,0:T(8,128)(2,1)}), bf16[16,128,128]{2,1,0:T(8,128)(2,1)}, u32[]{:S(2)}, u32[]{:S(2)}) async-start(bf16[16,128,128]{2,1,0:T(8,128)(2,1)} %copy.83), calls=%async_computation.3 | async-start | bytes 1048576 | tf_op jit(solution)/shard_map/all_to_all | solution.py:132
  122.4 4.9 %collective-permute-start.1 = (f32[16,128,1]{1,0,2:T(8,128)S(1)}, f32[16,128,1]{1,0,2:T(8,128)S(1)}, u32[]{:S(2)}, u32[]{:S(2)}) collective-permute-start(f32[16,128,1]{1,0,2:T(8,128)S(1)} %copy.106), channel_id=1, source_target_pairs={{1,0},{2,1},{3,2},{4,3},{5,4},{6,5},{7,6},{8,7},{9,8},{10,9},{11,1... | collective-permute-start | bytes 24584 | tf_op jit(solution)/shard_map/ppermute | solution.py:22
  124.7 5.0 %collective-permute-start = (f32[16,128,1]{1,0,2:T(8,128)S(1)}, f32[16,128,1]{1,0,2:T(8,128)S(1)}, u32[]{:S(2)}, u32[]{:S(2)}) collective-permute-start(f32[16,128,1]{1,0,2:T(8,128)S(1)} %copy.105), channel_id=1, source_target_pairs={{0,1},{1,2},{2,3},{3,4},{4,5},{5,6},{6,7},{7,8},{8,9},{9,10},{10,1... | collective-permute-start | bytes 24584 | tf_op jit(solution)/shard_map/ppermute | solution.py:20
  266.6 34.8 %all-to-all-start.6 = ((bf16[16,128,128]{2,1,0:T(8,128)(2,1)}), bf16[16,128,128]{2,1,0:T(8,128)(2,1)}, u32[]{:S(2)}, u32[]{:S(2)}) async-start(bf16[16,128,128]{2,1,0:T(8,128)(2,1)} %copy.91), calls=%async_computation.6 | async-start | bytes 1048576 | tf_op jit(solution)/shard_map/all_to_all | solution.py:132
  274.0 5.3 %collective-permute-start.3 = (f32[16,128,1]{1,0,2:T(8,128)S(1)}, f32[16,128,1]{1,0,2:T(8,128)S(1)}, u32[]{:S(2)}, u32[]{:S(2)}) collective-permute-start(f32[16,128,1]{1,0,2:T(8,128)S(1)} %copy.93), channel_id=1, source_target_pairs={{1,0},{2,1},{3,2},{4,3},{5,4},{6,5},{7,6},{8,7},{9,8},{10,9},{11,1... | collective-permute-start | bytes 24584 | tf_op jit(solution)/shard_map/ppermute | solution.py:22
  277.2 5.0 %collective-permute-start.2 = (f32[16,128,1]{1,0,2:T(8,128)S(1)}, f32[16,128,1]{1,0,2:T(8,128)S(1)}, u32[]{:S(2)}, u32[]{:S(2)}) collective-permute-start(f32[16,128,1]{1,0,2:T(8,128)S(1)} %copy.92), channel_id=1, source_target_pairs={{0,1},{1,2},{2,3},{3,4},{4,5},{5,6},{6,7},{7,8},{8,9},{9,10},{10,1... | collective-permute-start | bytes 24584 | tf_op jit(solution)/shard_map/ppermute | solution.py:20

commit v9 on v8

--- a/solution.py
+++ b/solution.py
@@ -105,11 +105,9 @@
         local_counts[:, None], (sky_rows, tile_edge)
     )
     sky_now = sky_start
+    request = sky_now.astype(jnp.bfloat16)[safe_rows]
     for iteration in range(ITERS):
-        sky_half = sky_now.astype(jnp.bfloat16)
-        replies = lax.all_to_all(
-            sky_half[safe_rows], "sky", split_axis=0, concat_axis=0, tiled=True
-        )
+        replies = lax.all_to_all(request, "sky", split_axis=0, concat_axis=0, tiled=True)
         fetched = replies[slot_of]
         adjoint = adjoint_tiles(fetched, left_kernels, right_kernels, tile_weights, observed)
         padded_adjoint = jnp.concatenate(
@@ -136,6 +134,11 @@
         gathered = lax.all_gather(scaled.astype(jnp.bfloat16), "exp", axis=0, tiled=True)
         laplacian = laplace_image(padded_2(sky_now, (("sky", 2),), 1))
         smooth = prior_weight * laplacian / denominator[:, None, None]
+        if iteration + 1 < ITERS:
+            request = (
+                sky_now[safe_rows]
+                - (gathered[safe_rows].astype(jnp.float32) + smooth[safe_rows])
+            ).astype(jnp.bfloat16)
         sky_now = sky_now - (gathered.astype(jnp.float32) + smooth)
     return sky_now
 

time: 342 us -> 350 us (1.023)
  local copies, waits for them, and re-layouts: 24.9 us -> 30.6 us
  other arithmetic: 15.3 us -> 20.9 us
    gather x2 -> x4, local copies, waits for them, and re-layouts: 4.29 us -> 9.9 us  [the longest x1 2.79 us: per_device(): smooth[safe_rows]]
    convert_element_type x2, other arithmetic: 2.83 us -> 6.54 us  [the longest x1 5.23 us: per_device(): request = (sky_now[safe_rows] - (gathered[safe_rows].astype(jnp.float32)...]
  transfers between devices with their start and end apart: 9 -> 9, of which waited for: 6 -> 5; matrix products, arithmetic and copies ran while one was open for 5% -> 6% of each run, Pallas kernels for 0% -> 0%
where the time goes in v9:
time: 350 us; the launch traced here: 345 us
  blocking collectives  163 us (47%)
  waiting for transfers between devices  57.6 us (16%)
  starting transfers between devices  46.7 us (13%)
  local copies, waits for them, and re-layouts  30.6 us (9%)
  matrix products  25 us (7%)
  other arithmetic  20.9 us (6%)
    all_gather x2, blocking collectives, per_device(): lax.all_gather(scaled.astype(jnp.bfloat16), 'exp', axis=0, tiled=True)  64.4 us
    unnamed x1, blocking collectives  34.6 us
    all_to_all x1, blocking collectives, per_device(): lax.all_to_all(outgoing, 'sky', split_axis=0, concat_axis=0, tiled=True)  32.6 us
    all_to_all x1, blocking collectives, per_device(): lax.all_to_all(request, 'sky', split_axis=0, concat_axis=0, tiled=True)  31.5 us
    all_to_all x2, waiting for transfers between devices, per_device(): lax.all_to_all(payload, 'exp', split_axis=0, concat_axis=0, tiled=True)  30.5 us
    all_to_all x1, waiting for transfers between devices, per_device(): lax.all_to_all(request, 'sky', split_axis=0, concat_axis=0, tiled=True)  20.7 us
    all_to_all x2, starting transfers between devices, per_device(): lax.all_to_all(payload, 'exp', split_axis=0, concat_axis=0, tiled=True)  13.4 us
    dot_general x2, matrix products, adjoint_tiles(): jnp.einsum('fetv,fewv->fetw', left_product, right_kernels, preferred_elem...  12.7 us
  transfers between devices with their start and end apart: 9, of which 5 were waited for; matrix products, arithmetic and copies ran while one was open for 6% of the time, Pallas kernels for 0%

profile of v9, /device:TPU:6, one launch (start us, length us, event | category | flops | bytes accessed | tf_op | source)
XLA Modules:
  0.0 345.0 jit_solution(14089129753878376498)
XLA Ops:
  3.8 9.4 %all-to-all-start = ((s32[32,2,1]{1,2,0:T(1,128)}), s32[32,2,1]{1,2,0:T(1,128)S(1)}, u32[]{:S(2)}, u32[]{:S(2)}) async-start(s32[32,2,1]{1,2,0:T(1,128)} %bitcast.2), calls=%async_computation | async-start | bytes 32768 | tf_op jit(solution)/shard_map/all_to_all | solution.py:96
  14.5 4.2 %all-to-all-done = s32[32,2,1]{1,2,0:T(1,128)S(1)} async-done(((s32[32,2,1]{1,2,0:T(1,128)}), s32[32,2,1]{1,2,0:T(1,128)S(1)}, u32[]{:S(2)}, u32[]{:S(2)}) %all-to-all-start) | async-done | bytes 288 | tf_op jit(solution)/shard_map/all_to_all | solution.py:96
  20.0 2.1 gather_fusion
  22.2 5.9 %all-to-all-start.1 = ((bf16[64,128,128]{2,1,0:T(8,128)(2,1)}), bf16[64,128,128]{2,1,0:T(8,128)(2,1)S(1)}, u32[]{:S(2)}, u32[]{:S(2)}) async-start(bf16[64,128,128]{2,1,0:T(8,128)(2,1)} %gather_fusion), calls=%async_computation.1 | async-start | bytes 4194304 | tf_op jit(solution)/shard_map/all_to_all | solution.py:110
  29.8 3.2 copy.108
  33.0 20.7 %all-to-all-done.1 = bf16[64,128,128]{2,1,0:T(8,128)(2,1)S(1)} async-done(((bf16[64,128,128]{2,1,0:T(8,128)(2,1)}), bf16[64,128,128]{2,1,0:T(8,128)(2,1)S(1)}, u32[]{:S(2)}, u32[]{:S(2)}) %all-to-all-start.1) | async-done | bytes 2097184 | tf_op jit(solution)/shard_map/all_to_all | solution.py:110
  54.5 6.3 %fusion.1 = bf16[32,2,128,128]{3,2,1,0:T(8,128)(2,1)} fusion(bf16[1,32,2,128,128]{4,3,2,1,0:T(8,128)(2,1)} %param.8, f32[32,2]{1,0:T(8,128)S(1)} %copy.79, bf16[32,2,2,128,128]{4,3,2,1,0:T(8,128)(2,1)} %bitcast.93, bf16[32,128,128]{2,1,0:T(8,128)(2,1)S(1)} %gather_fusion.1), kind=kOutput, calls=%fused_computation.12 | convolution fusion | flops 542113792 | bytes 9437440 | tf_op jit(solution)/shard_map/fetv,fewv->fetw/dot_general | solution.py:43
  60.8 4.3 %bitcast_convert_fusion.1 = bf16[32,128,128]{2,1,0:T(8,128)(2,1)S(1)} fusion(bf16[32,2,128,128]{3,2,1,0:T(8,128)(2,1)} %fusion.1, bf16[32,2,2,128,128]{4,3,2,1,0:T(8,128)(2,1)} %bitcast.94), kind=kOutput, calls=%fused_computation.22 | convolution fusion | flops 538443776 | bytes 7340032 | tf_op jit(solution)/shard_map/fetw,fewv->fetv/dot_general | solution.py:54
  65.2 2.1 gather_fusion.2
  67.4 8.4 %all-to-all-start.2 = ((bf16[64,128,128]{2,1,0:T(8,128)(2,1)}), bf16[64,128,128]{2,1,0:T(8,128)(2,1)S(1)}, u32[]{:S(2)}, u32[]{:S(2)}) async-start(bf16[64,128,128]{2,1,0:T(8,128)(2,1)} %gather_fusion.2), calls=%async_computation.2 | async-start | bytes 4194304 | tf_op jit(solution)/shard_map/all_to_all | solution.py:117
  78.0 34.6 %all-reduce.4 = f32[256]{0:T(256)S(1)} all-reduce(f32[256]{0:T(256)S(1)} %multiply_dynamic-update-slice_fusion), channel_id=2, replica_groups=mesh['exp'=16,'sky'=32] {'exp'}, use_global_device_ids=true, to_apply=%add.4 | all-reduce | flops 256 | bytes 2048
  115.0 6.8 %all-to-all-start.3 = ((bf16[16,128,128]{2,1,0:T(8,128)(2,1)}), bf16[16,128,128]{2,1,0:T(8,128)(2,1)}, u32[]{:S(2)}, u32[]{:S(2)}) async-start(bf16[16,128,128]{2,1,0:T(8,128)(2,1)} %copy.83), calls=%async_computation.3 | async-start | bytes 1048576 | tf_op jit(solution)/shard_map/all_to_all | solution.py:130
  122.5 1.9 collective-permute-start.1
  124.7 2.6 collective-permute-start
  127.3 2.8 gather_fusion.3
  134.3 13.2 %all-to-all-done.3 = bf16[16,128,128]{2,1,0:T(8,128)(2,1)} async-done(((bf16[16,128,128]{2,1,0:T(8,128)(2,1)}), bf16[16,128,128]{2,1,0:T(8,128)(2,1)}, u32[]{:S(2)}, u32[]{:S(2)}) %all-to-all-start.3) | async-done | bytes 524320 | tf_op jit(solution)/shard_map/all_to_all | solution.py:130
  149.3 32.0 %all-gather = bf16[2048,128]{1,0:T(8,128)(2,1)S(1)} all-gather(bf16[128,128]{1,0:T(8,128)(2,1)S(1)} %divide_convert_fusion.1), channel_id=3, replica_groups=mesh['exp'=16,'sky'=32] {'exp'}, dimensions={0}, use_global_device_ids=true | all-gather | bytes 557056 | tf_op jit(solution)/shard_map/all_gather | solution.py:134
  181.4 2.2 gather_fusion.4
  185.3 2.8 gather_fusion.5
  188.1 5.2 %subtract_convert_fusion = bf16[64,128,128]{2,1,0:T(8,128)(2,1)S(1)} fusion(f32[64,128,128]{2,1,0:T(8,128)} %gather_fusion.3, f32[64,128,128]{2,1,0:T(8,128)} %gather_fusion.5, bf16[64,128,128]{2,1,0:T(8,128)(2,1)} %gather_fusion.4), kind=kLoop, calls=%fused_computation.15 | loop fusion | flops 4194304 | bytes 12582912 | tf_op jit(solution)/shard_map/convert_element_type | solution.py:141
  193.3 31.5 %all_to_all.36 = bf16[64,128,128]{2,1,0:T(8,128)(2,1)} all-to-all(bf16[64,128,128]{2,1,0:T(8,128)(2,1)S(1)} %subtract_convert_fusion), channel_id=1, replica_groups=mesh['exp'=16,'sky'=32] {'sky'}, dimensions={0} | all-to-all | bytes 4194304 | tf_op jit(solution)/shard_map/all_to_all | solution.py:110
  224.8 2.3 gather_fusion.6
  227.1 6.3 %fusion.3 = bf16[32,2,128,128]{3,2,1,0:T(8,128)(2,1)} fusion(bf16[1,32,2,128,128]{4,3,2,1,0:T(8,128)(2,1)} %param.8, f32[32,2]{1,0:T(8,128)S(1)} %copy.79, bf16[32,2,2,128,128]{4,3,2,1,0:T(8,128)(2,1)} %bitcast.95, bf16[32,128,128]{2,1,0:T(8,128)(2,1)S(1)} %gather_fusion.6), kind=kOutput, calls=%fused_computation.14 | convolution fusion | flops 542113792 | bytes 9437440 | tf_op jit(solution)/shard_map/fetv,fewv->fetw/dot_general | solution.py:43
  233.5 4.3 %bitcast_convert_fusion = bf16[32,128,128]{2,1,0:T(8,128)(2,1)S(1)} fusion(bf16[32,2,128,128]{3,2,1,0:T(8,128)(2,1)} %fusion.3, bf16[32,2,2,128,128]{4,3,2,1,0:T(8,128)(2,1)} %bitcast.96), kind=kOutput, calls=%fused_computation.21 | convolution fusion | flops 538443776 | bytes 7340032 | tf_op jit(solution)/shard_map/fetw,fewv->fetv/dot_general | solution.py:54
  237.9 2.2 gather_fusion.7
  240.0 32.6 %all_to_all.37 = bf16[64,128,128]{2,1,0:T(8,128)(2,1)S(1)} all-to-all(bf16[64,128,128]{2,1,0:T(8,128)(2,1)} %gather_fusion.7), channel_id=1, replica_groups=mesh['exp'=16,'sky'=32] {'sky'}, dimensions={0} | all-to-all | bytes 4194304 | tf_op jit(solution)/shard_map/all_to_all | solution.py:117
  274.8 6.7 %all-to-all-start.6 = ((bf16[16,128,128]{2,1,0:T(8,128)(2,1)}), bf16[16,128,128]{2,1,0:T(8,128)(2,1)}, u32[]{:S(2)}, u32[]{:S(2)}) async-start(bf16[16,128,128]{2,1,0:T(8,128)(2,1)} %copy.91), calls=%async_computation.6 | async-start | bytes 1048576 | tf_op jit(solution)/shard_map/all_to_all | solution.py:130
  282.2 2.8 collective-permute-start.3
  285.3 2.3 collective-permute-start.2
  288.1 2.2 collective-permute-done.2
  292.4 17.3 %all-to-all-done.6 = bf16[16,128,128]{2,1,0:T(8,128)(2,1)} async-done(((bf16[16,128,128]{2,1,0:T(8,128)(2,1)}), bf16[16,128,128]{2,1,0:T(8,128)(2,1)}, u32[]{:S(2)}, u32[]{:S(2)}) %all-to-all-start.6) | async-done | bytes 524320 | tf_op jit(solution)/shard_map/all_to_all | solution.py:130
  311.4 32.3 %all-gather.1 = bf16[2048,128]{1,0:T(8,128)(2,1)S(1)} all-gather(bf16[128,128]{1,0:T(8,128)(2,1)S(1)} %divide_convert_fusion), channel_id=4, replica_groups=mesh['exp'=16,'sky'=32] {'exp'}, dimensions={0}, use_global_device_ids=true | all-gather | bytes 557056 | tf_op jit(solution)/shard_map/all_gather | solution.py:134
  (76 shorter events, 30.3 us)
Async XLA Ops:
  3.8 14.9 %all-to-all-start = ((s32[32,2,1]{1,2,0:T(1,128)}), s32[32,2,1]{1,2,0:T(1,128)S(1)}, u32[]{:S(2)}, u32[]{:S(2)}) async-start(s32[32,2,1]{1,2,0:T(1,128)} %bitcast.2), calls=%async_computation | async-start | bytes 32768 | tf_op jit(solution)/shard_map/all_to_all | solution.py:96
  22.2 5.9 %copy-start.5 = (bf16[1,32,2]{1,2,0:T(2,128)(2,1)S(1)}, bf16[1,32,2]{1,2,0:T(2,128)(2,1)}, u32[]{:S(2)}) copy-start(bf16[1,32,2]{1,2,0:T(2,128)(2,1)} %param.9) | copy-start | bytes 388
  22.2 6.0 %copy-start.4 = (s32[1,32,2,2]{1,3,2,0:T(2,128)S(1)}, s32[1,32,2,2]{1,3,2,0:T(2,128)}, u32[]{:S(2)}) copy-start(s32[1,32,2,2]{1,3,2,0:T(2,128)} %param.12) | copy-start | bytes 1540
  22.2 6.3 %copy-start.2 = (bf16[8,128,128]{2,1,0:T(8,128)(2,1)S(1)}, bf16[8,128,128]{2,1,0:T(8,128)(2,1)}, u32[]{:S(2)}) copy-start(bf16[8,128,128]{2,1,0:T(8,128)(2,1)} %param.13) | copy-start | bytes 786436
  22.2 31.5 %all-to-all-start.1 = ((bf16[64,128,128]{2,1,0:T(8,128)(2,1)}), bf16[64,128,128]{2,1,0:T(8,128)(2,1)S(1)}, u32[]{:S(2)}, u32[]{:S(2)}) async-start(bf16[64,128,128]{2,1,0:T(8,128)(2,1)} %gather_fusion), calls=%async_computation.1 | async-start | bytes 4194304 | tf_op jit(solution)/shard_map/all_to_all | solution.py:110
  29.8 3.2 copy-start.3
  67.4 45.2 %all-to-all-start.2 = ((bf16[64,128,128]{2,1,0:T(8,128)(2,1)}), bf16[64,128,128]{2,1,0:T(8,128)(2,1)S(1)}, u32[]{:S(2)}, u32[]{:S(2)}) async-start(bf16[64,128,128]{2,1,0:T(8,128)(2,1)} %gather_fusion.2), calls=%async_computation.2 | async-start | bytes 4194304 | tf_op jit(solution)/shard_map/all_to_all | solution.py:117
  112.7 9.1 %copy-start = (f32[16,128,128]{2,1,0:T(8,128)S(1)}, f32[16,128,128]{2,1,0:T(8,128)}, u32[]{:S(2)}) copy-start(f32[16,128,128]{2,1,0:T(8,128)} %param.7) | copy-start | bytes 3145732
  115.0 32.6 %all-to-all-start.3 = ((bf16[16,128,128]{2,1,0:T(8,128)(2,1)}), bf16[16,128,128]{2,1,0:T(8,128)(2,1)}, u32[]{:S(2)}, u32[]{:S(2)}) async-start(bf16[16,128,128]{2,1,0:T(8,128)(2,1)} %copy.83), calls=%async_computation.3 | async-start | bytes 1048576 | tf_op jit(solution)/shard_map/all_to_all | solution.py:130
  122.5 7.6 %collective-permute-start.1 = (f32[16,128,1]{1,0,2:T(8,128)S(1)}, f32[16,128,1]{1,0,2:T(8,128)S(1)}, u32[]{:S(2)}, u32[]{:S(2)}) collective-permute-start(f32[16,128,1]{1,0,2:T(8,128)S(1)} %copy.106), channel_id=1, source_target_pairs={{1,0},{2,1},{3,2},{4,3},{5,4},{6,5},{7,6},{8,7},{9,8},{10,9},{11,1... | collective-permute-start | bytes 24584 | tf_op jit(solution)/shard_map/ppermute | solution.py:22
  124.7 5.8 %collective-permute-start = (f32[16,128,1]{1,0,2:T(8,128)S(1)}, f32[16,128,1]{1,0,2:T(8,128)S(1)}, u32[]{:S(2)}, u32[]{:S(2)}) collective-permute-start(f32[16,128,1]{1,0,2:T(8,128)S(1)} %copy.105), channel_id=1, source_target_pairs={{0,1},{1,2},{2,3},{3,4},{4,5},{5,6},{6,7},{7,8},{8,9},{9,10},{10,1... | collective-permute-start | bytes 24584 | tf_op jit(solution)/shard_map/ppermute | solution.py:20
  181.4 2.2 copy-start.1
  274.8 34.8 %all-to-all-start.6 = ((bf16[16,128,128]{2,1,0:T(8,128)(2,1)}), bf16[16,128,128]{2,1,0:T(8,128)(2,1)}, u32[]{:S(2)}, u32[]{:S(2)}) async-start(bf16[16,128,128]{2,1,0:T(8,128)(2,1)} %copy.91), calls=%async_computation.6 | async-start | bytes 1048576 | tf_op jit(solution)/shard_map/all_to_all | solution.py:130
  282.2 5.5 %collective-permute-start.3 = (f32[16,128,1]{1,0,2:T(8,128)S(1)}, f32[16,128,1]{1,0,2:T(8,128)S(1)}, u32[]{:S(2)}, u32[]{:S(2)}) collective-permute-start(f32[16,128,1]{1,0,2:T(8,128)S(1)} %copy.93), channel_id=1, source_target_pairs={{1,0},{2,1},{3,2},{4,3},{5,4},{6,5},{7,6},{8,7},{9,8},{10,9},{11,1... | collective-permute-start | bytes 24584 | tf_op jit(solution)/shard_map/ppermute | solution.py:22
  285.3 5.0 %collective-permute-start.2 = (f32[16,128,1]{1,0,2:T(8,128)S(1)}, f32[16,128,1]{1,0,2:T(8,128)S(1)}, u32[]{:S(2)}, u32[]{:S(2)}) collective-permute-start(f32[16,128,1]{1,0,2:T(8,128)S(1)} %copy.92), channel_id=1, source_target_pairs={{0,1},{1,2},{2,3},{3,4},{4,5},{5,6},{6,7},{7,8},{8,9},{9,10},{10,1... | collective-permute-start | bytes 24584 | tf_op jit(solution)/shard_map/ppermute | solution.py:20

commit v10 on v8

--- a/solution.py
+++ b/solution.py
@@ -75,7 +75,7 @@
     foot_tiles = footprint_row.shape[1]
     expo_count = exposures.shape[2]
     n_sky = lax.axis_size("sky")
-    n_exp = lax.axis_size("exp")
+    n_exp = lax.axis_size("exp_hi") * lax.axis_size("exp_lo")
     capacity = max(2, 3 * foot_tiles // (2 * n_sky))
     slot_count = n_sky * capacity
     prior_weight = n_exp * foot_tiles * expo_count / (8.0 * sky_rows)
@@ -100,7 +100,7 @@
     receive_half = receive_map.astype(jnp.bfloat16)
     safe_rows = jnp.maximum(incoming, 0)
     rows_per = sky_rows // n_exp
-    own_rows = lax.axis_index("exp") * rows_per
+    own_rows = (lax.axis_index("exp_hi") * lax.axis_size("exp_lo") + lax.axis_index("exp_lo")) * rows_per
     count_tile = jnp.broadcast_to(
         local_counts[:, None], (sky_rows, tile_edge)
     )
@@ -118,7 +118,7 @@
         outgoing = padded_adjoint[slot_source]
         arrived = lax.all_to_all(outgoing, "sky", split_axis=0, concat_axis=0, tiled=True)
         if iteration == 0:
-            count_tiles = lax.all_gather(count_tile, "exp", axis=0, tiled=True)
+            count_tiles = lax.all_gather(count_tile, ("exp_hi", "exp_lo"), axis=0, tiled=True)
             count_tiles, arrived = lax.optimization_barrier((count_tiles, arrived))
             counts = jnp.sum(
                 count_tiles.astype(jnp.float32).reshape(n_exp, sky_rows, tile_edge)[:, :, 0], axis=0
@@ -129,11 +129,14 @@
             "rj,juv->ruv", receive_half, arrived, preferred_element_type=jnp.float32
         )
         payload = partial_value.astype(jnp.bfloat16).reshape(n_exp, rows_per * tile_edge, tile_edge)
-        row_parts = lax.all_to_all(payload, "exp", split_axis=0, concat_axis=0, tiled=True)
+        row_parts = lax.all_to_all(
+            payload, ("exp_hi", "exp_lo"), split_axis=0, concat_axis=0, tiled=True
+        )
         summed = jnp.sum(row_parts.astype(jnp.float32).reshape((n_exp,) + payload.shape[1:]), axis=0)
         own_total = summed[: rows_per * tile_edge].reshape(rows_per, tile_edge, tile_edge)
         scaled = own_total / own_denominator[:, None, None]
-        gathered = lax.all_gather(scaled.astype(jnp.bfloat16), "exp", axis=0, tiled=True)
+        gathered = lax.all_gather(scaled.astype(jnp.bfloat16), "exp_lo", axis=0, tiled=True)
+        gathered = lax.all_gather(gathered, "exp_hi", axis=0, tiled=True)
         laplacian = laplace_image(padded_2(sky_now, (("sky", 2),), 1))
         smooth = prior_weight * laplacian / denominator[:, None, None]
         sky_now = sky_now - (gathered.astype(jnp.float32) + smooth)
@@ -141,16 +144,23 @@
 
 
 def solution(mesh):
+    n_exp = mesh.shape["exp"]
+    inner = 4 if n_exp % 4 == 0 else 1
+    split_mesh = jax.sharding.Mesh(
+        mesh.devices.reshape((n_exp // inner, inner) + mesh.devices.shape[1:]),
+        ("exp_hi", "exp_lo", "sky"),
+    )
+    exp_axes = ("exp_hi", "exp_lo")
     in_specs = (
         P(None, None, "sky"),
-        P("exp", "sky", None, None, None),
-        P("exp", "sky", None),
-        P("exp", "sky", None),
-        P("exp", "sky"),
-        P("exp", "sky", None, None),
+        P(exp_axes, "sky", None, None, None),
+        P(exp_axes, "sky", None),
+        P(exp_axes, "sky", None),
+        P(exp_axes, "sky"),
+        P(exp_axes, "sky", None, None),
         P(),
     )
     out_specs = P(None, None, "sky")
     return jax.shard_map(
-        per_device, mesh=mesh, in_specs=in_specs, out_specs=out_specs, check_vma=False
+        per_device, mesh=split_mesh, in_specs=in_specs, out_specs=out_specs, check_vma=False
     )

time: 342 us -> 354 us (1.035)
  blocking collectives: 163 us -> 178 us
    all_gather x2 -> x4, blocking collectives: 64.4 us -> 76.6 us  [the longest x2 48.6 us: per_device(): gathered = lax.all_gather(gathered, 'exp_hi', axis=0, tiled=True)]
    ppermute x2, waiting for transfers between devices: 4.44 us -> 0.01 us  [padded_2(): lax.ppermute(tail, axis, [(i, (i + 1) % count) for i in range(ends)])]
where the time goes in v10:
time: 354 us; the launch traced here: 352 us
  blocking collectives  178 us (50%)
  waiting for transfers between devices  58.6 us (17%)
  starting transfers between devices  50 us (14%)
  matrix products  25 us (7%)
  local copies, waits for them, and re-layouts  24.9 us (7%)
  other arithmetic  14.2 us (4%)
    all_gather x2, blocking collectives, per_device(): gathered = lax.all_gather(gathered, 'exp_hi', axis=0, tiled=True)  48.6 us
    unnamed x1, blocking collectives  34.6 us
    all_to_all x1, blocking collectives, per_device(): lax.all_to_all(sky_half[safe_rows], 'sky', split_axis=0, concat_axis=0, t...  34 us
    all_to_all x1, blocking collectives, per_device(): lax.all_to_all(outgoing, 'sky', split_axis=0, concat_axis=0, tiled=True)  32.6 us
    all_to_all x2, waiting for transfers between devices, per_device(): lax.all_to_all(payload, ('exp_hi', 'exp_lo'), split_axis=0, concat_axis=0...  32.2 us
    all_gather x2, blocking collectives, per_device(): lax.all_gather(scaled.astype(jnp.bfloat16), 'exp_lo', axis=0, tiled=True)  28 us
    all_to_all x1, waiting for transfers between devices, per_device(): lax.all_to_all(sky_half[safe_rows], 'sky', split_axis=0, concat_axis=0, t...  20.7 us
    all_to_all x2, starting transfers between devices, per_device(): lax.all_to_all(payload, ('exp_hi', 'exp_lo'), split_axis=0, concat_axis=0...  14.9 us
  transfers between devices with their start and end apart: 9, of which 6 were waited for; matrix products, arithmetic and copies ran while one was open for 5% of the time, Pallas kernels for 0%

profile of v10, /device:TPU:6, one launch (start us, length us, event | category | flops | bytes accessed | tf_op | source)
XLA Modules:
  0.0 351.7 jit_solution(16046092523491671708)
XLA Ops:
  3.8 9.4 %all-to-all-start = ((s32[32,2,1]{1,2,0:T(1,128)}), s32[32,2,1]{1,2,0:T(1,128)S(1)}, u32[]{:S(2)}, u32[]{:S(2)}) async-start(s32[32,2,1]{1,2,0:T(1,128)} %bitcast.2), calls=%async_computation | async-start | bytes 32768 | tf_op jit(solution)/shard_map/all_to_all | solution.py:96
  13.1 1.3 convert_element_type.113
  14.5 4.2 %all-to-all-done = s32[32,2,1]{1,2,0:T(1,128)S(1)} async-done(((s32[32,2,1]{1,2,0:T(1,128)}), s32[32,2,1]{1,2,0:T(1,128)S(1)}, u32[]{:S(2)}, u32[]{:S(2)}) %all-to-all-start) | async-done | bytes 288 | tf_op jit(solution)/shard_map/all_to_all | solution.py:96
  20.0 2.1 gather_fusion
  22.2 5.9 %all-to-all-start.1 = ((bf16[64,128,128]{2,1,0:T(8,128)(2,1)}), bf16[64,128,128]{2,1,0:T(8,128)(2,1)S(1)}, u32[]{:S(2)}, u32[]{:S(2)}) async-start(bf16[64,128,128]{2,1,0:T(8,128)(2,1)} %gather_fusion), calls=%async_computation.1 | async-start | bytes 4194304 | tf_op jit(solution)/shard_map/all_to_all | solution.py:110
  29.7 3.2 copy.87
  33.0 20.7 %all-to-all-done.1 = bf16[64,128,128]{2,1,0:T(8,128)(2,1)S(1)} async-done(((bf16[64,128,128]{2,1,0:T(8,128)(2,1)}), bf16[64,128,128]{2,1,0:T(8,128)(2,1)S(1)}, u32[]{:S(2)}, u32[]{:S(2)}) %all-to-all-start.1) | async-done | bytes 2097184 | tf_op jit(solution)/shard_map/all_to_all | solution.py:110
  54.5 6.3 %fusion.1 = bf16[32,2,128,128]{3,2,1,0:T(8,128)(2,1)} fusion(bf16[1,32,2,128,128]{4,3,2,1,0:T(8,128)(2,1)} %param.8, f32[32,2]{1,0:T(8,128)S(1)} %copy.58, bf16[32,2,2,128,128]{4,3,2,1,0:T(8,128)(2,1)} %bitcast.90, bf16[32,128,128]{2,1,0:T(8,128)(2,1)S(1)} %gather_fusion.1), kind=kOutput, calls=%fused_computation.10 | convolution fusion | flops 542113792 | bytes 9437440 | tf_op jit(solution)/shard_map/fetv,fewv->fetw/dot_general | solution.py:43
  60.8 4.3 %bitcast_convert_fusion.1 = bf16[32,128,128]{2,1,0:T(8,128)(2,1)S(1)} fusion(bf16[32,2,128,128]{3,2,1,0:T(8,128)(2,1)} %fusion.1, bf16[32,2,2,128,128]{4,3,2,1,0:T(8,128)(2,1)} %bitcast.91), kind=kOutput, calls=%fused_computation.19 | convolution fusion | flops 538443776 | bytes 7340032 | tf_op jit(solution)/shard_map/fetw,fewv->fetv/dot_general | solution.py:54
  65.2 2.1 gather_fusion.2
  67.4 8.4 %all-to-all-start.2 = ((bf16[64,128,128]{2,1,0:T(8,128)(2,1)}), bf16[64,128,128]{2,1,0:T(8,128)(2,1)S(1)}, u32[]{:S(2)}, u32[]{:S(2)}) async-start(bf16[64,128,128]{2,1,0:T(8,128)(2,1)} %gather_fusion.2), calls=%async_computation.2 | async-start | bytes 4194304 | tf_op jit(solution)/shard_map/all_to_all | solution.py:119
  78.0 34.6 %all-reduce.4 = f32[256]{0:T(256)S(1)} all-reduce(f32[256]{0:T(256)S(1)} %multiply_dynamic-update-slice_fusion), channel_id=2, replica_groups=mesh['exp_hi'=4,'exp_lo'=4,'sky'=32] {'exp_hi','exp_lo'}, use_global_device_ids=true, to_apply=%add.4 | all-reduce | flops 256 | bytes 2048
  114.9 6.8 %all-to-all-start.3 = ((bf16[16,128,128]{2,1,0:T(8,128)(2,1)}), bf16[16,128,128]{2,1,0:T(8,128)(2,1)}, u32[]{:S(2)}, u32[]{:S(2)}) async-start(bf16[16,128,128]{2,1,0:T(8,128)(2,1)} %copy.62), calls=%async_computation.3 | async-start | bytes 1048576 | tf_op jit(solution)/shard_map/all_to_all | solution.py:132
  122.4 1.9 collective-permute-start
  124.7 3.8 %collective-permute-start.1 = (f32[16,128,1]{1,0,2:T(8,128)S(1)}, f32[16,128,1]{1,0,2:T(8,128)S(1)}, u32[]{:S(2)}, u32[]{:S(2)}) collective-permute-start(f32[16,128,1]{1,0,2:T(8,128)S(1)} %copy.85), channel_id=1, source_target_pairs={{1,0},{2,1},{3,2},{4,3},{5,4},{6,5},{7,6},{8,7},{9,8},{10,9},{11,1... | collective-permute-start | bytes 24584 | tf_op jit(solution)/shard_map/ppermute | solution.py:22
  131.3 1.5 fusion.38
  133.4 14.1 %all-to-all-done.3 = bf16[16,128,128]{2,1,0:T(8,128)(2,1)} async-done(((bf16[16,128,128]{2,1,0:T(8,128)(2,1)}), bf16[16,128,128]{2,1,0:T(8,128)(2,1)}, u32[]{:S(2)}, u32[]{:S(2)}) %all-to-all-start.3) | async-done | bytes 524320 | tf_op jit(solution)/shard_map/all_to_all | solution.py:132
  149.3 14.4 %all-gather = bf16[512,128]{1,0:T(8,128)(2,1)S(1)} all-gather(bf16[128,128]{1,0:T(8,128)(2,1)S(1)} %divide_convert_fusion.1), channel_id=3, replica_groups=mesh['exp_hi'=4,'exp_lo'=4,'sky'=32] {'exp_lo'}, dimensions={0}, use_global_device_ids=true | all-gather | bytes 163840 | tf_op jit(solution)/shard_map/all_gather | solution.py:138
  163.8 22.6 %all_gather.17 = bf16[16,128,128]{2,1,0:T(8,128)(2,1)S(1)} all-gather(bf16[4,128,128]{2,1,0:T(8,128)(2,1)S(1)} %bitcast.96), channel_id=1, replica_groups=mesh['exp_hi'=4,'exp_lo'=4,'sky'=32] {'exp_hi'}, dimensions={0}, use_global_device_ids=true | all-gather | bytes 655360 | tf_op jit(solution)/shard_map/all_gather | solution.py:139
  186.7 2.1 gather_fusion.3
  188.8 34.0 %all_to_all.36 = bf16[64,128,128]{2,1,0:T(8,128)(2,1)} all-to-all(bf16[64,128,128]{2,1,0:T(8,128)(2,1)} %gather_fusion.3), channel_id=1, replica_groups=mesh['exp_hi'=4,'exp_lo'=4,'sky'=32] {'sky'}, dimensions={0} | all-to-all | bytes 4194304 | tf_op jit(solution)/shard_map/all_to_all | solution.py:110
  222.8 2.3 gather_fusion.4
  225.2 6.3 %fusion.3 = bf16[32,2,128,128]{3,2,1,0:T(8,128)(2,1)} fusion(bf16[1,32,2,128,128]{4,3,2,1,0:T(8,128)(2,1)} %param.8, f32[32,2]{1,0:T(8,128)S(1)} %copy.58, bf16[32,2,2,128,128]{4,3,2,1,0:T(8,128)(2,1)} %bitcast.92, bf16[32,128,128]{2,1,0:T(8,128)(2,1)S(1)} %gather_fusion.4), kind=kOutput, calls=%fused_computation.12 | convolution fusion | flops 542113792 | bytes 9437440 | tf_op jit(solution)/shard_map/fetv,fewv->fetw/dot_general | solution.py:43
  231.5 4.3 %bitcast_convert_fusion = bf16[32,128,128]{2,1,0:T(8,128)(2,1)S(1)} fusion(bf16[32,2,128,128]{3,2,1,0:T(8,128)(2,1)} %fusion.3, bf16[32,2,2,128,128]{4,3,2,1,0:T(8,128)(2,1)} %bitcast.93), kind=kOutput, calls=%fused_computation.18 | convolution fusion | flops 538443776 | bytes 7340032 | tf_op jit(solution)/shard_map/fetw,fewv->fetv/dot_general | solution.py:54
  235.9 2.2 gather_fusion.5
  238.1 32.6 %all_to_all.37 = bf16[64,128,128]{2,1,0:T(8,128)(2,1)S(1)} all-to-all(bf16[64,128,128]{2,1,0:T(8,128)(2,1)} %gather_fusion.5), channel_id=1, replica_groups=mesh['exp_hi'=4,'exp_lo'=4,'sky'=32] {'sky'}, dimensions={0} | all-to-all | bytes 4194304 | tf_op jit(solution)/shard_map/all_to_all | solution.py:119
  272.9 8.1 %all-to-all-start.6 = ((bf16[16,128,128]{2,1,0:T(8,128)(2,1)}), bf16[16,128,128]{2,1,0:T(8,128)(2,1)}, u32[]{:S(2)}, u32[]{:S(2)}) async-start(bf16[16,128,128]{2,1,0:T(8,128)(2,1)} %copy.70), calls=%async_computation.6 | async-start | bytes 1048576 | tf_op jit(solution)/shard_map/all_to_all | solution.py:132
  281.7 3.0 collective-permute-start.2
  285.0 2.8 collective-permute-start.3
  291.0 18.1 %all-to-all-done.6 = bf16[16,128,128]{2,1,0:T(8,128)(2,1)} async-done(((bf16[16,128,128]{2,1,0:T(8,128)(2,1)}), bf16[16,128,128]{2,1,0:T(8,128)(2,1)}, u32[]{:S(2)}, u32[]{:S(2)}) %all-to-all-start.6) | async-done | bytes 524320 | tf_op jit(solution)/shard_map/all_to_all | solution.py:132
  310.9 13.6 %all-gather.1 = bf16[512,128]{1,0:T(8,128)(2,1)S(1)} all-gather(bf16[128,128]{1,0:T(8,128)(2,1)S(1)} %divide_convert_fusion), channel_id=4, replica_groups=mesh['exp_hi'=4,'exp_lo'=4,'sky'=32] {'exp_lo'}, dimensions={0}, use_global_device_ids=true | all-gather | bytes 163840 | tf_op jit(solution)/shard_map/all_gather | solution.py:138
  324.4 26.0 %all_gather.19 = bf16[16,128,128]{2,1,0:T(8,128)(2,1)S(1)} all-gather(bf16[4,128,128]{2,1,0:T(8,128)(2,1)S(1)} %bitcast.97), channel_id=1, replica_groups=mesh['exp_hi'=4,'exp_lo'=4,'sky'=32] {'exp_hi'}, dimensions={0}, use_global_device_ids=true | all-gather | bytes 655360 | tf_op jit(solution)/shard_map/all_gather | solution.py:139
  (75 shorter events, 27.5 us)
Async XLA Ops:
  3.8 14.9 %all-to-all-start = ((s32[32,2,1]{1,2,0:T(1,128)}), s32[32,2,1]{1,2,0:T(1,128)S(1)}, u32[]{:S(2)}, u32[]{:S(2)}) async-start(s32[32,2,1]{1,2,0:T(1,128)} %bitcast.2), calls=%async_computation | async-start | bytes 32768 | tf_op jit(solution)/shard_map/all_to_all | solution.py:96
  22.2 5.9 %copy-start.4 = (s32[1,32,2,2]{1,3,2,0:T(2,128)S(1)}, s32[1,32,2,2]{1,3,2,0:T(2,128)}, u32[]{:S(2)}) copy-start(s32[1,32,2,2]{1,3,2,0:T(2,128)} %param.12) | copy-start | bytes 1540
  22.2 6.2 %copy-start.2 = (bf16[8,128,128]{2,1,0:T(8,128)(2,1)S(1)}, bf16[8,128,128]{2,1,0:T(8,128)(2,1)}, u32[]{:S(2)}) copy-start(bf16[8,128,128]{2,1,0:T(8,128)(2,1)} %param.13) | copy-start | bytes 786436
  22.2 31.5 %all-to-all-start.1 = ((bf16[64,128,128]{2,1,0:T(8,128)(2,1)}), bf16[64,128,128]{2,1,0:T(8,128)(2,1)S(1)}, u32[]{:S(2)}, u32[]{:S(2)}) async-start(bf16[64,128,128]{2,1,0:T(8,128)(2,1)} %gather_fusion), calls=%async_computation.1 | async-start | bytes 4194304 | tf_op jit(solution)/shard_map/all_to_all | solution.py:110
  29.7 3.2 copy-start.5
  29.7 3.3 copy-start.3
  67.4 45.2 %all-to-all-start.2 = ((bf16[64,128,128]{2,1,0:T(8,128)(2,1)}), bf16[64,128,128]{2,1,0:T(8,128)(2,1)S(1)}, u32[]{:S(2)}, u32[]{:S(2)}) async-start(bf16[64,128,128]{2,1,0:T(8,128)(2,1)} %gather_fusion.2), calls=%async_computation.2 | async-start | bytes 4194304 | tf_op jit(solution)/shard_map/all_to_all | solution.py:119
  112.7 9.0 %copy-start = (f32[16,128,128]{2,1,0:T(8,128)S(1)}, f32[16,128,128]{2,1,0:T(8,128)}, u32[]{:S(2)}) copy-start(f32[16,128,128]{2,1,0:T(8,128)} %param.7) | copy-start | bytes 3145732
  114.9 32.6 %all-to-all-start.3 = ((bf16[16,128,128]{2,1,0:T(8,128)(2,1)}), bf16[16,128,128]{2,1,0:T(8,128)(2,1)}, u32[]{:S(2)}, u32[]{:S(2)}) async-start(bf16[16,128,128]{2,1,0:T(8,128)(2,1)} %copy.62), calls=%async_computation.3 | async-start | bytes 1048576 | tf_op jit(solution)/shard_map/all_to_all | solution.py:132
  122.4 6.1 %collective-permute-start = (f32[16,128,1]{1,0,2:T(8,128)S(1)}, f32[16,128,1]{1,0,2:T(8,128)S(1)}, u32[]{:S(2)}, u32[]{:S(2)}) collective-permute-start(f32[16,128,1]{1,0,2:T(8,128)S(1)} %copy.84), channel_id=1, source_target_pairs={{0,1},{1,2},{2,3},{3,4},{4,5},{5,6},{6,7},{7,8},{8,9},{9,10},{10,1... | collective-permute-start | bytes 24584 | tf_op jit(solution)/shard_map/ppermute | solution.py:20
  124.7 5.0 %collective-permute-start.1 = (f32[16,128,1]{1,0,2:T(8,128)S(1)}, f32[16,128,1]{1,0,2:T(8,128)S(1)}, u32[]{:S(2)}, u32[]{:S(2)}) collective-permute-start(f32[16,128,1]{1,0,2:T(8,128)S(1)} %copy.85), channel_id=1, source_target_pairs={{1,0},{2,1},{3,2},{4,3},{5,4},{6,5},{7,6},{8,7},{9,8},{10,9},{11,1... | collective-permute-start | bytes 24584 | tf_op jit(solution)/shard_map/ppermute | solution.py:22
  147.5 38.8 %copy-start.1 = (f32[2048,128]{1,0:T(8,128)S(1)}, f32[2048,128]{1,0:T(8,128)}, u32[]{:S(2)}) copy-start(f32[2048,128]{1,0:T(8,128)} %fusion.38) | copy-start | bytes 3145732
  272.9 36.3 %all-to-all-start.6 = ((bf16[16,128,128]{2,1,0:T(8,128)(2,1)}), bf16[16,128,128]{2,1,0:T(8,128)(2,1)}, u32[]{:S(2)}, u32[]{:S(2)}) async-start(bf16[16,128,128]{2,1,0:T(8,128)(2,1)} %copy.70), calls=%async_computation.6 | async-start | bytes 1048576 | tf_op jit(solution)/shard_map/all_to_all | solution.py:132
  281.7 6.1 %collective-permute-start.2 = (f32[16,128,1]{1,0,2:T(8,128)S(1)}, f32[16,128,1]{1,0,2:T(8,128)S(1)}, u32[]{:S(2)}, u32[]{:S(2)}) collective-permute-start(f32[16,128,1]{1,0,2:T(8,128)S(1)} %copy.71), channel_id=1, source_target_pairs={{0,1},{1,2},{2,3},{3,4},{4,5},{5,6},{6,7},{7,8},{8,9},{9,10},{10,1... | collective-permute-start | bytes 24584 | tf_op jit(solution)/shard_map/ppermute | solution.py:20
  285.0 3.9 %collective-permute-start.3 = (f32[16,128,1]{1,0,2:T(8,128)S(1)}, f32[16,128,1]{1,0,2:T(8,128)S(1)}, u32[]{:S(2)}, u32[]{:S(2)}) collective-permute-start(f32[16,128,1]{1,0,2:T(8,128)S(1)} %copy.72), channel_id=1, source_target_pairs={{1,0},{2,1},{3,2},{4,3},{5,4},{6,5},{7,6},{8,7},{9,8},{10,9},{11,1... | collective-permute-start | bytes 24584 | tf_op jit(solution)/shard_map/ppermute | solution.py:22

commit v11 on v8

--- a/solution.py
+++ b/solution.py
@@ -88,8 +88,6 @@
     slot_of = owner_ids * capacity + ranks
     packing = jnp.arange(slot_count, dtype=jnp.int32)[:, None] == slot_of[None, :]
     requested = jnp.sum(jnp.where(packing, tile_rows[None, :] + 1, 0), axis=1) - 1
-    slot_source = jnp.sum(jnp.where(packing, jnp.arange(foot_tiles)[None, :] + 1, 0), axis=1) - 1
-    slot_source = jnp.where(slot_source < 0, foot_tiles, slot_source)
     observed = exposures[0]
     tile_weights = weights[0]
     kernel_ids = kernel_index[0]
@@ -98,6 +96,7 @@
     receive_map = jnp.arange(sky_rows, dtype=jnp.int32)[:, None] == incoming[None, :]
     local_counts = float(expo_count) * jnp.sum(receive_map.astype(jnp.float32), axis=1)
     receive_half = receive_map.astype(jnp.bfloat16)
+    packing_half = packing.astype(jnp.bfloat16)
     safe_rows = jnp.maximum(incoming, 0)
     rows_per = sky_rows // n_exp
     own_rows = lax.axis_index("exp") * rows_per
@@ -110,12 +109,13 @@
         replies = lax.all_to_all(
             sky_half[safe_rows], "sky", split_axis=0, concat_axis=0, tiled=True
         )
-        fetched = replies[slot_of]
+        fetched = jnp.einsum(
+            "jf,juv->fuv", packing_half, replies, preferred_element_type=jnp.float32
+        ).astype(jnp.bfloat16)
         adjoint = adjoint_tiles(fetched, left_kernels, right_kernels, tile_weights, observed)
-        padded_adjoint = jnp.concatenate(
-            [adjoint, jnp.zeros((1, tile_edge, tile_edge), adjoint.dtype)], axis=0
-        )
-        outgoing = padded_adjoint[slot_source]
+        outgoing = jnp.einsum(
+            "jf,fuv->juv", packing_half, adjoint, preferred_element_type=jnp.float32
+        ).astype(jnp.bfloat16)
         arrived = lax.all_to_all(outgoing, "sky", split_axis=0, concat_axis=0, tiled=True)
         if iteration == 0:
             count_tiles = lax.all_gather(count_tile, "exp", axis=0, tiled=True)

time: 342 us -> 343 us (level)
  matrix products: 25 us -> 30.2 us
  local copies, waits for them, and re-layouts: 24.9 us -> 21.3 us
    gather x4 -> x0, local copies, waits for them, and re-layouts: 7.4 us -> none  [the longest x2 4.32 us: per_device(): outgoing = padded_adjoint[slot_source]]
    dot_general x0 -> x4, matrix products: none -> 5.02 us  [the longest x2 3.01 us: per_device(): jnp.einsum('jf,juv->fuv', packing_half, replies, preferred_element_type=j...]
    convert_element_type x0 -> x2, local copies, waits for them, and re-layouts: none -> 4.04 us  [per_device(): outgoing = jnp.einsum('jf,fuv->juv', packing_half, adjoint, preferred_ele...]
where the time goes in v11:
time: 343 us; the launch traced here: 338 us
  blocking collectives  163 us (48%)
  waiting for transfers between devices  60.9 us (18%)
  starting transfers between devices  46.1 us (13%)
  matrix products  30.2 us (9%)
  local copies, waits for them, and re-layouts  21.3 us (6%)
  other arithmetic  15.3 us (4%)
    all_gather x2, blocking collectives, per_device(): lax.all_gather(scaled.astype(jnp.bfloat16), 'exp', axis=0, tiled=True)  64.4 us
    unnamed x1, blocking collectives  34.8 us
    all_to_all x1, blocking collectives, per_device(): lax.all_to_all(outgoing, 'sky', split_axis=0, concat_axis=0, tiled=True)  31.9 us
    all_to_all x1, blocking collectives, per_device(): lax.all_to_all(sky_half[safe_rows], 'sky', split_axis=0, concat_axis=0, t...  31.7 us
    all_to_all x2, waiting for transfers between devices, per_device(): lax.all_to_all(payload, 'exp', split_axis=0, concat_axis=0, tiled=True)  31.2 us
    all_to_all x1, waiting for transfers between devices, per_device(): lax.all_to_all(sky_half[safe_rows], 'sky', split_axis=0, concat_axis=0, t...  20.8 us
    all_to_all x2, starting transfers between devices, per_device(): lax.all_to_all(payload, 'exp', split_axis=0, concat_axis=0, tiled=True)  13.2 us
    dot_general x2, matrix products, adjoint_tiles(): jnp.einsum('fetv,fewv->fetw', left_product, right_kernels, preferred_elem...  12.9 us
  transfers between devices with their start and end apart: 9, of which 6 were waited for; matrix products, arithmetic and copies ran while one was open for 5% of the time, Pallas kernels for 0%

profile of v11, /device:TPU:6, one launch (start us, length us, event | category | flops | bytes accessed | tf_op | source)
XLA Modules:
  0.0 337.6 jit_solution(3747101887943246997)
XLA Ops:
  3.8 9.4 %all-to-all-start = ((s32[32,2,1]{1,2,0:T(1,128)}), s32[32,2,1]{1,2,0:T(1,128)S(1)}, u32[]{:S(2)}, u32[]{:S(2)}) async-start(s32[32,2,1]{1,2,0:T(1,128)} %bitcast.2), calls=%async_computation | async-start | bytes 32768 | tf_op jit(solution)/shard_map/all_to_all | solution.py:94
  14.5 4.2 %all-to-all-done = s32[32,2,1]{1,2,0:T(1,128)S(1)} async-done(((s32[32,2,1]{1,2,0:T(1,128)}), s32[32,2,1]{1,2,0:T(1,128)S(1)}, u32[]{:S(2)}, u32[]{:S(2)}) %all-to-all-start) | async-done | bytes 288 | tf_op jit(solution)/shard_map/all_to_all | solution.py:94
  20.0 2.1 gather_fusion
  22.2 5.9 %all-to-all-start.1 = ((bf16[64,128,128]{2,1,0:T(8,128)(2,1)}), bf16[64,128,128]{2,1,0:T(8,128)(2,1)S(1)}, u32[]{:S(2)}, u32[]{:S(2)}) async-start(bf16[64,128,128]{2,1,0:T(8,128)(2,1)} %gather_fusion), calls=%async_computation.1 | async-start | bytes 4194304 | tf_op jit(solution)/shard_map/all_to_all | solution.py:109
  29.7 3.2 copy.163
  32.9 20.8 %all-to-all-done.1 = bf16[64,128,128]{2,1,0:T(8,128)(2,1)S(1)} async-done(((bf16[64,128,128]{2,1,0:T(8,128)(2,1)}), bf16[64,128,128]{2,1,0:T(8,128)(2,1)S(1)}, u32[]{:S(2)}, u32[]{:S(2)}) %all-to-all-start.1) | async-done | bytes 2097184 | tf_op jit(solution)/shard_map/all_to_all | solution.py:109
  53.7 1.5 fusion.40
  55.2 6.4 %fusion.1 = bf16[32,2,128,128]{3,2,1,0:T(8,128)(2,1)} fusion(bf16[1,32,2,128,128]{4,3,2,1,0:T(8,128)(2,1)} %param.8, f32[32,2]{1,0:T(8,128)S(1)} %copy.122, bf16[32,2,2,128,128]{4,3,2,1,0:T(8,128)(2,1)} %bitcast.78, bf16[32,128,128,1]{2,0,1,3:T(8,128)(2,1)S(1)} %fusion.40), kind=kOutput, calls=%fused_computation.6 | convolution fusion | flops 542113792 | bytes 9437440 | tf_op jit(solution)/shard_map/fetv,fewv->fetw/dot_general | solution.py:43
  61.7 4.3 %bitcast_convert_fusion.1 = bf16[32,128,128]{2,1,0:T(8,128)(2,1)S(1)} fusion(bf16[32,2,128,128]{3,2,1,0:T(8,128)(2,1)} %fusion.1, bf16[32,2,2,128,128]{4,3,2,1,0:T(8,128)(2,1)} %bitcast.79), kind=kOutput, calls=%fused_computation.15 | convolution fusion | flops 538443776 | bytes 7340032 | tf_op jit(solution)/shard_map/fetw,fewv->fetv/dot_general | solution.py:54
  66.9 2.7 copy.128
  69.6 8.4 %all-to-all-start.2 = ((bf16[64,128,128]{2,1,0:T(8,128)(2,1)}), bf16[64,128,128]{2,1,0:T(8,128)(2,1)S(1)}, u32[]{:S(2)}, u32[]{:S(2)}) async-start(bf16[64,128,128]{2,1,0:T(8,128)(2,1)} %copy.128), calls=%async_computation.2 | async-start | bytes 4194304 | tf_op jit(solution)/shard_map/all_to_all | solution.py:119
  80.3 34.8 %all-reduce.2 = f32[256]{0:T(256)S(1)} all-reduce(f32[256]{0:T(256)S(1)} %multiply_dynamic-update-slice_fusion), channel_id=2, replica_groups=mesh['exp'=16,'sky'=32] {'exp'}, use_global_device_ids=true, to_apply=%add.2 | all-reduce | flops 256 | bytes 2048
  117.4 6.8 %all-to-all-start.3 = ((bf16[16,128,128]{2,1,0:T(8,128)(2,1)}), bf16[16,128,128]{2,1,0:T(8,128)(2,1)}, u32[]{:S(2)}, u32[]{:S(2)}) async-start(bf16[16,128,128]{2,1,0:T(8,128)(2,1)} %copy.130), calls=%async_computation.3 | async-start | bytes 1048576 | tf_op jit(solution)/shard_map/all_to_all | solution.py:132
  124.9 1.9 collective-permute-start.1
  127.1 2.4 collective-permute-start
  129.9 2.2 collective-permute-done
  133.7 1.5 fusion.54
  135.9 14.0 %all-to-all-done.3 = bf16[16,128,128]{2,1,0:T(8,128)(2,1)} async-done(((bf16[16,128,128]{2,1,0:T(8,128)(2,1)}), bf16[16,128,128]{2,1,0:T(8,128)(2,1)}, u32[]{:S(2)}, u32[]{:S(2)}) %all-to-all-start.3) | async-done | bytes 524320 | tf_op jit(solution)/shard_map/all_to_all | solution.py:132
  151.6 32.0 %all-gather = bf16[2048,128]{1,0:T(8,128)(2,1)S(1)} all-gather(bf16[128,128]{1,0:T(8,128)(2,1)S(1)} %divide_convert_fusion.1), channel_id=3, replica_groups=mesh['exp'=16,'sky'=32] {'exp'}, dimensions={0}, use_global_device_ids=true | all-gather | bytes 557056 | tf_op jit(solution)/shard_map/all_gather | solution.py:136
  183.6 1.5 fusion.81
  185.1 2.1 gather_fusion.1
  187.3 31.7 %all_to_all.36 = bf16[64,128,128]{2,1,0:T(8,128)(2,1)S(1)} all-to-all(bf16[64,128,128]{2,1,0:T(8,128)(2,1)} %gather_fusion.1), channel_id=1, replica_groups=mesh['exp'=16,'sky'=32] {'sky'}, dimensions={0} | all-to-all | bytes 4194304 | tf_op jit(solution)/shard_map/all_to_all | solution.py:109
  219.0 1.5 fusion.37
  220.5 6.4 %fusion.3 = bf16[32,2,128,128]{3,2,1,0:T(8,128)(2,1)} fusion(bf16[1,32,2,128,128]{4,3,2,1,0:T(8,128)(2,1)} %param.8, f32[32,2]{1,0:T(8,128)S(1)} %copy.122, bf16[32,2,2,128,128]{4,3,2,1,0:T(8,128)(2,1)} %bitcast.80, bf16[32,128,128,1]{2,0,1,3:T(8,128)(2,1)S(1)} %fusion.37), kind=kOutput, calls=%fused_computation.8 | convolution fusion | flops 542113792 | bytes 9437440 | tf_op jit(solution)/shard_map/fetv,fewv->fetw/dot_general | solution.py:43
  226.9 4.3 %bitcast_convert_fusion = bf16[32,128,128]{2,1,0:T(8,128)(2,1)S(1)} fusion(bf16[32,2,128,128]{3,2,1,0:T(8,128)(2,1)} %fusion.3, bf16[32,2,2,128,128]{4,3,2,1,0:T(8,128)(2,1)} %bitcast.81), kind=kOutput, calls=%fused_computation.14 | convolution fusion | flops 538443776 | bytes 7340032 | tf_op jit(solution)/shard_map/fetw,fewv->fetv/dot_general | solution.py:54
  233.6 31.9 %all_to_all.37 = bf16[64,128,128]{2,1,0:T(8,128)(2,1)S(1)} all-to-all(bf16[64,128,128]{2,1,0:T(8,128)(2,1)S(1)} %copy.140), channel_id=1, replica_groups=mesh['exp'=16,'sky'=32] {'sky'}, dimensions={0} | all-to-all | bytes 4194304 | tf_op jit(solution)/shard_map/all_to_all | solution.py:119
  267.7 6.4 %all-to-all-start.6 = ((bf16[16,128,128]{2,1,0:T(8,128)(2,1)}), bf16[16,128,128]{2,1,0:T(8,128)(2,1)}, u32[]{:S(2)}, u32[]{:S(2)}) async-start(bf16[16,128,128]{2,1,0:T(8,128)(2,1)} %copy.142), calls=%async_computation.6 | async-start | bytes 1048576 | tf_op jit(solution)/shard_map/all_to_all | solution.py:132
  274.8 2.8 collective-permute-start.3
  278.0 2.1 collective-permute-start.2
  280.5 2.5 collective-permute-done.2
  285.1 17.2 %all-to-all-done.6 = bf16[16,128,128]{2,1,0:T(8,128)(2,1)} async-done(((bf16[16,128,128]{2,1,0:T(8,128)(2,1)}), bf16[16,128,128]{2,1,0:T(8,128)(2,1)}, u32[]{:S(2)}, u32[]{:S(2)}) %all-to-all-start.6) | async-done | bytes 524320 | tf_op jit(solution)/shard_map/all_to_all | solution.py:132
  304.0 32.4 %all-gather.1 = bf16[2048,128]{1,0:T(8,128)(2,1)S(1)} all-gather(bf16[128,128]{1,0:T(8,128)(2,1)S(1)} %divide_convert_fusion), channel_id=4, replica_groups=mesh['exp'=16,'sky'=32] {'exp'}, dimensions={0}, use_global_device_ids=true | all-gather | bytes 557056 | tf_op jit(solution)/shard_map/all_gather | solution.py:136
  (65 shorter events, 29.3 us)
Async XLA Ops:
  3.8 14.9 %all-to-all-start = ((s32[32,2,1]{1,2,0:T(1,128)}), s32[32,2,1]{1,2,0:T(1,128)S(1)}, u32[]{:S(2)}, u32[]{:S(2)}) async-start(s32[32,2,1]{1,2,0:T(1,128)} %bitcast.2), calls=%async_computation | async-start | bytes 32768 | tf_op jit(solution)/shard_map/all_to_all | solution.py:94
  22.2 5.9 %copy-start.3 = (bf16[1,32,2]{1,2,0:T(2,128)(2,1)S(1)}, bf16[1,32,2]{1,2,0:T(2,128)(2,1)}, u32[]{:S(2)}) copy-start(bf16[1,32,2]{1,2,0:T(2,128)(2,1)} %param.9) | copy-start | bytes 388
  22.2 6.0 %copy-start.2 = (s32[1,32,2,2]{1,3,2,0:T(2,128)S(1)}, s32[1,32,2,2]{1,3,2,0:T(2,128)}, u32[]{:S(2)}) copy-start(s32[1,32,2,2]{1,3,2,0:T(2,128)} %param.12) | copy-start | bytes 1540
  22.2 6.3 %copy-start.1 = (bf16[8,128,128]{2,1,0:T(8,128)(2,1)S(1)}, bf16[8,128,128]{2,1,0:T(8,128)(2,1)}, u32[]{:S(2)}) copy-start(bf16[8,128,128]{2,1,0:T(8,128)(2,1)} %param.13) | copy-start | bytes 786436
  22.2 31.5 %all-to-all-start.1 = ((bf16[64,128,128]{2,1,0:T(8,128)(2,1)}), bf16[64,128,128]{2,1,0:T(8,128)(2,1)S(1)}, u32[]{:S(2)}, u32[]{:S(2)}) async-start(bf16[64,128,128]{2,1,0:T(8,128)(2,1)} %gather_fusion), calls=%async_computation.1 | async-start | bytes 4194304 | tf_op jit(solution)/shard_map/all_to_all | solution.py:109
  69.6 45.4 %all-to-all-start.2 = ((bf16[64,128,128]{2,1,0:T(8,128)(2,1)}), bf16[64,128,128]{2,1,0:T(8,128)(2,1)S(1)}, u32[]{:S(2)}, u32[]{:S(2)}) async-start(bf16[64,128,128]{2,1,0:T(8,128)(2,1)} %copy.128), calls=%async_computation.2 | async-start | bytes 4194304 | tf_op jit(solution)/shard_map/all_to_all | solution.py:119
  115.1 9.0 %copy-start = (f32[16,128,128]{2,1,0:T(8,128)S(1)}, f32[16,128,128]{2,1,0:T(8,128)}, u32[]{:S(2)}) copy-start(f32[16,128,128]{2,1,0:T(8,128)} %param.7) | copy-start | bytes 3145732
  117.4 32.5 %all-to-all-start.3 = ((bf16[16,128,128]{2,1,0:T(8,128)(2,1)}), bf16[16,128,128]{2,1,0:T(8,128)(2,1)}, u32[]{:S(2)}, u32[]{:S(2)}) async-start(bf16[16,128,128]{2,1,0:T(8,128)(2,1)} %copy.130), calls=%async_computation.3 | async-start | bytes 1048576 | tf_op jit(solution)/shard_map/all_to_all | solution.py:132
  124.9 4.7 %collective-permute-start.1 = (f32[16,128,1]{1,0,2:T(8,128)S(1)}, f32[16,128,1]{1,0,2:T(8,128)S(1)}, u32[]{:S(2)}, u32[]{:S(2)}) collective-permute-start(f32[16,128,1]{1,0,2:T(8,128)S(1)} %copy.161), channel_id=1, source_target_pairs={{1,0},{2,1},{3,2},{4,3},{5,4},{6,5},{7,6},{8,7},{9,8},{10,9},{11,1... | collective-permute-start | bytes 24584 | tf_op jit(solution)/shard_map/ppermute | solution.py:22
  127.1 5.0 %collective-permute-start = (f32[16,128,1]{1,0,2:T(8,128)S(1)}, f32[16,128,1]{1,0,2:T(8,128)S(1)}, u32[]{:S(2)}, u32[]{:S(2)}) collective-permute-start(f32[16,128,1]{1,0,2:T(8,128)S(1)} %copy.160), channel_id=1, source_target_pairs={{0,1},{1,2},{2,3},{3,4},{4,5},{5,6},{6,7},{7,8},{8,9},{9,10},{10,1... | collective-permute-start | bytes 24584 | tf_op jit(solution)/shard_map/ppermute | solution.py:20
  267.7 34.5 %all-to-all-start.6 = ((bf16[16,128,128]{2,1,0:T(8,128)(2,1)}), bf16[16,128,128]{2,1,0:T(8,128)(2,1)}, u32[]{:S(2)}, u32[]{:S(2)}) async-start(bf16[16,128,128]{2,1,0:T(8,128)(2,1)} %copy.142), calls=%async_computation.6 | async-start | bytes 1048576 | tf_op jit(solution)/shard_map/all_to_all | solution.py:132
  274.8 5.3 %collective-permute-start.3 = (f32[16,128,1]{1,0,2:T(8,128)S(1)}, f32[16,128,1]{1,0,2:T(8,128)S(1)}, u32[]{:S(2)}, u32[]{:S(2)}) collective-permute-start(f32[16,128,1]{1,0,2:T(8,128)S(1)} %copy.144), channel_id=1, source_target_pairs={{1,0},{2,1},{3,2},{4,3},{5,4},{6,5},{7,6},{8,7},{9,8},{10,9},{11,1... | collective-permute-start | bytes 24584 | tf_op jit(solution)/shard_map/ppermute | solution.py:22
  278.0 5.0 %collective-permute-start.2 = (f32[16,128,1]{1,0,2:T(8,128)S(1)}, f32[16,128,1]{1,0,2:T(8,128)S(1)}, u32[]{:S(2)}, u32[]{:S(2)}) collective-permute-start(f32[16,128,1]{1,0,2:T(8,128)S(1)} %copy.143), channel_id=1, source_target_pairs={{0,1},{1,2},{2,3},{3,4},{4,5},{5,6},{6,7},{7,8},{8,9},{9,10},{10,1... | collective-permute-start | bytes 24584 | tf_op jit(solution)/shard_map/ppermute | solution.py:20

commit v12 on v8

--- a/solution.py
+++ b/solution.py
@@ -81,10 +81,11 @@
     prior_weight = n_exp * foot_tiles * expo_count / (8.0 * sky_rows)
     owner_ids = footprint_owner[0, :, 0]
     tile_rows = footprint_row[0]
-    onehot_owner = (owner_ids[:, None] == jnp.arange(n_sky, dtype=jnp.int32)[None, :]).astype(
-        jnp.int32
+    positions = jnp.arange(foot_tiles, dtype=jnp.int32)
+    earlier_same = (owner_ids[:, None] == owner_ids[None, :]) & (
+        positions[:, None] > positions[None, :]
     )
-    ranks = jnp.sum((jnp.cumsum(onehot_owner, axis=0) - onehot_owner) * onehot_owner, axis=1)
+    ranks = jnp.sum(earlier_same.astype(jnp.int32), axis=1)
     slot_of = owner_ids * capacity + ranks
     packing = jnp.arange(slot_count, dtype=jnp.int32)[:, None] == slot_of[None, :]
     requested = jnp.sum(jnp.where(packing, tile_rows[None, :] + 1, 0), axis=1) - 1

time: 342 us -> 341 us (level)
  no operation moved by 1% of the time
where the time goes in v12:
time: 341 us; the launch traced here: 336 us
  blocking collectives  163 us (48%)
  waiting for transfers between devices  60.7 us (18%)
  starting transfers between devices  46.5 us (14%)
  matrix products  25 us (7%)
  local copies, waits for them, and re-layouts  24.9 us (7%)
  other arithmetic  14.6 us (4%)
    all_gather x2, blocking collectives, per_device(): lax.all_gather(scaled.astype(jnp.bfloat16), 'exp', axis=0, tiled=True)  64.5 us
    unnamed x1, blocking collectives  34.6 us
    all_to_all x1, blocking collectives, per_device(): lax.all_to_all(outgoing, 'sky', split_axis=0, concat_axis=0, tiled=True)  32.6 us
    all_to_all x1, blocking collectives, per_device(): lax.all_to_all(sky_half[safe_rows], 'sky', split_axis=0, concat_axis=0, t...  31.6 us
    all_to_all x2, waiting for transfers between devices, per_device(): lax.all_to_all(payload, 'exp', split_axis=0, concat_axis=0, tiled=True)  31.3 us
    all_to_all x1, waiting for transfers between devices, per_device(): lax.all_to_all(sky_half[safe_rows], 'sky', split_axis=0, concat_axis=0, t...  20.7 us
    all_to_all x2, starting transfers between devices, per_device(): lax.all_to_all(payload, 'exp', split_axis=0, concat_axis=0, tiled=True)  13.5 us
    dot_general x2, matrix products, adjoint_tiles(): jnp.einsum('fetv,fewv->fetw', left_product, right_kernels, preferred_elem...  12.7 us
  transfers between devices with their start and end apart: 9, of which 6 were waited for; matrix products, arithmetic and copies ran while one was open for 5% of the time, Pallas kernels for 0%

profile of v12, /device:TPU:6, one launch (start us, length us, event | category | flops | bytes accessed | tf_op | source)
XLA Modules:
  0.0 336.0 jit_solution(602514145983787084)
XLA Ops:
  3.1 9.4 %all-to-all-start = ((s32[32,2,1]{1,2,0:T(1,128)}), s32[32,2,1]{1,2,0:T(1,128)S(1)}, u32[]{:S(2)}, u32[]{:S(2)}) async-start(s32[32,2,1]{1,2,0:T(1,128)} %bitcast.2), calls=%async_computation | async-start | bytes 32768 | tf_op jit(solution)/shard_map/all_to_all | solution.py:97
  13.7 4.2 %all-to-all-done = s32[32,2,1]{1,2,0:T(1,128)S(1)} async-done(((s32[32,2,1]{1,2,0:T(1,128)}), s32[32,2,1]{1,2,0:T(1,128)S(1)}, u32[]{:S(2)}, u32[]{:S(2)}) %all-to-all-start) | async-done | bytes 288 | tf_op jit(solution)/shard_map/all_to_all | solution.py:97
  19.3 2.1 gather_fusion
  21.5 5.9 %all-to-all-start.1 = ((bf16[64,128,128]{2,1,0:T(8,128)(2,1)}), bf16[64,128,128]{2,1,0:T(8,128)(2,1)S(1)}, u32[]{:S(2)}, u32[]{:S(2)}) async-start(bf16[64,128,128]{2,1,0:T(8,128)(2,1)} %gather_fusion), calls=%async_computation.1 | async-start | bytes 4194304 | tf_op jit(solution)/shard_map/all_to_all | solution.py:111
  29.1 3.2 copy.108
  32.3 20.7 %all-to-all-done.1 = bf16[64,128,128]{2,1,0:T(8,128)(2,1)S(1)} async-done(((bf16[64,128,128]{2,1,0:T(8,128)(2,1)}), bf16[64,128,128]{2,1,0:T(8,128)(2,1)S(1)}, u32[]{:S(2)}, u32[]{:S(2)}) %all-to-all-start.1) | async-done | bytes 2097184 | tf_op jit(solution)/shard_map/all_to_all | solution.py:111
  53.8 6.3 %fusion.1 = bf16[32,2,128,128]{3,2,1,0:T(8,128)(2,1)} fusion(bf16[1,32,2,128,128]{4,3,2,1,0:T(8,128)(2,1)} %param.8, f32[32,2]{1,0:T(8,128)S(1)} %copy.79, bf16[32,2,2,128,128]{4,3,2,1,0:T(8,128)(2,1)} %bitcast.92, bf16[32,128,128]{2,1,0:T(8,128)(2,1)S(1)} %gather_fusion.1), kind=kOutput, calls=%fused_computation.10 | convolution fusion | flops 542113792 | bytes 9437440 | tf_op jit(solution)/shard_map/fetv,fewv->fetw/dot_general | solution.py:43
  60.1 4.3 %bitcast_convert_fusion.1 = bf16[32,128,128]{2,1,0:T(8,128)(2,1)S(1)} fusion(bf16[32,2,128,128]{3,2,1,0:T(8,128)(2,1)} %fusion.1, bf16[32,2,2,128,128]{4,3,2,1,0:T(8,128)(2,1)} %bitcast.93), kind=kOutput, calls=%fused_computation.19 | convolution fusion | flops 538443776 | bytes 7340032 | tf_op jit(solution)/shard_map/fetw,fewv->fetv/dot_general | solution.py:54
  64.5 2.1 gather_fusion.2
  66.7 8.4 %all-to-all-start.2 = ((bf16[64,128,128]{2,1,0:T(8,128)(2,1)}), bf16[64,128,128]{2,1,0:T(8,128)(2,1)S(1)}, u32[]{:S(2)}, u32[]{:S(2)}) async-start(bf16[64,128,128]{2,1,0:T(8,128)(2,1)} %gather_fusion.2), calls=%async_computation.2 | async-start | bytes 4194304 | tf_op jit(solution)/shard_map/all_to_all | solution.py:120
  77.3 34.6 %all-reduce.4 = f32[256]{0:T(256)S(1)} all-reduce(f32[256]{0:T(256)S(1)} %multiply_dynamic-update-slice_fusion), channel_id=2, replica_groups=mesh['exp'=16,'sky'=32] {'exp'}, use_global_device_ids=true, to_apply=%add.4 | all-reduce | flops 256 | bytes 2048
  114.2 6.8 %all-to-all-start.3 = ((bf16[16,128,128]{2,1,0:T(8,128)(2,1)}), bf16[16,128,128]{2,1,0:T(8,128)(2,1)}, u32[]{:S(2)}, u32[]{:S(2)}) async-start(bf16[16,128,128]{2,1,0:T(8,128)(2,1)} %copy.83), calls=%async_computation.3 | async-start | bytes 1048576 | tf_op jit(solution)/shard_map/all_to_all | solution.py:133
  121.7 1.9 collective-permute-start.1
  124.0 2.6 collective-permute-start
  126.9 2.0 collective-permute-done
  130.5 1.5 fusion.38
  132.7 14.1 %all-to-all-done.3 = bf16[16,128,128]{2,1,0:T(8,128)(2,1)} async-done(((bf16[16,128,128]{2,1,0:T(8,128)(2,1)}), bf16[16,128,128]{2,1,0:T(8,128)(2,1)}, u32[]{:S(2)}, u32[]{:S(2)}) %all-to-all-start.3) | async-done | bytes 524320 | tf_op jit(solution)/shard_map/all_to_all | solution.py:133
  148.5 32.2 %all-gather = bf16[2048,128]{1,0:T(8,128)(2,1)S(1)} all-gather(bf16[128,128]{1,0:T(8,128)(2,1)S(1)} %divide_convert_fusion.1), channel_id=3, replica_groups=mesh['exp'=16,'sky'=32] {'exp'}, dimensions={0}, use_global_device_ids=true | all-gather | bytes 557056 | tf_op jit(solution)/shard_map/all_gather | solution.py:137
  180.6 1.5 fusion.56
  182.2 2.1 gather_fusion.3
  184.3 31.6 %all_to_all.36 = bf16[64,128,128]{2,1,0:T(8,128)(2,1)} all-to-all(bf16[64,128,128]{2,1,0:T(8,128)(2,1)} %gather_fusion.3), channel_id=1, replica_groups=mesh['exp'=16,'sky'=32] {'sky'}, dimensions={0} | all-to-all | bytes 4194304 | tf_op jit(solution)/shard_map/all_to_all | solution.py:111
  215.9 2.3 gather_fusion.4
  218.2 6.3 %fusion.3 = bf16[32,2,128,128]{3,2,1,0:T(8,128)(2,1)} fusion(bf16[1,32,2,128,128]{4,3,2,1,0:T(8,128)(2,1)} %param.8, f32[32,2]{1,0:T(8,128)S(1)} %copy.79, bf16[32,2,2,128,128]{4,3,2,1,0:T(8,128)(2,1)} %bitcast.94, bf16[32,128,128]{2,1,0:T(8,128)(2,1)S(1)} %gather_fusion.4), kind=kOutput, calls=%fused_computation.12 | convolution fusion | flops 542113792 | bytes 9437440 | tf_op jit(solution)/shard_map/fetv,fewv->fetw/dot_general | solution.py:43
  224.6 4.3 %bitcast_convert_fusion = bf16[32,128,128]{2,1,0:T(8,128)(2,1)S(1)} fusion(bf16[32,2,128,128]{3,2,1,0:T(8,128)(2,1)} %fusion.3, bf16[32,2,2,128,128]{4,3,2,1,0:T(8,128)(2,1)} %bitcast.95), kind=kOutput, calls=%fused_computation.18 | convolution fusion | flops 538443776 | bytes 7340032 | tf_op jit(solution)/shard_map/fetw,fewv->fetv/dot_general | solution.py:54
  229.0 2.2 gather_fusion.5
  231.2 32.6 %all_to_all.37 = bf16[64,128,128]{2,1,0:T(8,128)(2,1)S(1)} all-to-all(bf16[64,128,128]{2,1,0:T(8,128)(2,1)} %gather_fusion.5), channel_id=1, replica_groups=mesh['exp'=16,'sky'=32] {'sky'}, dimensions={0} | all-to-all | bytes 4194304 | tf_op jit(solution)/shard_map/all_to_all | solution.py:120
  265.9 6.7 %all-to-all-start.6 = ((bf16[16,128,128]{2,1,0:T(8,128)(2,1)}), bf16[16,128,128]{2,1,0:T(8,128)(2,1)}, u32[]{:S(2)}, u32[]{:S(2)}) async-start(bf16[16,128,128]{2,1,0:T(8,128)(2,1)} %copy.91), calls=%async_computation.6 | async-start | bytes 1048576 | tf_op jit(solution)/shard_map/all_to_all | solution.py:133
  273.3 2.8 collective-permute-start.3
  276.5 2.1 collective-permute-start.2
  279.0 2.5 collective-permute-done.2
  283.5 17.3 %all-to-all-done.6 = bf16[16,128,128]{2,1,0:T(8,128)(2,1)} async-done(((bf16[16,128,128]{2,1,0:T(8,128)(2,1)}), bf16[16,128,128]{2,1,0:T(8,128)(2,1)}, u32[]{:S(2)}, u32[]{:S(2)}) %all-to-all-start.6) | async-done | bytes 524320 | tf_op jit(solution)/shard_map/all_to_all | solution.py:133
  302.5 32.3 %all-gather.1 = bf16[2048,128]{1,0:T(8,128)(2,1)S(1)} all-gather(bf16[128,128]{1,0:T(8,128)(2,1)S(1)} %divide_convert_fusion), channel_id=4, replica_groups=mesh['exp'=16,'sky'=32] {'exp'}, dimensions={0}, use_global_device_ids=true | all-gather | bytes 557056 | tf_op jit(solution)/shard_map/all_gather | solution.py:137
  (69 shorter events, 26.2 us)
Async XLA Ops:
  3.1 14.9 %all-to-all-start = ((s32[32,2,1]{1,2,0:T(1,128)}), s32[32,2,1]{1,2,0:T(1,128)S(1)}, u32[]{:S(2)}, u32[]{:S(2)}) async-start(s32[32,2,1]{1,2,0:T(1,128)} %bitcast.2), calls=%async_computation | async-start | bytes 32768 | tf_op jit(solution)/shard_map/all_to_all | solution.py:97
  21.5 5.9 %copy-start.4 = (bf16[1,32,2]{1,2,0:T(2,128)(2,1)S(1)}, bf16[1,32,2]{1,2,0:T(2,128)(2,1)}, u32[]{:S(2)}) copy-start(bf16[1,32,2]{1,2,0:T(2,128)(2,1)} %param.9) | copy-start | bytes 388
  21.5 6.0 %copy-start.2 = (s32[1,32,2,2]{1,3,2,0:T(2,128)S(1)}, s32[1,32,2,2]{1,3,2,0:T(2,128)}, u32[]{:S(2)}) copy-start(s32[1,32,2,2]{1,3,2,0:T(2,128)} %param.12) | copy-start | bytes 1540
  21.5 6.3 %copy-start.1 = (bf16[8,128,128]{2,1,0:T(8,128)(2,1)S(1)}, bf16[8,128,128]{2,1,0:T(8,128)(2,1)}, u32[]{:S(2)}) copy-start(bf16[8,128,128]{2,1,0:T(8,128)(2,1)} %param.13) | copy-start | bytes 786436
  21.5 31.5 %all-to-all-start.1 = ((bf16[64,128,128]{2,1,0:T(8,128)(2,1)}), bf16[64,128,128]{2,1,0:T(8,128)(2,1)S(1)}, u32[]{:S(2)}, u32[]{:S(2)}) async-start(bf16[64,128,128]{2,1,0:T(8,128)(2,1)} %gather_fusion), calls=%async_computation.1 | async-start | bytes 4194304 | tf_op jit(solution)/shard_map/all_to_all | solution.py:111
  29.0 3.2 copy-start.3
  66.7 45.2 %all-to-all-start.2 = ((bf16[64,128,128]{2,1,0:T(8,128)(2,1)}), bf16[64,128,128]{2,1,0:T(8,128)(2,1)S(1)}, u32[]{:S(2)}, u32[]{:S(2)}) async-start(bf16[64,128,128]{2,1,0:T(8,128)(2,1)} %gather_fusion.2), calls=%async_computation.2 | async-start | bytes 4194304 | tf_op jit(solution)/shard_map/all_to_all | solution.py:120
  112.0 9.0 %copy-start = (f32[16,128,128]{2,1,0:T(8,128)S(1)}, f32[16,128,128]{2,1,0:T(8,128)}, u32[]{:S(2)}) copy-start(f32[16,128,128]{2,1,0:T(8,128)} %param.7) | copy-start | bytes 3145732
  114.2 32.6 %all-to-all-start.3 = ((bf16[16,128,128]{2,1,0:T(8,128)(2,1)}), bf16[16,128,128]{2,1,0:T(8,128)(2,1)}, u32[]{:S(2)}, u32[]{:S(2)}) async-start(bf16[16,128,128]{2,1,0:T(8,128)(2,1)} %copy.83), calls=%async_computation.3 | async-start | bytes 1048576 | tf_op jit(solution)/shard_map/all_to_all | solution.py:133
  121.7 4.9 %collective-permute-start.1 = (f32[16,128,1]{1,0,2:T(8,128)S(1)}, f32[16,128,1]{1,0,2:T(8,128)S(1)}, u32[]{:S(2)}, u32[]{:S(2)}) collective-permute-start(f32[16,128,1]{1,0,2:T(8,128)S(1)} %copy.106), channel_id=1, source_target_pairs={{1,0},{2,1},{3,2},{4,3},{5,4},{6,5},{7,6},{8,7},{9,8},{10,9},{11,1... | collective-permute-start | bytes 24584 | tf_op jit(solution)/shard_map/ppermute | solution.py:22
  124.0 5.0 %collective-permute-start = (f32[16,128,1]{1,0,2:T(8,128)S(1)}, f32[16,128,1]{1,0,2:T(8,128)S(1)}, u32[]{:S(2)}, u32[]{:S(2)}) collective-permute-start(f32[16,128,1]{1,0,2:T(8,128)S(1)} %copy.105), channel_id=1, source_target_pairs={{0,1},{1,2},{2,3},{3,4},{4,5},{5,6},{6,7},{7,8},{8,9},{9,10},{10,1... | collective-permute-start | bytes 24584 | tf_op jit(solution)/shard_map/ppermute | solution.py:20
  265.9 34.9 %all-to-all-start.6 = ((bf16[16,128,128]{2,1,0:T(8,128)(2,1)}), bf16[16,128,128]{2,1,0:T(8,128)(2,1)}, u32[]{:S(2)}, u32[]{:S(2)}) async-start(bf16[16,128,128]{2,1,0:T(8,128)(2,1)} %copy.91), calls=%async_computation.6 | async-start | bytes 1048576 | tf_op jit(solution)/shard_map/all_to_all | solution.py:133
  273.3 5.3 %collective-permute-start.3 = (f32[16,128,1]{1,0,2:T(8,128)S(1)}, f32[16,128,1]{1,0,2:T(8,128)S(1)}, u32[]{:S(2)}, u32[]{:S(2)}) collective-permute-start(f32[16,128,1]{1,0,2:T(8,128)S(1)} %copy.93), channel_id=1, source_target_pairs={{1,0},{2,1},{3,2},{4,3},{5,4},{6,5},{7,6},{8,7},{9,8},{10,9},{11,1... | collective-permute-start | bytes 24584 | tf_op jit(solution)/shard_map/ppermute | solution.py:22
  276.5 5.0 %collective-permute-start.2 = (f32[16,128,1]{1,0,2:T(8,128)S(1)}, f32[16,128,1]{1,0,2:T(8,128)S(1)}, u32[]{:S(2)}, u32[]{:S(2)}) collective-permute-start(f32[16,128,1]{1,0,2:T(8,128)S(1)} %copy.92), channel_id=1, source_target_pairs={{0,1},{1,2},{2,3},{3,4},{4,5},{5,6},{6,7},{7,8},{8,9},{9,10},{10,1... | collective-permute-start | bytes 24584 | tf_op jit(solution)/shard_map/ppermute | solution.py:20

commit v13 on v8

--- a/solution.py
+++ b/solution.py
@@ -106,9 +106,8 @@
     )
     sky_now = sky_start
     for iteration in range(ITERS):
-        sky_half = sky_now.astype(jnp.bfloat16)
         replies = lax.all_to_all(
-            sky_half[safe_rows], "sky", split_axis=0, concat_axis=0, tiled=True
+            sky_now[safe_rows].astype(jnp.bfloat16), "sky", split_axis=0, concat_axis=0, tiled=True
         )
         fetched = replies[slot_of]
         adjoint = adjoint_tiles(fetched, left_kernels, right_kernels, tile_weights, observed)

time: 342 us -> 341 us (level)
  blocking collectives: 163 us -> 178 us
  starting transfers between devices: 46.5 us -> 37.2 us
  other arithmetic: 15.3 us -> 11.8 us
    all_to_all x1 -> x2, blocking collectives: 31.7 us -> 45.8 us  [the longest x1 31.7 us: per_device(): lax.all_to_all(sky_now[safe_rows].astype(jnp.bfloat16), 'sky', split_axis...]
    all_to_all x2 -> x1, starting transfers between devices: 15.3 us -> 5.89 us  [per_device(): lax.all_to_all(sky_now[safe_rows].astype(jnp.bfloat16), 'sky', split_axis...]
    all_to_all x2 -> x1, waiting for transfers between devices: 24.9 us -> 20.7 us  [per_device(): lax.all_to_all(sky_now[safe_rows].astype(jnp.bfloat16), 'sky', split_axis...]
  transfers between devices with their start and end apart: 9 -> 8, of which waited for: 6 -> 5; matrix products, arithmetic and copies ran while one was open for 5% -> 4% of each run, Pallas kernels for 0% -> 0%
where the time goes in v13:
time: 341 us; the launch traced here: 336 us
  blocking collectives  178 us (52%)
  waiting for transfers between devices  57.5 us (17%)
  starting transfers between devices  37.2 us (11%)
  local copies, waits for them, and re-layouts  25.3 us (7%)
  matrix products  25 us (7%)
  other arithmetic  11.8 us (3%)
    all_gather x2, blocking collectives, per_device(): lax.all_gather(scaled.astype(jnp.bfloat16), 'exp', axis=0, tiled=True)  64.4 us
    unnamed x1, blocking collectives  35.3 us
    all_to_all x1, blocking collectives, per_device(): lax.all_to_all(outgoing, 'sky', split_axis=0, concat_axis=0, tiled=True)  32.6 us
    all_to_all x2, waiting for transfers between devices, per_device(): lax.all_to_all(payload, 'exp', split_axis=0, concat_axis=0, tiled=True)  32.3 us
    all_to_all x1, blocking collectives, per_device(): lax.all_to_all(sky_now[safe_rows].astype(jnp.bfloat16), 'sky', split_axis...  31.7 us
    all_to_all x1, waiting for transfers between devices, per_device(): lax.all_to_all(sky_now[safe_rows].astype(jnp.bfloat16), 'sky', split_axis...  20.7 us
    all_to_all x1, blocking collectives, per_device(): lax.all_to_all(requested, 'sky', split_axis=0, concat_axis=0, tiled=True)  14.1 us
    all_to_all x2, starting transfers between devices, per_device(): lax.all_to_all(payload, 'exp', split_axis=0, concat_axis=0, tiled=True)  13.4 us
  transfers between devices with their start and end apart: 8, of which 5 were waited for; matrix products, arithmetic and copies ran while one was open for 4% of the time, Pallas kernels for 0%

profile of v13, /device:TPU:6, one launch (start us, length us, event | category | flops | bytes accessed | tf_op | source)
XLA Modules:
  0.0 335.8 jit_solution(13853807895159281387)
XLA Ops:
  3.1 14.1 %all_to_all.36 = s32[32,2,1]{1,2,0:T(1,128)S(1)} all-to-all(s32[32,2,1]{1,2,0:T(1,128)S(1)} %bitcast.102), channel_id=1, replica_groups=mesh['exp'=16,'sky'=32] {'sky'}, dimensions={0} | all-to-all | bytes 512 | tf_op jit(solution)/shard_map/all_to_all | solution.py:96
  18.6 3.3 gather_fusion
  21.9 5.9 %all-to-all-start.1 = ((bf16[64,128,128]{2,1,0:T(8,128)(2,1)}), bf16[64,128,128]{2,1,0:T(8,128)(2,1)S(1)}, u32[]{:S(2)}, u32[]{:S(2)}) async-start(bf16[64,128,128]{2,1,0:T(8,128)(2,1)} %gather_fusion), calls=%async_computation.1 | async-start | bytes 4194304 | tf_op jit(solution)/shard_map/all_to_all | solution.py:109
  28.2 1.3 fusion.4
  29.5 3.2 copy.108
  32.7 20.7 %all-to-all-done.1 = bf16[64,128,128]{2,1,0:T(8,128)(2,1)S(1)} async-done(((bf16[64,128,128]{2,1,0:T(8,128)(2,1)}), bf16[64,128,128]{2,1,0:T(8,128)(2,1)S(1)}, u32[]{:S(2)}, u32[]{:S(2)}) %all-to-all-start.1) | async-done | bytes 2097184 | tf_op jit(solution)/shard_map/all_to_all | solution.py:109
  54.2 6.3 %fusion.1 = bf16[32,2,128,128]{3,2,1,0:T(8,128)(2,1)} fusion(bf16[1,32,2,128,128]{4,3,2,1,0:T(8,128)(2,1)} %param.8, f32[32,2]{1,0:T(8,128)S(1)} %copy.79, bf16[32,2,2,128,128]{4,3,2,1,0:T(8,128)(2,1)} %bitcast.92, bf16[32,128,128]{2,1,0:T(8,128)(2,1)S(1)} %gather_fusion.1), kind=kOutput, calls=%fused_computation.10 | convolution fusion | flops 542113792 | bytes 9437440 | tf_op jit(solution)/shard_map/fetv,fewv->fetw/dot_general | solution.py:43
  60.6 4.3 %bitcast_convert_fusion.1 = bf16[32,128,128]{2,1,0:T(8,128)(2,1)S(1)} fusion(bf16[32,2,128,128]{3,2,1,0:T(8,128)(2,1)} %fusion.1, bf16[32,2,2,128,128]{4,3,2,1,0:T(8,128)(2,1)} %bitcast.93), kind=kOutput, calls=%fused_computation.19 | convolution fusion | flops 538443776 | bytes 7340032 | tf_op jit(solution)/shard_map/fetw,fewv->fetv/dot_general | solution.py:54
  65.0 2.1 gather_fusion.2
  67.1 8.4 %all-to-all-start.2 = ((bf16[64,128,128]{2,1,0:T(8,128)(2,1)}), bf16[64,128,128]{2,1,0:T(8,128)(2,1)S(1)}, u32[]{:S(2)}, u32[]{:S(2)}) async-start(bf16[64,128,128]{2,1,0:T(8,128)(2,1)} %gather_fusion.2), calls=%async_computation.2 | async-start | bytes 4194304 | tf_op jit(solution)/shard_map/all_to_all | solution.py:118
  75.5 1.3 dynamic-slice
  77.8 35.3 %all-reduce.4 = f32[256]{0:T(256)S(1)} all-reduce(f32[256]{0:T(256)S(1)} %multiply_dynamic-update-slice_fusion), channel_id=2, replica_groups=mesh['exp'=16,'sky'=32] {'exp'}, use_global_device_ids=true, to_apply=%add.4 | all-reduce | flops 256 | bytes 2048
  113.2 1.3 fusion.27
  115.3 6.8 %all-to-all-start.3 = ((bf16[16,128,128]{2,1,0:T(8,128)(2,1)}), bf16[16,128,128]{2,1,0:T(8,128)(2,1)}, u32[]{:S(2)}, u32[]{:S(2)}) async-start(bf16[16,128,128]{2,1,0:T(8,128)(2,1)} %copy.83), calls=%async_computation.3 | async-start | bytes 1048576 | tf_op jit(solution)/shard_map/all_to_all | solution.py:131
  122.8 1.9 collective-permute-start.1
  125.1 2.6 collective-permute-start
  128.0 2.0 collective-permute-done
  132.8 15.1 %all-to-all-done.3 = bf16[16,128,128]{2,1,0:T(8,128)(2,1)} async-done(((bf16[16,128,128]{2,1,0:T(8,128)(2,1)}), bf16[16,128,128]{2,1,0:T(8,128)(2,1)}, u32[]{:S(2)}, u32[]{:S(2)}) %all-to-all-start.3) | async-done | bytes 524320 | tf_op jit(solution)/shard_map/all_to_all | solution.py:131
  149.6 32.0 %all-gather = bf16[2048,128]{1,0:T(8,128)(2,1)S(1)} all-gather(bf16[128,128]{1,0:T(8,128)(2,1)S(1)} %divide_convert_fusion.1), channel_id=3, replica_groups=mesh['exp'=16,'sky'=32] {'exp'}, dimensions={0}, use_global_device_ids=true | all-gather | bytes 557056 | tf_op jit(solution)/shard_map/all_gather | solution.py:135
  181.9 2.1 gather_fusion.3
  184.0 31.7 %all_to_all.37 = bf16[64,128,128]{2,1,0:T(8,128)(2,1)} all-to-all(bf16[64,128,128]{2,1,0:T(8,128)(2,1)} %gather_fusion.3), channel_id=1, replica_groups=mesh['exp'=16,'sky'=32] {'sky'}, dimensions={0} | all-to-all | bytes 4194304 | tf_op jit(solution)/shard_map/all_to_all | solution.py:109
  215.7 2.3 gather_fusion.4
  218.0 6.3 %fusion.3 = bf16[32,2,128,128]{3,2,1,0:T(8,128)(2,1)} fusion(bf16[1,32,2,128,128]{4,3,2,1,0:T(8,128)(2,1)} %param.8, f32[32,2]{1,0:T(8,128)S(1)} %copy.79, bf16[32,2,2,128,128]{4,3,2,1,0:T(8,128)(2,1)} %bitcast.94, bf16[32,128,128]{2,1,0:T(8,128)(2,1)S(1)} %gather_fusion.4), kind=kOutput, calls=%fused_computation.12 | convolution fusion | flops 542113792 | bytes 9437440 | tf_op jit(solution)/shard_map/fetv,fewv->fetw/dot_general | solution.py:43
  224.4 4.3 %bitcast_convert_fusion = bf16[32,128,128]{2,1,0:T(8,128)(2,1)S(1)} fusion(bf16[32,2,128,128]{3,2,1,0:T(8,128)(2,1)} %fusion.3, bf16[32,2,2,128,128]{4,3,2,1,0:T(8,128)(2,1)} %bitcast.95), kind=kOutput, calls=%fused_computation.18 | convolution fusion | flops 538443776 | bytes 7340032 | tf_op jit(solution)/shard_map/fetw,fewv->fetv/dot_general | solution.py:54
  228.8 2.2 gather_fusion.5
  230.9 32.6 %all_to_all.38 = bf16[64,128,128]{2,1,0:T(8,128)(2,1)S(1)} all-to-all(bf16[64,128,128]{2,1,0:T(8,128)(2,1)} %gather_fusion.5), channel_id=1, replica_groups=mesh['exp'=16,'sky'=32] {'sky'}, dimensions={0} | all-to-all | bytes 4194304 | tf_op jit(solution)/shard_map/all_to_all | solution.py:118
  265.7 6.7 %all-to-all-start.6 = ((bf16[16,128,128]{2,1,0:T(8,128)(2,1)}), bf16[16,128,128]{2,1,0:T(8,128)(2,1)}, u32[]{:S(2)}, u32[]{:S(2)}) async-start(bf16[16,128,128]{2,1,0:T(8,128)(2,1)} %copy.91), calls=%async_computation.6 | async-start | bytes 1048576 | tf_op jit(solution)/shard_map/all_to_all | solution.py:131
  273.1 2.8 collective-permute-start.3
  276.2 2.1 collective-permute-start.2
  278.8 2.5 collective-permute-done.2
  283.3 17.3 %all-to-all-done.6 = bf16[16,128,128]{2,1,0:T(8,128)(2,1)} async-done(((bf16[16,128,128]{2,1,0:T(8,128)(2,1)}), bf16[16,128,128]{2,1,0:T(8,128)(2,1)}, u32[]{:S(2)}, u32[]{:S(2)}) %all-to-all-start.6) | async-done | bytes 524320 | tf_op jit(solution)/shard_map/all_to_all | solution.py:131
  302.3 32.3 %all-gather.1 = bf16[2048,128]{1,0:T(8,128)(2,1)S(1)} all-gather(bf16[128,128]{1,0:T(8,128)(2,1)S(1)} %divide_convert_fusion), channel_id=4, replica_groups=mesh['exp'=16,'sky'=32] {'exp'}, dimensions={0}, use_global_device_ids=true | all-gather | bytes 557056 | tf_op jit(solution)/shard_map/all_gather | solution.py:135
  (69 shorter events, 21.9 us)
Async XLA Ops:
  21.9 5.9 %copy-start.4 = (bf16[1,32,2]{1,2,0:T(2,128)(2,1)S(1)}, bf16[1,32,2]{1,2,0:T(2,128)(2,1)}, u32[]{:S(2)}) copy-start(bf16[1,32,2]{1,2,0:T(2,128)(2,1)} %param.9) | copy-start | bytes 388
  21.9 6.0 %copy-start.3 = (s32[1,32,2,2]{1,3,2,0:T(2,128)S(1)}, s32[1,32,2,2]{1,3,2,0:T(2,128)}, u32[]{:S(2)}) copy-start(s32[1,32,2,2]{1,3,2,0:T(2,128)} %param.12) | copy-start | bytes 1540
  21.9 6.3 %copy-start.1 = (bf16[8,128,128]{2,1,0:T(8,128)(2,1)S(1)}, bf16[8,128,128]{2,1,0:T(8,128)(2,1)}, u32[]{:S(2)}) copy-start(bf16[8,128,128]{2,1,0:T(8,128)(2,1)} %param.13) | copy-start | bytes 786436
  21.9 31.5 %all-to-all-start.1 = ((bf16[64,128,128]{2,1,0:T(8,128)(2,1)}), bf16[64,128,128]{2,1,0:T(8,128)(2,1)S(1)}, u32[]{:S(2)}, u32[]{:S(2)}) async-start(bf16[64,128,128]{2,1,0:T(8,128)(2,1)} %gather_fusion), calls=%async_computation.1 | async-start | bytes 4194304 | tf_op jit(solution)/shard_map/all_to_all | solution.py:109
  29.5 3.2 copy-start.2
  67.1 45.9 %all-to-all-start.2 = ((bf16[64,128,128]{2,1,0:T(8,128)(2,1)}), bf16[64,128,128]{2,1,0:T(8,128)(2,1)S(1)}, u32[]{:S(2)}, u32[]{:S(2)}) async-start(bf16[64,128,128]{2,1,0:T(8,128)(2,1)} %gather_fusion.2), calls=%async_computation.2 | async-start | bytes 4194304 | tf_op jit(solution)/shard_map/all_to_all | solution.py:118
  113.1 9.0 %copy-start = (f32[16,128,128]{2,1,0:T(8,128)S(1)}, f32[16,128,128]{2,1,0:T(8,128)}, u32[]{:S(2)}) copy-start(f32[16,128,128]{2,1,0:T(8,128)} %param.7) | copy-start | bytes 3145732
  115.3 32.6 %all-to-all-start.3 = ((bf16[16,128,128]{2,1,0:T(8,128)(2,1)}), bf16[16,128,128]{2,1,0:T(8,128)(2,1)}, u32[]{:S(2)}, u32[]{:S(2)}) async-start(bf16[16,128,128]{2,1,0:T(8,128)(2,1)} %copy.83), calls=%async_computation.3 | async-start | bytes 1048576 | tf_op jit(solution)/shard_map/all_to_all | solution.py:131
  122.8 4.9 %collective-permute-start.1 = (f32[16,128,1]{1,0,2:T(8,128)S(1)}, f32[16,128,1]{1,0,2:T(8,128)S(1)}, u32[]{:S(2)}, u32[]{:S(2)}) collective-permute-start(f32[16,128,1]{1,0,2:T(8,128)S(1)} %copy.106), channel_id=1, source_target_pairs={{1,0},{2,1},{3,2},{4,3},{5,4},{6,5},{7,6},{8,7},{9,8},{10,9},{11,1... | collective-permute-start | bytes 24584 | tf_op jit(solution)/shard_map/ppermute | solution.py:22
  125.1 5.0 %collective-permute-start = (f32[16,128,1]{1,0,2:T(8,128)S(1)}, f32[16,128,1]{1,0,2:T(8,128)S(1)}, u32[]{:S(2)}, u32[]{:S(2)}) collective-permute-start(f32[16,128,1]{1,0,2:T(8,128)S(1)} %copy.105), channel_id=1, source_target_pairs={{0,1},{1,2},{2,3},{3,4},{4,5},{5,6},{6,7},{7,8},{8,9},{9,10},{10,1... | collective-permute-start | bytes 24584 | tf_op jit(solution)/shard_map/ppermute | solution.py:20
  265.7 34.9 %all-to-all-start.6 = ((bf16[16,128,128]{2,1,0:T(8,128)(2,1)}), bf16[16,128,128]{2,1,0:T(8,128)(2,1)}, u32[]{:S(2)}, u32[]{:S(2)}) async-start(bf16[16,128,128]{2,1,0:T(8,128)(2,1)} %copy.91), calls=%async_computation.6 | async-start | bytes 1048576 | tf_op jit(solution)/shard_map/all_to_all | solution.py:131
  273.1 5.3 %collective-permute-start.3 = (f32[16,128,1]{1,0,2:T(8,128)S(1)}, f32[16,128,1]{1,0,2:T(8,128)S(1)}, u32[]{:S(2)}, u32[]{:S(2)}) collective-permute-start(f32[16,128,1]{1,0,2:T(8,128)S(1)} %copy.93), channel_id=1, source_target_pairs={{1,0},{2,1},{3,2},{4,3},{5,4},{6,5},{7,6},{8,7},{9,8},{10,9},{11,1... | collective-permute-start | bytes 24584 | tf_op jit(solution)/shard_map/ppermute | solution.py:22
  276.2 5.0 %collective-permute-start.2 = (f32[16,128,1]{1,0,2:T(8,128)S(1)}, f32[16,128,1]{1,0,2:T(8,128)S(1)}, u32[]{:S(2)}, u32[]{:S(2)}) collective-permute-start(f32[16,128,1]{1,0,2:T(8,128)S(1)} %copy.92), channel_id=1, source_target_pairs={{0,1},{1,2},{2,3},{3,4},{4,5},{5,6},{6,7},{7,8},{8,9},{9,10},{10,1... | collective-permute-start | bytes 24584 | tf_op jit(solution)/shard_map/ppermute | solution.py:20

commit v14 on v13

--- a/solution.py
+++ b/solution.py
@@ -111,10 +111,11 @@
         )
         fetched = replies[slot_of]
         adjoint = adjoint_tiles(fetched, left_kernels, right_kernels, tile_weights, observed)
-        padded_adjoint = jnp.concatenate(
-            [adjoint, jnp.zeros((1, tile_edge, tile_edge), adjoint.dtype)], axis=0
+        outgoing = jnp.where(
+            (slot_source < foot_tiles)[:, None, None],
+            adjoint[jnp.minimum(slot_source, foot_tiles - 1)],
+            jnp.zeros((), adjoint.dtype),
         )
-        outgoing = padded_adjoint[slot_source]
         arrived = lax.all_to_all(outgoing, "sky", split_axis=0, concat_axis=0, tiled=True)
         if iteration == 0:
             count_tiles = lax.all_gather(count_tile, "exp", axis=0, tiled=True)

time: 341 us -> 340 us (level)
  no operation moved by 1% of the time
where the time goes in v14:
time: 340 us; the launch traced here: 335 us
  blocking collectives  177 us (52%)
  waiting for transfers between devices  57.2 us (17%)
  starting transfers between devices  37.4 us (11%)
  local copies, waits for them, and re-layouts  23.9 us (7%)
  matrix products  23.1 us (7%)
  other arithmetic  15.1 us (4%)
    all_gather x2, blocking collectives, per_device(): lax.all_gather(scaled.astype(jnp.bfloat16), 'exp', axis=0, tiled=True)  64.5 us
    unnamed x1, blocking collectives  35.3 us
    all_to_all x2, waiting for transfers between devices, per_device(): lax.all_to_all(payload, 'exp', split_axis=0, concat_axis=0, tiled=True)  32.3 us
    all_to_all x1, blocking collectives, per_device(): lax.all_to_all(outgoing, 'sky', split_axis=0, concat_axis=0, tiled=True)  31.9 us
    all_to_all x1, blocking collectives, per_device(): lax.all_to_all(sky_now[safe_rows].astype(jnp.bfloat16), 'sky', split_axis...  31.6 us
    all_to_all x1, waiting for transfers between devices, per_device(): lax.all_to_all(sky_now[safe_rows].astype(jnp.bfloat16), 'sky', split_axis...  20.7 us
    all_to_all x1, blocking collectives, per_device(): lax.all_to_all(requested, 'sky', split_axis=0, concat_axis=0, tiled=True)  14.1 us
    all_to_all x2, starting transfers between devices, per_device(): lax.all_to_all(payload, 'exp', split_axis=0, concat_axis=0, tiled=True)  13.5 us
  transfers between devices with their start and end apart: 8, of which 5 were waited for; matrix products, arithmetic and copies ran while one was open for 4% of the time, Pallas kernels for 0%

profile of v14, /device:TPU:6, one launch (start us, length us, event | category | flops | bytes accessed | tf_op | source)
XLA Modules:
  0.0 335.1 jit_solution(3702893933402710310)
XLA Ops:
  3.1 14.1 %all_to_all.36 = s32[32,2,1]{1,2,0:T(1,128)S(1)} all-to-all(s32[32,2,1]{1,2,0:T(1,128)S(1)} %bitcast.102), channel_id=1, replica_groups=mesh['exp'=16,'sky'=32] {'sky'}, dimensions={0} | all-to-all | bytes 512 | tf_op jit(solution)/shard_map/all_to_all | solution.py:96
  18.6 3.3 gather_fusion
  21.9 5.9 %all-to-all-start.1 = ((bf16[64,128,128]{2,1,0:T(8,128)(2,1)}), bf16[64,128,128]{2,1,0:T(8,128)(2,1)S(1)}, u32[]{:S(2)}, u32[]{:S(2)}) async-start(bf16[64,128,128]{2,1,0:T(8,128)(2,1)} %gather_fusion), calls=%async_computation.1 | async-start | bytes 4194304 | tf_op jit(solution)/shard_map/all_to_all | solution.py:109
  28.2 1.3 fusion.4
  29.5 3.2 copy.109
  32.8 20.7 %all-to-all-done.1 = bf16[64,128,128]{2,1,0:T(8,128)(2,1)S(1)} async-done(((bf16[64,128,128]{2,1,0:T(8,128)(2,1)}), bf16[64,128,128]{2,1,0:T(8,128)(2,1)S(1)}, u32[]{:S(2)}, u32[]{:S(2)}) %all-to-all-start.1) | async-done | bytes 2097184 | tf_op jit(solution)/shard_map/all_to_all | solution.py:109
  54.2 5.0 %fusion.1 = bf16[32,2,128,128]{3,2,1,0:T(8,128)(2,1)S(1)} fusion(bf16[1,32,2,128,128]{4,3,2,1,0:T(8,128)(2,1)} %param.8, f32[32,2]{1,0:T(8,128)S(1)} %copy.80, bf16[32,2,2,128,128]{4,3,2,1,0:T(8,128)(2,1)} %bitcast.92, bf16[32,128,128]{2,1,0:T(8,128)(2,1)S(1)} %gather_fusion.1), kind=kOutput, calls=%fused_computation.10 | convolution fusion | flops 542113792 | bytes 9437440 | tf_op jit(solution)/shard_map/fetv,fewv->fetw/dot_general | solution.py:43
  59.2 3.6 %bitcast_convert_fusion.1 = bf16[32,128,128]{2,1,0:T(8,128)(2,1)S(1)} fusion(bf16[32,2,128,128]{3,2,1,0:T(8,128)(2,1)S(1)} %fusion.1, bf16[32,2,2,128,128]{4,3,2,1,0:T(8,128)(2,1)} %bitcast.93), kind=kOutput, calls=%fused_computation.19 | convolution fusion | flops 538443776 | bytes 7340032 | tf_op jit(solution)/shard_map/fetw,fewv->fetv/dot_general | solution.py:54
  63.8 1.5 broadcast_select_fusion.1
  65.4 8.4 %all-to-all-start.2 = ((bf16[64,128,128]{2,1,0:T(8,128)(2,1)}), bf16[64,128,128]{2,1,0:T(8,128)(2,1)S(1)}, u32[]{:S(2)}, u32[]{:S(2)}) async-start(bf16[64,128,128]{2,1,0:T(8,128)(2,1)} %broadcast_select_fusion.1), calls=%async_computation.2 | async-start | bytes 4194304 | tf_op jit(solution)/shard_map/all_to_all | solution.py:119
  73.8 1.3 dynamic-slice
  76.0 35.3 %all-reduce.2 = f32[256]{0:T(256)S(1)} all-reduce(f32[256]{0:T(256)S(1)} %multiply_dynamic-update-slice_fusion), channel_id=2, replica_groups=mesh['exp'=16,'sky'=32] {'exp'}, use_global_device_ids=true, to_apply=%add.2 | all-reduce | flops 256 | bytes 2048
  113.6 6.8 %all-to-all-start.3 = ((bf16[16,128,128]{2,1,0:T(8,128)(2,1)}), bf16[16,128,128]{2,1,0:T(8,128)(2,1)}, u32[]{:S(2)}, u32[]{:S(2)}) async-start(bf16[16,128,128]{2,1,0:T(8,128)(2,1)} %copy.84), calls=%async_computation.3 | async-start | bytes 1048576 | tf_op jit(solution)/shard_map/all_to_all | solution.py:132
  121.1 1.9 collective-permute-start.1
  123.3 2.6 collective-permute-start
  126.3 2.0 collective-permute-done
  131.1 15.1 %all-to-all-done.3 = bf16[16,128,128]{2,1,0:T(8,128)(2,1)} async-done(((bf16[16,128,128]{2,1,0:T(8,128)(2,1)}), bf16[16,128,128]{2,1,0:T(8,128)(2,1)}, u32[]{:S(2)}, u32[]{:S(2)}) %all-to-all-start.3) | async-done | bytes 524320 | tf_op jit(solution)/shard_map/all_to_all | solution.py:132
  147.9 32.2 %all-gather = bf16[2048,128]{1,0:T(8,128)(2,1)S(1)} all-gather(bf16[128,128]{1,0:T(8,128)(2,1)S(1)} %divide_convert_fusion.1), channel_id=3, replica_groups=mesh['exp'=16,'sky'=32] {'exp'}, dimensions={0}, use_global_device_ids=true | all-gather | bytes 557056 | tf_op jit(solution)/shard_map/all_gather | solution.py:136
  180.3 2.1 gather_fusion.3
  182.4 31.6 %all_to_all.37 = bf16[64,128,128]{2,1,0:T(8,128)(2,1)} all-to-all(bf16[64,128,128]{2,1,0:T(8,128)(2,1)} %gather_fusion.3), channel_id=1, replica_groups=mesh['exp'=16,'sky'=32] {'sky'}, dimensions={0} | all-to-all | bytes 4194304 | tf_op jit(solution)/shard_map/all_to_all | solution.py:109
  214.0 2.3 gather_fusion.4
  216.3 6.3 %fusion.3 = bf16[32,2,128,128]{3,2,1,0:T(8,128)(2,1)} fusion(bf16[1,32,2,128,128]{4,3,2,1,0:T(8,128)(2,1)} %param.8, f32[32,2]{1,0:T(8,128)S(1)} %copy.80, bf16[32,2,2,128,128]{4,3,2,1,0:T(8,128)(2,1)} %bitcast.94, bf16[32,128,128]{2,1,0:T(8,128)(2,1)S(1)} %gather_fusion.4), kind=kOutput, calls=%fused_computation.12 | convolution fusion | flops 542113792 | bytes 9437440 | tf_op jit(solution)/shard_map/fetv,fewv->fetw/dot_general | solution.py:43
  222.6 4.3 %bitcast_convert_fusion = bf16[32,128,128]{2,1,0:T(8,128)(2,1)S(1)} fusion(bf16[32,2,128,128]{3,2,1,0:T(8,128)(2,1)} %fusion.3, bf16[32,2,2,128,128]{4,3,2,1,0:T(8,128)(2,1)} %bitcast.95), kind=kOutput, calls=%fused_computation.18 | convolution fusion | flops 538443776 | bytes 7340032 | tf_op jit(solution)/shard_map/fetw,fewv->fetv/dot_general | solution.py:54
  226.9 2.2 gather_fusion.5
  229.1 1.8 broadcast_select_fusion
  230.9 31.9 %all_to_all.38 = bf16[64,128,128]{2,1,0:T(8,128)(2,1)S(1)} all-to-all(bf16[64,128,128]{2,1,0:T(8,128)(2,1)S(1)} %broadcast_select_fusion), channel_id=1, replica_groups=mesh['exp'=16,'sky'=32] {'sky'}, dimensions={0} | all-to-all | bytes 4194304 | tf_op jit(solution)/shard_map/all_to_all | solution.py:119
  265.0 6.7 %all-to-all-start.6 = ((bf16[16,128,128]{2,1,0:T(8,128)(2,1)}), bf16[16,128,128]{2,1,0:T(8,128)(2,1)}, u32[]{:S(2)}, u32[]{:S(2)}) async-start(bf16[16,128,128]{2,1,0:T(8,128)(2,1)} %copy.92), calls=%async_computation.6 | async-start | bytes 1048576 | tf_op jit(solution)/shard_map/all_to_all | solution.py:132
  272.4 2.8 collective-permute-start.3
  275.6 2.3 collective-permute-start.2
  278.3 2.2 collective-permute-done.2
  282.6 17.2 %all-to-all-done.6 = bf16[16,128,128]{2,1,0:T(8,128)(2,1)} async-done(((bf16[16,128,128]{2,1,0:T(8,128)(2,1)}), bf16[16,128,128]{2,1,0:T(8,128)(2,1)}, u32[]{:S(2)}, u32[]{:S(2)}) %all-to-all-start.6) | async-done | bytes 524320 | tf_op jit(solution)/shard_map/all_to_all | solution.py:132
  301.5 32.4 %all-gather.1 = bf16[2048,128]{1,0:T(8,128)(2,1)S(1)} all-gather(bf16[128,128]{1,0:T(8,128)(2,1)S(1)} %divide_convert_fusion), channel_id=4, replica_groups=mesh['exp'=16,'sky'=32] {'exp'}, dimensions={0}, use_global_device_ids=true | all-gather | bytes 557056 | tf_op jit(solution)/shard_map/all_gather | solution.py:136
  (70 shorter events, 23.8 us)
Async XLA Ops:
  21.9 5.9 %copy-start.4 = (bf16[1,32,2]{1,2,0:T(2,128)(2,1)S(1)}, bf16[1,32,2]{1,2,0:T(2,128)(2,1)}, u32[]{:S(2)}) copy-start(bf16[1,32,2]{1,2,0:T(2,128)(2,1)} %param.9) | copy-start | bytes 388
  21.9 6.0 %copy-start.3 = (s32[1,32,2,2]{1,3,2,0:T(2,128)S(1)}, s32[1,32,2,2]{1,3,2,0:T(2,128)}, u32[]{:S(2)}) copy-start(s32[1,32,2,2]{1,3,2,0:T(2,128)} %param.12) | copy-start | bytes 1540
  21.9 6.3 %copy-start.1 = (bf16[8,128,128]{2,1,0:T(8,128)(2,1)S(1)}, bf16[8,128,128]{2,1,0:T(8,128)(2,1)}, u32[]{:S(2)}) copy-start(bf16[8,128,128]{2,1,0:T(8,128)(2,1)} %param.13) | copy-start | bytes 786436
  21.9 31.5 %all-to-all-start.1 = ((bf16[64,128,128]{2,1,0:T(8,128)(2,1)}), bf16[64,128,128]{2,1,0:T(8,128)(2,1)S(1)}, u32[]{:S(2)}, u32[]{:S(2)}) async-start(bf16[64,128,128]{2,1,0:T(8,128)(2,1)} %gather_fusion), calls=%async_computation.1 | async-start | bytes 4194304 | tf_op jit(solution)/shard_map/all_to_all | solution.py:109
  29.5 3.2 copy-start.2
  65.4 45.9 %all-to-all-start.2 = ((bf16[64,128,128]{2,1,0:T(8,128)(2,1)}), bf16[64,128,128]{2,1,0:T(8,128)(2,1)S(1)}, u32[]{:S(2)}, u32[]{:S(2)}) async-start(bf16[64,128,128]{2,1,0:T(8,128)(2,1)} %broadcast_select_fusion.1), calls=%async_computation.2 | async-start | bytes 4194304 | tf_op jit(solution)/shard_map/all_to_all | solution.py:119
  111.4 9.0 %copy-start = (f32[16,128,128]{2,1,0:T(8,128)S(1)}, f32[16,128,128]{2,1,0:T(8,128)}, u32[]{:S(2)}) copy-start(f32[16,128,128]{2,1,0:T(8,128)} %param.7) | copy-start | bytes 3145732
  113.6 32.6 %all-to-all-start.3 = ((bf16[16,128,128]{2,1,0:T(8,128)(2,1)}), bf16[16,128,128]{2,1,0:T(8,128)(2,1)}, u32[]{:S(2)}, u32[]{:S(2)}) async-start(bf16[16,128,128]{2,1,0:T(8,128)(2,1)} %copy.84), calls=%async_computation.3 | async-start | bytes 1048576 | tf_op jit(solution)/shard_map/all_to_all | solution.py:132
  121.1 4.9 %collective-permute-start.1 = (f32[16,128,1]{1,0,2:T(8,128)S(1)}, f32[16,128,1]{1,0,2:T(8,128)S(1)}, u32[]{:S(2)}, u32[]{:S(2)}) collective-permute-start(f32[16,128,1]{1,0,2:T(8,128)S(1)} %copy.107), channel_id=1, source_target_pairs={{1,0},{2,1},{3,2},{4,3},{5,4},{6,5},{7,6},{8,7},{9,8},{10,9},{11,1... | collective-permute-start | bytes 24584 | tf_op jit(solution)/shard_map/ppermute | solution.py:22
  123.3 5.0 %collective-permute-start = (f32[16,128,1]{1,0,2:T(8,128)S(1)}, f32[16,128,1]{1,0,2:T(8,128)S(1)}, u32[]{:S(2)}, u32[]{:S(2)}) collective-permute-start(f32[16,128,1]{1,0,2:T(8,128)S(1)} %copy.106), channel_id=1, source_target_pairs={{0,1},{1,2},{2,3},{3,4},{4,5},{5,6},{6,7},{7,8},{8,9},{9,10},{10,1... | collective-permute-start | bytes 24584 | tf_op jit(solution)/shard_map/ppermute | solution.py:20
  265.0 34.8 %all-to-all-start.6 = ((bf16[16,128,128]{2,1,0:T(8,128)(2,1)}), bf16[16,128,128]{2,1,0:T(8,128)(2,1)}, u32[]{:S(2)}, u32[]{:S(2)}) async-start(bf16[16,128,128]{2,1,0:T(8,128)(2,1)} %copy.92), calls=%async_computation.6 | async-start | bytes 1048576 | tf_op jit(solution)/shard_map/all_to_all | solution.py:132
  272.4 5.5 %collective-permute-start.3 = (f32[16,128,1]{1,0,2:T(8,128)S(1)}, f32[16,128,1]{1,0,2:T(8,128)S(1)}, u32[]{:S(2)}, u32[]{:S(2)}) collective-permute-start(f32[16,128,1]{1,0,2:T(8,128)S(1)} %copy.94), channel_id=1, source_target_pairs={{1,0},{2,1},{3,2},{4,3},{5,4},{6,5},{7,6},{8,7},{9,8},{10,9},{11,1... | collective-permute-start | bytes 24584 | tf_op jit(solution)/shard_map/ppermute | solution.py:22
  275.6 5.0 %collective-permute-start.2 = (f32[16,128,1]{1,0,2:T(8,128)S(1)}, f32[16,128,1]{1,0,2:T(8,128)S(1)}, u32[]{:S(2)}, u32[]{:S(2)}) collective-permute-start(f32[16,128,1]{1,0,2:T(8,128)S(1)} %copy.93), channel_id=1, source_target_pairs={{0,1},{1,2},{2,3},{3,4},{4,5},{5,6},{6,7},{7,8},{8,9},{9,10},{10,1... | collective-permute-start | bytes 24584 | tf_op jit(solution)/shard_map/ppermute | solution.py:20
